TPU v7x, 512 devices: a whole 4x8x8 slice. The times are simulated.
512 devices in a mesh: chan: 128 (over z, y, core), tm: 4 (over x).
Axes of the slice: x: 4, y: 8, z: 8, core: 2. Of those that a mesh axis runs over, the one named last changes fastest.
Arguments:
- visibilities: bfloat16 [4, 1024, 16384], P('tm', 'chan'), may hold values from -6 to 6
- flags: int32 [4, 1024, 2048], P('tm', 'chan'), may hold values 0 or 1
- taper: float32 [1024], P('chan'), may hold values from 0.3 to 1
- group_ids: int32 [2048], replicated, may hold values from 0 to 15
Outputs:
- spectrum: float32 [4, 16, 1024], P(None, None, 'chan')
Inputs may be any that keep to these rules, and one draw needn't show every extreme that they name: `group_ids`: each baseline's group number.
All inputs are finite; a program needn't handle non-finite values. No bound on the sum of `flags` on one device may be relied on, other than what follows from the above.
Results may differ from a plain program's by a relative error of at most 0.0051.
Values may be sent and summed in bfloat16 or wider, within the bound.
No kernel may reach another device: no remote copies, remote signals or barrier semaphores. Data moves between devices by JAX's collectives and lax.ppermute only.
A program may use at most 64 MiB of HBM per device.

v0:
```python
import math

import jax
import jax.numpy as jnp
from jax import lax
from jax.sharding import PartitionSpec as P

G = 16


def tables(length):
    positions = jnp.arange(length, dtype=jnp.int32)
    product = positions[:, None] * positions[None, :] % length
    phases = product.astype(jnp.float32) * (2.0 * math.pi / length)
    normalizing_scale = 1.0 / math.sqrt(length)
    return (
        (jnp.cos(phases) * normalizing_scale).astype(jnp.bfloat16),
        (jnp.sin(phases) * normalizing_scale).astype(jnp.bfloat16),
    )


def body(visibilities, flags, taper, group_ids):
    local_times, local_chans, column_entries = visibilities.shape
    baseline_pairs = column_entries // 8
    channels = local_chans * lax.axis_size("chan")
    shard_count = baseline_pairs // lax.axis_size("chan")
    times_all = local_times * lax.axis_size("tm")
    cos_tab, sin_tab = tables(channels)
    group_range = jnp.arange(G, dtype=jnp.int32)
    shard_group_index = lax.dynamic_slice_in_dim(
        group_ids, lax.axis_index("chan") * shard_count, shard_count
    )
    group_member = (shard_group_index[None, :] == group_range[:, None]).astype(jnp.float32)
    turned = lax.all_to_all(visibilities, "chan", split_axis=2, concat_axis=1, tiled=True)
    turned_flags = lax.all_to_all(flags, "chan", split_axis=2, concat_axis=1, tiled=True)
    full_taper = lax.all_gather(taper, "chan", axis=0, tiled=True)
    weight = (1 - turned_flags).astype(jnp.float32) * full_taper[None, :, None]
    shaped = turned.reshape(local_times, channels, shard_count, 8).astype(jnp.float32)
    tapered = (
        (shaped * weight[..., None])
        .astype(jnp.bfloat16)
        .reshape(local_times, channels, shard_count * 8)
    )
    items = tapered.shape[0]
    cosine_part = jnp.einsum(
        "dc,tcn->tdn", cos_tab, tapered, preferred_element_type=jnp.float32
    ).reshape(items, channels, shard_count, 4, 2)
    sine_part = jnp.einsum(
        "dc,tcn->tdn", sin_tab, tapered, preferred_element_type=jnp.float32
    ).reshape(items, channels, shard_count, 4, 2)
    real_part = cosine_part[..., 0] + sine_part[..., 1]
    imag_part = cosine_part[..., 1] - sine_part[..., 0]
    group_real = jnp.einsum(
        "tdbs,gb->tsgd", real_part, group_member, precision=lax.Precision.HIGHEST
    )
    group_imag = jnp.einsum(
        "tdbs,gb->tsgd", imag_part, group_member, precision=lax.Precision.HIGHEST
    )
    autocorrelation_terms = jnp.einsum(
        "tdbs,gb->tsgd",
        real_part * real_part + imag_part * imag_part,
        group_member,
        precision=lax.Precision.HIGHEST,
    )
    group_terms = jnp.stack([group_real, group_imag, autocorrelation_terms], axis=1)
    owned = lax.psum_scatter(group_terms, "chan", scatter_dimension=4, tiled=True)
    spectrum = jnp.sum(owned[:, 0] * owned[:, 0] + owned[:, 1] * owned[:, 1] - owned[:, 2], axis=0)
    spectrum = lax.psum(spectrum, "tm")
    member_all = (group_ids[None, :] == group_range[:, None]).astype(jnp.float32)
    counts = jnp.sum(member_all, axis=1)
    pair_count = jnp.maximum(counts * (counts - 1.0), 1.0)
    return spectrum / jnp.sqrt(pair_count * times_all)[None, :, None]


def solution(mesh):
    return jax.shard_map(
        body,
        mesh=mesh,
        in_specs=(P("tm", "chan", None), P("tm", "chan", None), P("chan"), P()),
        out_specs=P(None, None, "chan"),
        check_vma=False,
    )
```

profile of v0, /device:TPU:6, one launch (start us, length us, event | category | flops | bytes accessed | tf_op | source)
XLA Modules:
  0.0 720.9 jit_solution(13528118081946566250)
XLA Ops:
  6.5 0.0 copy-start
  6.5 1.9 copy.69
  8.4 0.5 broadcast.92
  8.9 9.3 %reduce = s32[2048,8]{1,0:T(8,128)S(1)} reduce(s32[2048,1,8]{2,1,0:T(1,128)S(1)} %bitcast.79, s32[]{:T(128)} %broadcast.92), dimensions={1}, to_apply=%bitcast.69.reduce_sub_computation | reduce | bytes 131076
  18.3 1.1 reshape.135
  19.4 18.0 %all-to-all-start.1 = ((s32[128,1,128]{2,1,0:T(1,128)}), s32[128,1,128]{2,1,0:T(1,128)S(1)}, u32[]{:S(2)}, u32[]{:S(2)}) async-start(s32[128,1,128]{2,1,0:T(1,128)} %reshape.135), calls=%async_computation.1 | async-start | bytes 131072 | tf_op jit(solution)/shard_map/all_to_all | solution.py:35
  37.4 0.0 copy-done
  37.5 12.7 %copy.66 = bf16[1,8,16384]{1,0,2:T(2,128)(2,1)} copy(bf16[1,8,16384]{2,1,0:T(8,128)(2,1)S(1)} %copy-done) | data formatting | bytes 524288 | tf_op args[0]
  50.1 0.5 broadcast.94
  50.7 90.8 %reduce.2 = bf16[16384,8]{1,0:T(8,128)(2,1)} reduce(bf16[16384,1,8]{2,1,0:T(2,128)(2,1)} %bitcast.77, bf16[]{:T(256)} %broadcast.94), dimensions={1}, to_apply=%bitcast.71.reduce_sub_computation | reduce | bytes 524290
  141.4 0.0 copy-start.2
  141.4 0.0 copy-start.1
  141.4 0.0 copy-start.3
  141.5 6.9 reshape.137
  148.3 0.0 copy-done.2
  148.3 0.6 fusion.48
  149.6 0.0 copy-done.1
  149.6 0.1 dynamic_slice.3
  149.7 0.0 copy-done.3
  149.7 0.2 dynamic-update-slice
  149.9 251.5 %all-reduce = f32[1024]{0:T(1024)S(1)} all-reduce(f32[1024]{0:T(1024)S(1)} %dynamic-update-slice), channel_id=1, replica_groups=mesh['chan'=128,'tm'=4] {'chan'}, use_global_device_ids=true, to_apply=%add | all-reduce | flops 1024 | bytes 8192
  401.5 0.0 all-to-all-done.1
  401.5 6.3 all-to-all-start
  407.8 0.3 all-reduce.4.cloned.1.call-start
  408.1 0.8 reduce.1
  408.9 1.6 reshape.136
  410.5 0.5 copy.70
  411.0 0.2 convert_element_type.63
  411.2 0.3 bitcast_multiply_fusion
  411.6 0.2 copy.72
  411.8 0.1 broadcast_bitcast_fusion
  411.8 0.2 copy.73
  412.0 10.5 %all-to-all-done = bf16[128,2,512]{2,1,0:T(2,128)(2,1)S(1)} async-done(((bf16[128,2,512]{2,1,0:T(2,128)(2,1)}), bf16[128,2,512]{2,1,0:T(2,128)(2,1)S(1)}, u32[]{:S(2)}, u32[]{:S(2)}) %all-to-all-start) | async-done | bytes 262176 | tf_op jit(solution)/shard_map/all_to_all | solution.py:34
  422.5 17.1 %reshape.138 = bf16[16384,1,8]{2,1,0:T(2,128)(2,1)} reshape(bf16[128,2,512]{2,1,0:T(2,128)(2,1)S(1)} %all-to-all-done) | data formatting | bytes 524288
  439.6 14.8 %copy.67 = bf16[1,8,16384]{2,1,0:T(8,128)(2,1)S(1)} copy(bf16[1,8,16384]{1,0,2:T(2,128)(2,1)} %bitcast.78) | data formatting | bytes 524288 | tf_op jit(solution)/shard_map/all_to_all | solution.py:34
  454.4 0.1 copy.128
  454.6 0.3 fusion.14
  454.9 16.1 %fusion.13 = f32[1,1024,128]{1,2,0:T(8,128)S(1)} fusion(bf16[1024,128]{1,0:T(8,128)(2,1)S(1)} %fusion.14), kind=kOutput, calls=%fused_computation.16 | convolution fusion | flops 285212672 | bytes 786432 | tf_op jit(solution)/shard_map/dc,tcn->tdn/dot_general | solution.py:45
  471.0 16.5 %fusion.12 = f32[1,1024,128]{1,2,0:T(8,128)S(1)} fusion(bf16[1024,128]{1,0:T(8,128)(2,1)S(1)} %fusion.14), kind=kOutput, calls=%fused_computation.15 | convolution fusion | flops 285212672 | bytes 786432 | tf_op jit(solution)/shard_map/dc,tcn->tdn/dot_general | solution.py:48
  487.4 0.3 reshape.124
  487.7 0.3 reshape.125
  488.0 1.2 fusion.46
  489.2 0.6 convolution_bitcast_fusion.2
  489.8 1.1 convolution_bitcast_fusion
  490.9 0.6 convolution_bitcast_fusion.1
  491.5 0.1 pad_maximum_fusion
  491.6 4.6 copy.78
  496.2 0.0 all-reduce.4.cloned.1.call-update
  496.8 0.1 convert_reduce_fusion
  497.0 201.8 %all-reduce.4.cloned.1.call-done = f32[1,3,4,16,1024]{3,2,1,0,4:T(4,128)} async-done(((f32[1,3,4,16,1024]{3,2,1,0,4:T(4,128)}), f32[1,3,4,16,1024]{3,2,1,0,4:T(4,128)}) %all-reduce.4.cloned.1.call-update) | async-done | bytes 786448
  698.8 0.8 constant_dynamic-slice_fusion.1
  699.5 13.9 %psum.7 = f32[4,16,8]{1,2,0:T(8,128)S(1)} all-reduce(f32[4,16,8]{1,2,0:T(8,128)S(1)} %fusion.24), channel_id=1, replica_groups=mesh['chan'=128,'tm'=4] {'tm'}, use_global_device_ids=true, to_apply=%region_1.2 | all-reduce | flops 512 | bytes 4096 | tf_op jit(solution)/shard_map/psum | solution.py:68
  713.4 0.6 broadcast_divide_fusion
  (5 shorter events, 0.1 us)
Async XLA Ops:
  6.5 30.9 %copy-start = (bf16[1,8,16384]{2,1,0:T(8,128)(2,1)S(1)}, bf16[1,8,16384]{2,1,0:T(8,128)(2,1)}, u32[]{:S(2)}) copy-start(bf16[1,8,16384]{2,1,0:T(8,128)(2,1)} %param.4) | copy-start | bytes 786436
  19.4 382.0 %all-to-all-start.1 = ((s32[128,1,128]{2,1,0:T(1,128)}), s32[128,1,128]{2,1,0:T(1,128)S(1)}, u32[]{:S(2)}, u32[]{:S(2)}) async-start(s32[128,1,128]{2,1,0:T(1,128)} %reshape.135), calls=%async_computation.1 | async-start | bytes 131072 | tf_op jit(solution)/shard_map/all_to_all | solution.py:35
  141.4 6.9 copy-start.2
  141.4 8.2 %copy-start.1 = (s32[2048]{0:T(1024)S(1)}, s32[2048]{0:T(1024)}, u32[]{:S(2)}) copy-start(s32[2048]{0:T(1024)} %param.7) | copy-start | bytes 24580
  141.4 8.3 %copy-start.3 = (f32[8]{0:T(128)S(1)}, f32[8]{0:T(128)}, u32[]{:S(2)}) copy-start(f32[8]{0:T(128)} %param.6) | copy-start | bytes 100
  401.5 21.1 %all-to-all-start = ((bf16[128,2,512]{2,1,0:T(2,128)(2,1)}), bf16[128,2,512]{2,1,0:T(2,128)(2,1)S(1)}, u32[]{:S(2)}, u32[]{:S(2)}) async-start(bf16[128,2,512]{2,1,0:T(2,128)(2,1)} %reshape.137), calls=%async_computation | async-start | bytes 524288 | tf_op jit(solution)/shard_map/all_to_all | solution.py:34
  407.8 291.0 %all-reduce.4.cloned.1.call-start = ((), (), s32[]{:S(2)}) async-start(), calls=%async_computation.2 | async-start | bytes 12582912
Sparse Core Ops, SparseCore 0:
  496.3 202.3 all-reduce.3
where the time goes:
time: 726 us; the launch traced here: 721 us
  blocking collectives  265 us (37%)
  waiting for transfers between devices  212 us (29%)
  other arithmetic  102 us (14%)
  local copies, waits for them, and re-layouts  66.5 us (9%)
  matrix products  34.8 us (5%)
  starting transfers between devices  24.6 us (3%)
  between operations  14.9 us (2%)
    unnamed x1, blocking collectives  252 us
    unnamed x2, waiting for transfers between devices  202 us
    unnamed x3, other arithmetic  100 us
    unnamed x20, local copies, waits for them, and re-layouts  43.4 us
    all_to_all x1, starting transfers between devices, body(): lax.all_to_all(flags, 'chan', split_axis=2, concat_axis=1, tiled=True)  18 us
    dot_general x1, matrix products, body(): jnp.einsum('dc,tcn->tdn', sin_tab, tapered, preferred_element_type=jnp.fl...  16.5 us
    dot_general x1, matrix products, body(): jnp.einsum('dc,tcn->tdn', cos_tab, tapered, preferred_element_type=jnp.fl...  16.1 us
    all_to_all x1, local copies, waits for them, and re-layouts, body(): lax.all_to_all(visibilities, 'chan', split_axis=2, concat_axis=1, tiled=T...  14.8 us
  transfers between devices with their start and end apart: 3, of which 2 were waited for; matrix products, arithmetic and copies ran while one was open for 16% of the time, Pallas kernels for 0%

commit v1 on v0

v1 whole, which is shorter than its diff:
```python
import math

import jax
import jax.numpy as jnp
from jax import lax
from jax.sharding import PartitionSpec as P

G = 16
REDUCE_BY_ALL_TO_ALL = True


def tables(length, minor):
    major = length // minor
    d = jnp.arange(length, dtype=jnp.int32)
    c1 = jnp.arange(major, dtype=jnp.int32)
    c0 = jnp.arange(minor, dtype=jnp.int32)
    step = 2.0 * math.pi / length
    ka = (d[:, None] * (minor * c1)[None, :]) % length
    kb = (d[:, None] * c0[None, :]) % length
    pa = ka.astype(jnp.float32) * step
    pb = kb.astype(jnp.float32) * step
    ca, sa = jnp.cos(pa)[:, :, None], jnp.sin(pa)[:, :, None]
    cb, sb = jnp.cos(pb)[:, None, :], jnp.sin(pb)[:, None, :]
    scale = 1.0 / math.sqrt(length)
    cos_tab = ((ca * cb - sa * sb) * scale).astype(jnp.bfloat16).reshape(length, length)
    sin_tab = ((sa * cb + ca * sb) * scale).astype(jnp.bfloat16).reshape(length, length)
    return cos_tab, sin_tab


def hi_dot(a, b):
    return jnp.dot(a, b, precision=lax.Precision.HIGHEST, preferred_element_type=jnp.float32)


def body(visibilities, flags, taper, group_ids):
    _, local_chans, column_entries = visibilities.shape
    baselines = column_entries // 8
    n_chan = lax.axis_size("chan")
    channels = local_chans * n_chan
    shard_bl = baselines // n_chan
    shard_cols = shard_bl * 8
    times_all = lax.axis_size("tm")

    weight = (1 - flags[0]).astype(jnp.float32) * taper[:, None]
    shaped = visibilities[0].reshape(local_chans, baselines, 8).astype(jnp.float32)
    tapered = (shaped * weight[..., None]).astype(jnp.bfloat16)
    tapered = tapered.reshape(local_chans, n_chan, shard_cols).transpose(1, 0, 2)
    turned = lax.all_to_all(tapered, "chan", 0, 0, tiled=True)
    turned = turned.reshape(channels, shard_cols)

    cos_tab, sin_tab = tables(channels, 128)
    cos_part = jnp.dot(cos_tab, turned, preferred_element_type=jnp.float32)
    sin_part = jnp.dot(sin_tab, turned, preferred_element_type=jnp.float32)

    me = lax.axis_index("chan")
    shard_groups = lax.dynamic_slice_in_dim(group_ids, me * shard_bl, shard_bl)
    member = (shard_groups[:, None] == jnp.arange(G, dtype=jnp.int32)[None, :]).astype(jnp.float32)
    eye_s = jnp.eye(4, dtype=jnp.float32)
    eye_b = jnp.eye(shard_bl, dtype=jnp.float32)
    r_one = jnp.array([0.0, 1.0], jnp.float32)
    r_zero = 1.0 - r_one
    m_gs = member[:, None, None, :, None] * eye_s[None, :, None, None, :]
    m0 = (m_gs * r_zero[None, None, :, None, None]).reshape(shard_cols, G * 4)
    m1 = (m_gs * r_one[None, None, :, None, None]).reshape(shard_cols, G * 4)
    p_bs = eye_b[:, None, None, :, None] * eye_s[None, :, None, None, :]
    p0 = (p_bs * r_zero[None, None, :, None, None]).reshape(shard_cols, shard_bl * 4)
    p1 = (p_bs * r_one[None, None, :, None, None]).reshape(shard_cols, shard_bl * 4)
    m_pow = (member[:, None, :, None] * eye_s[None, :, None, :]).reshape(shard_bl * 4, G * 4)

    group_real = hi_dot(cos_part, m0) + hi_dot(sin_part, m1)
    group_imag = hi_dot(cos_part, m1) - hi_dot(sin_part, m0)
    real_part = hi_dot(cos_part, p0) + hi_dot(sin_part, p1)
    imag_part = hi_dot(cos_part, p1) - hi_dot(sin_part, p0)
    auto = hi_dot(real_part * real_part + imag_part * imag_part, m_pow)

    own_d = channels // n_chan
    terms = jnp.stack([group_real, group_imag, auto], axis=0)
    terms = terms.reshape(3, n_chan, own_d, G * 4).transpose(1, 0, 2, 3)
    if REDUCE_BY_ALL_TO_ALL:
        owned = jnp.sum(lax.all_to_all(terms, "chan", 0, 0, tiled=True), axis=0)
    else:
        owned = lax.psum_scatter(terms, "chan", scatter_dimension=0, tiled=True)[0]
    cross = owned[0] * owned[0] + owned[1] * owned[1] - owned[2]
    cross = lax.psum(cross, "tm")

    member_all = (group_ids[None, :] == jnp.arange(G, dtype=jnp.int32)[:, None]).astype(jnp.float32)
    counts = jnp.sum(member_all, axis=1)
    pair_count = jnp.maximum(counts * (counts - 1.0), 1.0)
    norm = jnp.sqrt(pair_count * times_all)
    spectrum = cross.reshape(own_d, G, 4).transpose(2, 1, 0)
    return spectrum / norm[None, :, None]


def solution(mesh):
    return jax.shard_map(
        body,
        mesh=mesh,
        in_specs=(P("tm", "chan", None), P("tm", "chan", None), P("chan"), P()),
        out_specs=P(None, None, "chan"),
        check_vma=False,
    )
```

time: 726 us -> 122 us (0.17)
  the two profiles are of different devices: /device:TPU:6 before, /device:TPU:8 now
where the time goes in v1:
time: 122 us; the launch traced here: 121 us
  starting transfers between devices  29.9 us (25%)
  waiting for transfers between devices  26.8 us (22%)
  local copies, waits for them, and re-layouts  21.2 us (17%)
  blocking collectives  17.1 us (14%)
  other arithmetic  13.1 us (11%)
  matrix products  12.6 us (10%)
    all_to_all x1, waiting for transfers between devices, body(): owned = jnp.sum(lax.all_to_all(terms, 'chan', 0, 0, tiled=True), axis=0)  25.6 us
    all_to_all x1, starting transfers between devices, body(): turned = lax.all_to_all(tapered, 'chan', 0, 0, tiled=True)  17.4 us
    psum x1, blocking collectives, body(): cross = lax.psum(cross, 'tm')  17.1 us
    all_to_all x1, starting transfers between devices, body(): owned = jnp.sum(lax.all_to_all(terms, 'chan', 0, 0, tiled=True), axis=0)  12.5 us
    mul x2, local copies, waits for them, and re-layouts, body(): tapered = (shaped * weight[..., None]).astype(jnp.bfloat16)  10.9 us
    dot_general x9, matrix products, hi_dot(): jnp.dot(a, b, precision=lax.Precision.HIGHEST, preferred_element_type=jnp...  8.52 us
    convert_element_type x1, other arithmetic, tables(): ((sa * cb + ca * sb) * scale).astype(jnp.bfloat16).reshape(length, length)  6.5 us
    all_to_all x1, other arithmetic, body(): owned = jnp.sum(lax.all_to_all(terms, 'chan', 0, 0, tiled=True), axis=0)  2.51 us
  transfers between devices with their start and end apart: 2, of which 2 were waited for; matrix products, arithmetic and copies ran while one was open for 11% of the time, Pallas kernels for 0%

profile of v1, /device:TPU:8, one launch (start us, length us, event | category | flops | bytes accessed | tf_op | source)
XLA Modules:
  0.0 120.9 jit_solution(898899628003425704)
XLA Ops:
  0.0 0.9 bitcast_multiply_fusion.1
  0.9 4.5 %mul.392 = f32[8,2048,8]{2,1,0:T(8,128)} broadcast(f32[8,2048]{1,0:T(8,128)S(1)} %bitcast_multiply_fusion.1), dimensions={0,1} | broadcast | bytes 589824 | tf_op jit(solution)/shard_map/mul | solution.py:45
  5.4 0.0 copy-start
  5.4 6.4 %mul.393 = f32[8,128,128]{2,1,0:T(8,128)S(1)} reshape(f32[8,2048,8]{2,1,0:T(8,128)} %mul.392) | data formatting | bytes 1048576 | tf_op jit(solution)/shard_map/mul | solution.py:45
  11.8 0.0 copy-done
  11.8 0.0 copy-start.3
  11.9 0.1 fusion.17
  12.0 0.9 copy.54
  12.9 17.4 %all-to-all-start = ((bf16[128,8,128]{2,1,0:T(8,128)(2,1)}), bf16[128,8,128]{2,1,0:T(8,128)(2,1)S(1)}, u32[]{:S(2)}, u32[]{:S(2)}) async-start(bf16[128,8,128]{2,1,0:T(8,128)(2,1)} %copy.54), calls=%async_computation | async-start | bytes 524288 | tf_op jit(solution)/shard_map/all_to_all | solution.py:47
  30.2 2.1 %fusion.20 = (f32[1024,128]{1,0:T(8,128)S(1)}, f32[1024,128]{1,0:T(8,128)S(1)}) fusion(), kind=kLoop, calls=%fused_computation.35 | loop fusion | flops 1835008 | bytes 1048576 | tf_op jit(solution)/shard_map/sin | solution.py:23
  32.3 0.2 fusion.50
  32.6 1.0 copy.53
  33.6 1.0 copy.52
  34.6 0.0 copy-done.3
  34.6 0.1 dynamic_slice.3
  34.6 0.1 fusion.51
  34.7 0.1 broadcast_multiply_fusion.1
  34.9 0.1 mul.414
  35.0 0.5 mul.415
  35.5 0.1 mul.402
  35.6 0.1 mul.409
  35.8 0.8 mul.420
  36.6 0.1 mul.399
  36.7 0.5 mul.400
  37.2 6.5 %multiply_convert_fusion = (bf16[1024,8,128]{2,1,0:T(8,128)(2,1)S(1)}, bf16[1024,8,128]{2,1,0:T(8,128)(2,1)}) fusion(f32[1024,128]{1,0:T(8,128)S(1)} %get-tuple-element.11, f32[1024,8]{1,0:T(8,128)} %copy.53, f32[1024,128]{1,0:T(8,128)S(1)} %get-tuple-element.12, f32[1024,8]{1,0:T(8,128)} %copy.52), kind=kLoop, calls=%fused_computation | loop fusion | flops 10485760 | bytes 5308416 | tf_op jit(solution)/shard_map/convert_element_type | solution.py:26
  43.7 1.2 %all-to-all-done = bf16[128,8,128]{2,1,0:T(8,128)(2,1)S(1)} async-done(((bf16[128,8,128]{2,1,0:T(8,128)(2,1)}), bf16[128,8,128]{2,1,0:T(8,128)(2,1)S(1)}, u32[]{:S(2)}, u32[]{:S(2)}) %all-to-all-start) | async-done | bytes 262176 | tf_op jit(solution)/shard_map/all_to_all | solution.py:47
  44.9 0.0 copy-start.1
  44.9 2.4 %fusion.3 = f32[1024,128]{1,0:T(8,128)S(1)} fusion(bf16[128,8,8,128]{3,2,1,0:T(8,128)(2,1)} %bitcast.54, bf16[128,8,128]{2,1,0:T(8,128)(2,1)S(1)} %all-to-all-done), kind=kOutput, calls=%fused_computation.5 | convolution fusion | flops 268435456 | bytes 2883584 | tf_op jit(solution)/shard_map/dot_general | solution.py:51
  47.3 0.8 fusion.26
  48.1 0.8 fusion.22
  48.9 0.0 copy-done.1
  48.9 1.5 %fusion.28 = f32[1024,64]{0,1:T(8,128)} fusion(f32[1024,128]{1,0:T(8,128)S(1)} %fusion.3, f32[128,64]{1,0:T(8,128)S(1)} %mul.400, f32[128]{0:T(128)S(1)} %mul.409), kind=kOutput, calls=%fused_computation.46 | convolution fusion | flops 100671488 | bytes 819712 | tf_op jit(solution)/shard_map/dot_general | solution.py:31
  50.3 0.8 fusion.32
  51.1 1.7 %fusion = f32[1024,128]{1,0:T(8,128)S(1)} fusion(bf16[128,8,8,128]{3,2,1,0:T(8,128)(2,1)S(1)} %bitcast.53, bf16[128,8,128]{2,1,0:T(8,128)(2,1)} %copy-done.1), kind=kOutput, calls=%fused_computation.2 | convolution fusion | flops 268435456 | bytes 2883584 | tf_op jit(solution)/shard_map/dot_general | solution.py:52
  52.7 0.0 copy-start.2
  52.8 0.8 fusion.8
  53.5 0.8 fusion.7
  54.3 0.2 copy.57
  54.5 1.7 %convolution_subtract_fusion.1 = f32[1024,64]{0,1:T(8,128)S(1)} fusion(f32[1024,64]{0,1:T(8,128)} %fusion.28, f32[1024,128]{1,0:T(8,128)S(1)} %fusion, f32[128,64]{1,0:T(8,128)S(1)} %mul.400, f32[128]{0:T(128)S(1)} %mul.402), kind=kOutput, calls=%fused_computation.14 | convolution fusion | flops 100737024 | bytes 1081856 | tf_op jit(solution)/shard_map/dot_general | solution.py:31
  56.2 0.2 copy.56
  56.4 0.2 copy.61
  56.6 0.8 convolution_add_fusion.1
  57.4 0.2 copy.55
  57.6 0.2 copy.60
  57.8 0.0 copy-done.2
  57.8 0.8 convolution_bitcast_fusion
  58.6 0.1 maximum_bitcast_fusion
  58.7 0.6 copy.62
  59.2 1.9 %reshape.296 = f32[128,1,1536]{2,1,0:T(1,128)} reshape(f32[128,3,8,64]{3,2,1,0:T(8,128)S(1)} %copy.62) | data formatting | bytes 1572864
  61.1 12.5 %all-to-all-start.1 = ((f32[128,1,1536]{2,1,0:T(1,128)}), f32[128,1,1536]{2,1,0:T(1,128)S(1)}, u32[]{:S(2)}, u32[]{:S(2)}) async-start(f32[128,1,1536]{2,1,0:T(1,128)} %reshape.296), calls=%async_computation.1 | async-start | bytes 1572864 | tf_op jit(solution)/shard_map/all_to_all | solution.py:79
  73.6 0.1 convert_reduce_fusion
  73.8 25.6 %all-to-all-done.1 = f32[128,1,1536]{2,1,0:T(1,128)S(1)} async-done(((f32[128,1,1536]{2,1,0:T(1,128)}), f32[128,1,1536]{2,1,0:T(1,128)S(1)}, u32[]{:S(2)}, u32[]{:S(2)}) %all-to-all-start.1) | async-done | bytes 786464 | tf_op jit(solution)/shard_map/all_to_all | solution.py:79
  99.4 0.5 broadcast.316
  99.9 2.5 %reduce = f32[128,1536]{1,0:T(8,128)S(1)} reduce(f32[128,1,1536]{2,1,0:T(1,128)S(1)} %all-to-all-done.1, f32[]{:T(128)} %broadcast.316), dimensions={1}, to_apply=%all_to_all.7.reduce_sub_computation | reduce | bytes 1572868 | tf_op jit(solution)/shard_map/all_to_all | solution.py:79
  102.4 0.3 reshape.297
  102.8 0.2 reduce_sum.18
  102.9 0.1 copy.64
  103.0 17.1 %psum.7 = f32[8,16,4]{0,2,1:T(4,128)S(1)} all-reduce(f32[8,16,4]{0,2,1:T(4,128)S(1)} %bitcast.58), channel_id=1, replica_groups=mesh['chan'=128,'tm'=4] {'tm'}, use_global_device_ids=true, to_apply=%region_1.2 | all-reduce | flops 512 | bytes 4096 | tf_op jit(solution)/shard_map/psum | solution.py:83
  120.1 0.1 divide_bitcast_fusion
  120.2 0.7 copy.65
  (8 shorter events, 0.1 us)
Async XLA Ops:
  5.4 6.4 %copy-start = (bf16[1,8,16384]{2,1,0:T(8,128)(2,1)S(1)}, bf16[1,8,16384]{2,1,0:T(8,128)(2,1)}, u32[]{:S(2)}) copy-start(bf16[1,8,16384]{2,1,0:T(8,128)(2,1)} %param.5) | copy-start | bytes 786436
  11.8 22.8 %copy-start.3 = (s32[2048]{0:T(1024)S(1)}, s32[2048]{0:T(1024)}, u32[]{:S(2)}) copy-start(s32[2048]{0:T(1024)} %param.8) | copy-start | bytes 24580
  12.9 32.0 %all-to-all-start = ((bf16[128,8,128]{2,1,0:T(8,128)(2,1)}), bf16[128,8,128]{2,1,0:T(8,128)(2,1)S(1)}, u32[]{:S(2)}, u32[]{:S(2)}) async-start(bf16[128,8,128]{2,1,0:T(8,128)(2,1)} %copy.54), calls=%async_computation | async-start | bytes 524288 | tf_op jit(solution)/shard_map/all_to_all | solution.py:47
  44.9 3.9 %copy-start.1 = (bf16[128,8,128]{2,1,0:T(8,128)(2,1)}, bf16[128,8,128]{2,1,0:T(8,128)(2,1)S(1)}, u32[]{:S(2)}) copy-start(bf16[128,8,128]{2,1,0:T(8,128)(2,1)S(1)} %all-to-all-done) | copy-start | bytes 786436
  52.7 5.1 %copy-start.2 = (f32[64,64]{1,0:T(8,128)S(1)}, f32[64,64]{1,0:T(8,128)}, u32[]{:S(2)}) copy-start(f32[64,64]{1,0:T(8,128)} %mul.420) | copy-start | bytes 49156
  61.1 38.3 %all-to-all-start.1 = ((f32[128,1,1536]{2,1,0:T(1,128)}), f32[128,1,1536]{2,1,0:T(1,128)S(1)}, u32[]{:S(2)}, u32[]{:S(2)}) async-start(f32[128,1,1536]{2,1,0:T(1,128)} %reshape.296), calls=%async_computation.1 | async-start | bytes 1572864 | tf_op jit(solution)/shard_map/all_to_all | solution.py:79

commit v2 on v1

--- a/solution.py
+++ b/solution.py
@@ -31,6 +31,17 @@
     return jnp.dot(a, b, precision=lax.Precision.HIGHEST, preferred_element_type=jnp.float32)
 
 
+def tm_sum(x, n):
+    if n & (n - 1):
+        return lax.psum(x, "tm")
+    step = 1
+    while step < n:
+        pairs = [(i, i ^ step) for i in range(n)]
+        x = x + lax.ppermute(x, "tm", pairs)
+        step *= 2
+    return x
+
+
 def body(visibilities, flags, taper, group_ids):
     _, local_chans, column_entries = visibilities.shape
     baselines = column_entries // 8
@@ -40,10 +51,12 @@
     shard_cols = shard_bl * 8
     times_all = lax.axis_size("tm")
 
-    weight = (1 - flags[0]).astype(jnp.float32) * taper[:, None]
-    shaped = visibilities[0].reshape(local_chans, baselines, 8).astype(jnp.float32)
-    tapered = (shaped * weight[..., None]).astype(jnp.bfloat16)
-    tapered = tapered.reshape(local_chans, n_chan, shard_cols).transpose(1, 0, 2)
+    keep = (1 - flags[0]).astype(jnp.bfloat16).reshape(local_chans, n_chan, shard_bl)
+    spread = (jnp.arange(shard_cols, dtype=jnp.int32)[None, :] // 8
+              == jnp.arange(shard_bl, dtype=jnp.int32)[:, None]).astype(jnp.bfloat16)
+    keep_cols = jnp.einsum("cjb,bl->jcl", keep, spread, preferred_element_type=jnp.float32)
+    shaped = visibilities[0].reshape(local_chans, n_chan, shard_cols).transpose(1, 0, 2)
+    tapered = (shaped.astype(jnp.float32) * (keep_cols * taper[None, :, None])).astype(jnp.bfloat16)
     turned = lax.all_to_all(tapered, "chan", 0, 0, tiled=True)
     turned = turned.reshape(channels, shard_cols)
 
@@ -80,7 +93,7 @@
     else:
         owned = lax.psum_scatter(terms, "chan", scatter_dimension=0, tiled=True)[0]
     cross = owned[0] * owned[0] + owned[1] * owned[1] - owned[2]
-    cross = lax.psum(cross, "tm")
+    cross = tm_sum(cross, times_all)
 
     member_all = (group_ids[None, :] == jnp.arange(G, dtype=jnp.int32)[:, None]).astype(jnp.float32)
     counts = jnp.sum(member_all, axis=1)

time: 122 us -> 106 us (0.87)
  the two profiles are of different devices: /device:TPU:8 before, /device:TPU:6 now
where the time goes in v2:
time: 106 us; the launch traced here: 104 us
  blocking collectives  37.1 us (35%)
  starting transfers between devices  23.8 us (22%)
  other arithmetic  13.8 us (13%)
  matrix products  11.9 us (11%)
  local copies, waits for them, and re-layouts  9.94 us (9%)
  waiting for transfers between devices  7.55 us (7%)
    all_to_all x1, blocking collectives, body(): owned = jnp.sum(lax.all_to_all(terms, 'chan', 0, 0, tiled=True), axis=0)  37.1 us
    all_to_all x1, starting transfers between devices, body(): turned = lax.all_to_all(tapered, 'chan', 0, 0, tiled=True)  17.8 us
    dot_general x9, matrix products, hi_dot(): jnp.dot(a, b, precision=lax.Precision.HIGHEST, preferred_element_type=jnp...  7.57 us
    convert_element_type x1, other arithmetic, tables(): ((sa * cb + ca * sb) * scale).astype(jnp.bfloat16).reshape(length, length)  6.5 us
    ppermute x2, waiting for transfers between devices, tm_sum(): x = x + lax.ppermute(x, 'tm', pairs)  6.3 us
    ppermute x2, starting transfers between devices, tm_sum(): x = x + lax.ppermute(x, 'tm', pairs)  6.03 us
    all_to_all x1, other arithmetic, body(): owned = jnp.sum(lax.all_to_all(terms, 'chan', 0, 0, tiled=True), axis=0)  2.51 us
    dot_general x1, matrix products, body(): cos_part = jnp.dot(cos_tab, turned, preferred_element_type=jnp.float32)  2.39 us
  transfers between devices with their start and end apart: 3, of which 3 were waited for; matrix products, arithmetic and copies ran while one was open for 13% of the time, Pallas kernels for 0%

profile of v2, /device:TPU:6, one launch (start us, length us, event | category | flops | bytes accessed | tf_op | source)
XLA Modules:
  0.0 104.5 jit_solution(400234885229753179)
XLA Ops:
  0.0 0.9 subtract_convert_fusion
  0.9 0.2 convert_element_type.116
  1.1 1.0 convert_bitcast_fusion
  2.1 0.1 copy.88
  2.2 0.2 copy.53
  2.4 0.0 copy-done.4
  2.4 0.0 copy-start.3
  2.4 0.3 fusion.8
  2.7 0.9 copy.55
  3.6 17.8 %all-to-all-start = ((bf16[128,8,128]{2,1,0:T(8,128)(2,1)}), bf16[128,8,128]{2,1,0:T(8,128)(2,1)S(1)}, u32[]{:S(2)}, u32[]{:S(2)}) async-start(bf16[128,8,128]{2,1,0:T(8,128)(2,1)} %copy.55), calls=%async_computation | async-start | bytes 524288 | tf_op jit(solution)/shard_map/all_to_all | solution.py:60
  21.4 2.1 %fusion.21 = (f32[1024,128]{1,0:T(8,128)S(1)}, f32[1024,128]{1,0:T(8,128)S(1)}) fusion(), kind=kLoop, calls=%fused_computation.37 | loop fusion | flops 1835008 | bytes 1048576 | tf_op jit(solution)/shard_map/sin | solution.py:23
  23.5 0.2 fusion.51
  23.7 1.0 copy.52
  24.7 1.0 copy.51
  25.7 0.0 copy-done.3
  25.7 0.1 dynamic_slice.3
  25.8 0.1 fusion.54
  25.9 0.1 broadcast_multiply_fusion.1
  26.0 0.1 mul.404
  26.1 0.5 mul.405
  26.6 0.1 mul.392
  26.8 0.1 mul.399
  26.9 0.8 mul.410
  27.7 0.1 mul.389
  27.8 0.5 mul.390
  28.3 6.5 %multiply_convert_fusion = (bf16[1024,8,128]{2,1,0:T(8,128)(2,1)S(1)}, bf16[1024,8,128]{2,1,0:T(8,128)(2,1)}) fusion(f32[1024,128]{1,0:T(8,128)S(1)} %get-tuple-element.11, f32[1024,8]{1,0:T(8,128)} %copy.52, f32[1024,128]{1,0:T(8,128)S(1)} %get-tuple-element.12, f32[1024,8]{1,0:T(8,128)} %copy.51), kind=kLoop, calls=%fused_computation | loop fusion | flops 10485760 | bytes 5308416 | tf_op jit(solution)/shard_map/convert_element_type | solution.py:26
  34.8 1.3 %all-to-all-done = bf16[128,8,128]{2,1,0:T(8,128)(2,1)S(1)} async-done(((bf16[128,8,128]{2,1,0:T(8,128)(2,1)}), bf16[128,8,128]{2,1,0:T(8,128)(2,1)S(1)}, u32[]{:S(2)}, u32[]{:S(2)}) %all-to-all-start) | async-done | bytes 262176 | tf_op jit(solution)/shard_map/all_to_all | solution.py:60
  36.1 2.4 %fusion.3 = f32[1024,128]{1,0:T(8,128)S(1)} fusion(bf16[128,8,8,128]{3,2,1,0:T(8,128)(2,1)} %bitcast.65, bf16[128,8,128]{2,1,0:T(8,128)(2,1)S(1)} %all-to-all-done), kind=kOutput, calls=%fused_computation.5 | convolution fusion | flops 268435456 | bytes 2883584 | tf_op jit(solution)/shard_map/dot_general | solution.py:64
  38.5 0.8 fusion.27
  39.3 0.8 fusion.23
  40.0 0.0 copy-done.1
  40.0 1.5 %fusion.29 = f32[1024,64]{0,1:T(8,128)} fusion(f32[1024,128]{1,0:T(8,128)S(1)} %fusion.3, f32[128,64]{1,0:T(8,128)S(1)} %mul.390, f32[128]{0:T(128)S(1)} %mul.399), kind=kOutput, calls=%fused_computation.48 | convolution fusion | flops 100671488 | bytes 819712 | tf_op jit(solution)/shard_map/dot_general | solution.py:31
  41.5 0.8 fusion.33
  42.3 1.7 %fusion = f32[1024,128]{1,0:T(8,128)S(1)} fusion(bf16[128,8,8,128]{3,2,1,0:T(8,128)(2,1)S(1)} %bitcast.64, bf16[128,8,128]{2,1,0:T(8,128)(2,1)} %copy-done.1), kind=kOutput, calls=%fused_computation.2 | convolution fusion | flops 268435456 | bytes 2883584 | tf_op jit(solution)/shard_map/dot_general | solution.py:65
  43.9 0.0 copy-start
  43.9 0.8 fusion.11
  44.7 0.8 fusion.10
  45.5 0.2 copy.58
  45.7 0.0 copy-done
  45.7 0.8 convolution_subtract_fusion.1
  46.5 0.0 copy-start.2
  46.5 0.2 copy.57
  46.7 0.2 copy.62
  46.9 0.8 convolution_add_fusion.1
  47.7 0.2 copy.56
  47.9 0.2 copy.61
  48.1 0.0 copy-done.2
  48.1 0.8 convolution_bitcast_fusion
  48.9 0.1 maximum_bitcast_fusion
  48.9 0.6 copy.63
  49.5 1.0 reshape.311
  50.5 37.1 %all_to_all.10 = f32[128,1,1536]{2,1,0:T(1,128)S(1)} all-to-all(f32[128,1,1536]{2,1,0:T(1,128)S(1)} %reshape.311), channel_id=1, replica_groups=mesh['chan'=128,'tm'=4] {'chan'}, dimensions={0} | all-to-all | bytes 1572864 | tf_op jit(solution)/shard_map/all_to_all | solution.py:92
  87.5 0.5 broadcast.342
  88.1 2.5 %reduce = f32[128,1536]{1,0:T(8,128)S(1)} reduce(f32[128,1,1536]{2,1,0:T(1,128)S(1)} %all_to_all.10, f32[]{:T(128)} %broadcast.342), dimensions={1}, to_apply=%all_to_all.7.reduce_sub_computation | reduce | bytes 1572868 | tf_op jit(solution)/shard_map/all_to_all | solution.py:92
  90.6 0.3 reshape.312
  90.9 0.2 reduce_sum.18
  91.1 2.7 %collective-permute-start = (f32[8,64]{1,0:T(8,128)S(1)}, f32[8,64]{1,0:T(8,128)S(1)}, u32[]{:S(2)}, u32[]{:S(2)}) collective-permute-start(f32[8,64]{1,0:T(8,128)S(1)} %fusion.57), channel_id=1, source_target_pairs={{0,1},{1,0},{2,3},{3,2},{4,5},{5,4},{6,7},{7,6},{8,9},{9,8},{10,11... | collective-permute-start | bytes 6152 | tf_op jit(solution)/shard_map/ppermute | solution.py:40
  93.8 0.1 convert_reduce_fusion
  94.0 2.6 %collective-permute-done = f32[8,64]{1,0:T(8,128)S(1)} collective-permute-done((f32[8,64]{1,0:T(8,128)S(1)}, f32[8,64]{1,0:T(8,128)S(1)}, u32[]{:S(2)}, u32[]{:S(2)}) %collective-permute-start) | collective-permute-done | bytes 2080 | tf_op jit(solution)/shard_map/ppermute | solution.py:40
  96.6 3.3 %collective-permute-start.1 = (f32[8,64]{1,0:T(8,128)S(1)}, f32[8,64]{1,0:T(8,128)S(1)}, u32[]{:S(2)}, u32[]{:S(2)}) collective-permute-start(f32[8,64]{1,0:T(8,128)S(1)} %fusion.73), channel_id=1, source_target_pairs={{0,2},{1,3},{2,0},{3,1},{4,6},{5,7},{6,4},{7,5},{8,10},{9,11},{10,... | collective-permute-start | bytes 6152 | tf_op jit(solution)/shard_map/ppermute | solution.py:40
  99.9 3.7 %collective-permute-done.1 = f32[8,64]{1,0:T(8,128)S(1)} collective-permute-done((f32[8,64]{1,0:T(8,128)S(1)}, f32[8,64]{1,0:T(8,128)S(1)}, u32[]{:S(2)}, u32[]{:S(2)}) %collective-permute-start.1) | collective-permute-done | bytes 2080 | tf_op jit(solution)/shard_map/ppermute | solution.py:40
  103.6 0.1 copy.65
  103.7 0.1 divide_bitcast_fusion
  103.8 0.7 copy.66
  (12 shorter events, 0.1 us)
Async XLA Ops:
  0.0 2.4 %copy-start.4 = (f32[8]{0:T(128)S(1)}, f32[8]{0:T(128)}, u32[]{:S(2)}) copy-start(f32[8]{0:T(128)} %param.7) | copy-start | bytes 100
  2.4 23.3 %copy-start.3 = (s32[2048]{0:T(1024)S(1)}, s32[2048]{0:T(1024)}, u32[]{:S(2)}) copy-start(s32[2048]{0:T(1024)} %param.8) | copy-start | bytes 24580
  3.6 32.5 %all-to-all-start = ((bf16[128,8,128]{2,1,0:T(8,128)(2,1)}), bf16[128,8,128]{2,1,0:T(8,128)(2,1)S(1)}, u32[]{:S(2)}, u32[]{:S(2)}) async-start(bf16[128,8,128]{2,1,0:T(8,128)(2,1)} %copy.55), calls=%async_computation | async-start | bytes 524288 | tf_op jit(solution)/shard_map/all_to_all | solution.py:60
  36.1 3.9 %copy-start.1 = (bf16[128,8,128]{2,1,0:T(8,128)(2,1)}, bf16[128,8,128]{2,1,0:T(8,128)(2,1)S(1)}, u32[]{:S(2)}) copy-start(bf16[128,8,128]{2,1,0:T(8,128)(2,1)S(1)} %all-to-all-done) | copy-start | bytes 786436
  43.9 1.8 %copy-start = (f32[1024,64]{0,1:T(8,128)S(1)}, f32[1024,64]{0,1:T(8,128)}, u32[]{:S(2)}) copy-start(f32[1024,64]{0,1:T(8,128)} %fusion.29) | copy-start | bytes 786436
  46.5 1.6 %copy-start.2 = (f32[64,64]{1,0:T(8,128)S(1)}, f32[64,64]{1,0:T(8,128)}, u32[]{:S(2)}) copy-start(f32[64,64]{1,0:T(8,128)} %mul.410) | copy-start | bytes 49156
  91.1 5.5 %collective-permute-start = (f32[8,64]{1,0:T(8,128)S(1)}, f32[8,64]{1,0:T(8,128)S(1)}, u32[]{:S(2)}, u32[]{:S(2)}) collective-permute-start(f32[8,64]{1,0:T(8,128)S(1)} %fusion.57), channel_id=1, source_target_pairs={{0,1},{1,0},{2,3},{3,2},{4,5},{5,4},{6,7},{7,6},{8,9},{9,8},{10,11... | collective-permute-start | bytes 6152 | tf_op jit(solution)/shard_map/ppermute | solution.py:40
  96.6 7.0 %collective-permute-start.1 = (f32[8,64]{1,0:T(8,128)S(1)}, f32[8,64]{1,0:T(8,128)S(1)}, u32[]{:S(2)}, u32[]{:S(2)}) collective-permute-start(f32[8,64]{1,0:T(8,128)S(1)} %fusion.73), channel_id=1, source_target_pairs={{0,2},{1,3},{2,0},{3,1},{4,6},{5,7},{6,4},{7,5},{8,10},{9,11},{10,... | collective-permute-start | bytes 6152 | tf_op jit(solution)/shard_map/ppermute | solution.py:40

commit v3 on v2

--- a/solution.py
+++ b/solution.py
@@ -6,7 +6,6 @@
 from jax.sharding import PartitionSpec as P
 
 G = 16
-REDUCE_BY_ALL_TO_ALL = True
 
 
 def tables(length, minor):
@@ -64,6 +63,18 @@
     cos_part = jnp.dot(cos_tab, turned, preferred_element_type=jnp.float32)
     sin_part = jnp.dot(sin_tab, turned, preferred_element_type=jnp.float32)
 
+    member_full = (group_ids[:, None] == jnp.arange(G, dtype=jnp.int32)[None, :]).astype(jnp.bfloat16)
+    member_full = member_full.reshape(n_chan, shard_bl, G)
+    sums = jnp.einsum("jcbk,jbg->cgk", tapered.reshape(n_chan, local_chans, shard_bl, 8), member_full,
+                      preferred_element_type=jnp.float32)
+    sums = sums.reshape(local_chans, G * 8).T
+    column = lax.all_to_all(sums, "chan", 0, 0, tiled=True).reshape(channels)
+    col_hi = column.astype(jnp.bfloat16)
+    col_lo = (column - col_hi.astype(jnp.float32)).astype(jnp.bfloat16)
+    col_parts = jnp.stack([col_hi, col_lo], axis=1)
+    col_cos = jnp.sum(jnp.dot(cos_tab, col_parts, preferred_element_type=jnp.float32), axis=1)
+    col_sin = jnp.sum(jnp.dot(sin_tab, col_parts, preferred_element_type=jnp.float32), axis=1)
+
     me = lax.axis_index("chan")
     shard_groups = lax.dynamic_slice_in_dim(group_ids, me * shard_bl, shard_bl)
     member = (shard_groups[:, None] == jnp.arange(G, dtype=jnp.int32)[None, :]).astype(jnp.float32)
@@ -71,35 +82,33 @@
     eye_b = jnp.eye(shard_bl, dtype=jnp.float32)
     r_one = jnp.array([0.0, 1.0], jnp.float32)
     r_zero = 1.0 - r_one
-    m_gs = member[:, None, None, :, None] * eye_s[None, :, None, None, :]
-    m0 = (m_gs * r_zero[None, None, :, None, None]).reshape(shard_cols, G * 4)
-    m1 = (m_gs * r_one[None, None, :, None, None]).reshape(shard_cols, G * 4)
     p_bs = eye_b[:, None, None, :, None] * eye_s[None, :, None, None, :]
     p0 = (p_bs * r_zero[None, None, :, None, None]).reshape(shard_cols, shard_bl * 4)
     p1 = (p_bs * r_one[None, None, :, None, None]).reshape(shard_cols, shard_bl * 4)
     m_pow = (member[:, None, :, None] * eye_s[None, :, None, :]).reshape(shard_bl * 4, G * 4)
-
-    group_real = hi_dot(cos_part, m0) + hi_dot(sin_part, m1)
-    group_imag = hi_dot(cos_part, m1) - hi_dot(sin_part, m0)
     real_part = hi_dot(cos_part, p0) + hi_dot(sin_part, p1)
     imag_part = hi_dot(cos_part, p1) - hi_dot(sin_part, p0)
     auto = hi_dot(real_part * real_part + imag_part * imag_part, m_pow)
 
     own_d = channels // n_chan
-    terms = jnp.stack([group_real, group_imag, auto], axis=0)
-    terms = terms.reshape(3, n_chan, own_d, G * 4).transpose(1, 0, 2, 3)
-    if REDUCE_BY_ALL_TO_ALL:
-        owned = jnp.sum(lax.all_to_all(terms, "chan", 0, 0, tiled=True), axis=0)
-    else:
-        owned = lax.psum_scatter(terms, "chan", scatter_dimension=0, tiled=True)[0]
-    cross = owned[0] * owned[0] + owned[1] * owned[1] - owned[2]
+    payload = jnp.concatenate([
+        auto.reshape(n_chan, own_d * G * 4),
+        col_cos.reshape(n_chan, own_d),
+        col_sin.reshape(n_chan, own_d),
+    ], axis=1)
+    got = lax.all_to_all(payload, "chan", 0, 0, tiled=True)
+    auto_own = jnp.sum(got[:, :own_d * G * 4], axis=0).reshape(own_d, G, 4)
+    cs = got[:, own_d * G * 4:].reshape(G, 4, 2, 2, own_d)
+    group_real = cs[:, :, 0, 0] + cs[:, :, 1, 1]
+    group_imag = cs[:, :, 1, 0] - cs[:, :, 0, 1]
+    cross = group_real * group_real + group_imag * group_imag - auto_own.transpose(1, 2, 0)
     cross = tm_sum(cross, times_all)
 
     member_all = (group_ids[None, :] == jnp.arange(G, dtype=jnp.int32)[:, None]).astype(jnp.float32)
     counts = jnp.sum(member_all, axis=1)
     pair_count = jnp.maximum(counts * (counts - 1.0), 1.0)
     norm = jnp.sqrt(pair_count * times_all)
-    spectrum = cross.reshape(own_d, G, 4).transpose(2, 1, 0)
+    spectrum = cross.transpose(1, 0, 2)
     return spectrum / norm[None, :, None]
 
 

time: 106 us -> 111 us (1.047); the launches traced: 104 us -> 111 us
  blocking collectives: 37.1 us -> 21.5 us
  starting transfers between devices: 23.8 us -> 37.8 us
  waiting for transfers between devices: 7.55 us -> 16.9 us
  matrix products: 11.9 us -> 10.5 us
    all_to_all x0 -> x1, starting transfers between devices: none -> 17.8 us  [body(): column = lax.all_to_all(sums, 'chan', 0, 0, tiled=True).reshape(channels)]
    all_to_all x1, blocking collectives: 37.1 us -> 21.5 us  [body(): got = lax.all_to_all(payload, 'chan', 0, 0, tiled=True)]
    all_to_all x1, waiting for transfers between devices: 1.26 us -> 9.99 us  [body(): turned = lax.all_to_all(tapered, 'chan', 0, 0, tiled=True)]
    all_to_all x1, starting transfers between devices: 17.8 us -> 13.9 us  [body(): turned = lax.all_to_all(tapered, 'chan', 0, 0, tiled=True)]
    dot_general x9 -> x5, matrix products: 7.57 us -> 4.05 us  [hi_dot(): jnp.dot(a, b, precision=lax.Precision.HIGHEST, preferred_element_type=jnp...]
    dot_general x0 -> x3, matrix products: none -> 3.13 us  [the longest x1 2.25 us: body(): jnp.dot(cos_tab, col_parts, preferred_element_type=jnp.float32)]
    all_to_all x1 -> x2, other arithmetic: 2.51 us -> 0.9 us  [the longest x1 0.81 us: body(): column = lax.all_to_all(sums, 'chan', 0, 0, tiled=True).reshape(channels)]
    unnamed x13 -> x5, local copies, waits for them, and re-layouts: 1.44 us -> 0.11 us
  transfers between devices with their start and end apart: 3 -> 4, of which waited for: 3 -> 3; matrix products, arithmetic and copies ran while one was open for 13% -> 19% of each run, Pallas kernels for 0% -> 0%
where the time goes in v3:
time: 111 us
  starting transfers between devices  37.8 us (34%)
  blocking collectives  21.5 us (19%)
  waiting for transfers between devices  16.9 us (15%)
  other arithmetic  13.2 us (12%)
  matrix products  10.5 us (9%)
  local copies, waits for them, and re-layouts  10.3 us (9%)
    all_to_all x1, blocking collectives, body(): got = lax.all_to_all(payload, 'chan', 0, 0, tiled=True)  21.5 us
    all_to_all x1, starting transfers between devices, body(): column = lax.all_to_all(sums, 'chan', 0, 0, tiled=True).reshape(channels)  17.8 us
    all_to_all x1, starting transfers between devices, body(): turned = lax.all_to_all(tapered, 'chan', 0, 0, tiled=True)  13.9 us
    all_to_all x1, waiting for transfers between devices, body(): turned = lax.all_to_all(tapered, 'chan', 0, 0, tiled=True)  9.99 us
    ppermute x2, waiting for transfers between devices, tm_sum(): x = x + lax.ppermute(x, 'tm', pairs)  6.91 us
    convert_element_type x1, other arithmetic, tables(): ((ca * cb - sa * sb) * scale).astype(jnp.bfloat16).reshape(length, length)  6.51 us
    ppermute x2, starting transfers between devices, tm_sum(): x = x + lax.ppermute(x, 'tm', pairs)  6.04 us
    dot_general x5, matrix products, hi_dot(): jnp.dot(a, b, precision=lax.Precision.HIGHEST, preferred_element_type=jnp...  4.05 us
  transfers between devices with their start and end apart: 4, of which 3 were waited for; matrix products, arithmetic and copies ran while one was open for 19% of the time, Pallas kernels for 0%

profile of v3, /device:TPU:6, one launch (start us, length us, event | category | flops | bytes accessed | tf_op | source)
XLA Modules:
  0.0 110.6 jit_solution(17346087731575904861)
XLA Ops:
  0.0 0.9 subtract_convert_fusion
  0.9 0.2 convert_element_type.165
  1.1 1.0 convert_bitcast_fusion
  2.1 0.1 copy.91
  2.2 0.2 copy.52
  2.4 0.0 copy-done
  2.4 0.1 eq.95
  2.5 0.1 copy.56
  2.6 0.0 copy-done.1
  2.6 0.3 fusion.14
  2.9 0.2 convolution_bitcast_fusion
  3.1 0.1 copy.57
  3.1 0.1 reshape.339
  3.2 0.7 copy.58
  4.0 17.8 %all-to-all-start.1 = ((f32[128,1,8]{2,1,0:T(1,128)}), f32[128,1,8]{2,1,0:T(1,128)S(1)}, u32[]{:S(2)}, u32[]{:S(2)}) async-start(f32[128,1,8]{2,1,0:T(1,128)} %copy.58), calls=%async_computation.1 | async-start | bytes 131072 | tf_op jit(solution)/shard_map/all_to_all | solution.py:71
  21.8 2.1 %fusion.33 = (f32[1024,128]{1,0:T(8,128)S(1)}, f32[1024,128]{1,0:T(8,128)S(1)}) fusion(), kind=kLoop, calls=%fused_computation.44 | loop fusion | flops 1835008 | bytes 1048576 | tf_op jit(solution)/shard_map/sin | solution.py:22
  23.9 0.2 fusion.58
  24.1 1.0 copy.51
  25.1 1.0 copy.50
  26.1 0.1 dynamic_slice.3
  26.2 0.1 fusion.61
  26.3 1.1 %broadcast_multiply_fusion = (f32[16,4,16,4]{3,2,1,0:T(8,128)}, f32[16,4,16,4]{3,2,1,0:T(8,128)}) fusion(f32[16,16]{1,0:T(8,128)S(1)} %get-tuple-element.16, f32[4,4]{1,0:T(4,128)S(1)} %fusion.65, f32[16,16]{1,0:T(8,128)S(1)} %get-tuple-element.15), kind=kLoop, calls=%fused_computation.42 | loop fusion | flops 8192 | bytes 34880 | tf_op jit(solution)/shard_map/mul | solution.py:88
  27.4 6.5 %multiply_convert_fusion.1 = (bf16[1024,8,128]{2,1,0:T(8,128)(2,1)}, bf16[1024,8,128]{2,1,0:T(8,128)(2,1)S(1)}) fusion(f32[1024,128]{1,0:T(8,128)S(1)} %get-tuple-element.13, f32[1024,8]{1,0:T(8,128)} %copy.51, f32[1024,128]{1,0:T(8,128)S(1)} %get-tuple-element.14, f32[1024,8]{1,0:T(8,128)} %copy.50), kind=kLoop, calls=%fused_computation.1 | loop fusion | flops 10485760 | bytes 5308416 | tf_op jit(solution)/shard_map/convert_element_type | solution.py:24
  33.9 0.9 copy.54
  34.8 1.1 %mul.418 = f32[16,4,2,16,4]{4,3,2,1,0:T(8,128)S(1)} broadcast(f32[16,4,16,4]{3,2,1,0:T(8,128)} %get-tuple-element.10), dimensions={0,1,3,4} | broadcast | bytes 49152 | tf_op jit(solution)/shard_map/mul | solution.py:86
  36.0 0.5 mul.419
  36.5 0.1 mul.421
  36.6 0.1 mul.428
  36.8 1.3 %mul.436 = f32[64,64]{1,0:T(8,128)S(1)} reshape(f32[16,4,16,4]{3,2,1,0:T(8,128)} %get-tuple-element.9) | data formatting | bytes 32768 | tf_op jit(solution)/shard_map/mul | solution.py:88
  38.0 0.0 all-to-all-done.1
  38.0 13.9 %all-to-all-start = ((bf16[128,8,128]{2,1,0:T(8,128)(2,1)}), bf16[128,8,128]{2,1,0:T(8,128)(2,1)S(1)}, u32[]{:S(2)}, u32[]{:S(2)}) async-start(bf16[128,8,128]{2,1,0:T(8,128)(2,1)} %copy.54), calls=%async_computation | async-start | bytes 524288 | tf_op jit(solution)/shard_map/all_to_all | solution.py:59
  52.0 0.5 broadcast.319
  52.5 0.8 reduce.3
  53.3 0.1 reshape.340
  53.4 0.7 fusion.21
  54.1 0.1 reshape.342
  54.2 2.3 %fusion.18 = f32[1024]{0:T(1024)S(1)} fusion(bf16[128,8,8,128]{3,2,1,0:T(8,128)(2,1)} %bitcast.75, bf16[1024,1]{0,1:T(2,128)(2,1)S(1)} %get-tuple-element.8, bf16[1024,1]{0,1:T(2,128)(2,1)S(1)} %get-tuple-element.7), kind=kOutput, calls=%fused_computation.24 | convolution fusion | flops 4203520 | bytes 2105344 | tf_op jit(solution)/shard_map/dot_general | solution.py:75
  56.4 0.1 reshape.341
  56.5 10.0 %all-to-all-done = bf16[128,8,128]{2,1,0:T(8,128)(2,1)S(1)} async-done(((bf16[128,8,128]{2,1,0:T(8,128)(2,1)}), bf16[128,8,128]{2,1,0:T(8,128)(2,1)S(1)}, u32[]{:S(2)}, u32[]{:S(2)}) %all-to-all-start) | async-done | bytes 262176 | tf_op jit(solution)/shard_map/all_to_all | solution.py:59
  66.5 2.3 %fusion.6 = f32[1024,128]{1,0:T(8,128)S(1)} fusion(bf16[128,8,8,128]{3,2,1,0:T(8,128)(2,1)} %bitcast.76, bf16[128,8,128]{2,1,0:T(8,128)(2,1)S(1)} %all-to-all-done), kind=kOutput, calls=%fused_computation.8 | convolution fusion | flops 268435456 | bytes 2883584 | tf_op jit(solution)/shard_map/dot_general | solution.py:63
  68.8 0.8 fusion.42
  69.6 0.8 fusion.38
  70.3 0.7 fusion.2
  71.1 0.8 fusion.17
  71.8 0.8 fusion.16
  72.6 1.0 fusion.70
  73.6 0.1 reshape.337
  73.8 0.1 maximum_bitcast_fusion
  73.8 0.3 copy.59
  74.2 21.5 %all_to_all.26 = f32[128,1,528]{2,1,0:T(1,128)S(1)} all-to-all(f32[128,1,528]{2,1,0:T(1,128)S(1)} %copy.59), channel_id=1, replica_groups=mesh['chan'=128,'tm'=4] {'chan'}, dimensions={0} | all-to-all | bytes 540672 | tf_op jit(solution)/shard_map/all_to_all | solution.py:99
  95.7 0.2 copy.60
  95.9 0.1 slice_reduce_fusion
  96.0 0.1 copy.61
  96.1 0.1 reshape.343
  96.3 0.1 fusion.48
  96.4 0.1 reshape.344
  96.5 0.2 copy.62
  96.7 2.7 %collective-permute-start = (f32[16,4,8]{2,1,0:T(4,128)S(1)}, f32[16,4,8]{2,1,0:T(4,128)S(1)}, u32[]{:S(2)}, u32[]{:S(2)}) collective-permute-start(f32[16,4,8]{2,1,0:T(4,128)S(1)} %bitcast_subtract_fusion), channel_id=1, source_target_pairs={{0,1},{1,0},{2,3},{3,2},{4,5},{5,4},{6,7},{7,6},{8,9},{9,8},{10,11... | collective-permute-start | bytes 6152 | tf_op jit(solution)/shard_map/ppermute | solution.py:39
  99.4 0.1 convert_reduce_fusion
  99.6 2.9 %collective-permute-done = f32[16,4,8]{2,1,0:T(4,128)S(1)} collective-permute-done((f32[16,4,8]{2,1,0:T(4,128)S(1)}, f32[16,4,8]{2,1,0:T(4,128)S(1)}, u32[]{:S(2)}, u32[]{:S(2)}) %collective-permute-start) | collective-permute-done | bytes 2080 | tf_op jit(solution)/shard_map/ppermute | solution.py:39
  102.5 3.3 %collective-permute-start.1 = (f32[16,4,8]{2,1,0:T(4,128)S(1)}, f32[16,4,8]{2,1,0:T(4,128)S(1)}, u32[]{:S(2)}, u32[]{:S(2)}) collective-permute-start(f32[16,4,8]{2,1,0:T(4,128)S(1)} %add.97), channel_id=1, source_target_pairs={{0,2},{1,3},{2,0},{3,1},{4,6},{5,7},{6,4},{7,5},{8,10},{9,11},{10,... | collective-permute-start | bytes 6152 | tf_op jit(solution)/shard_map/ppermute | solution.py:39
  105.8 4.0 %collective-permute-done.1 = f32[16,4,8]{2,1,0:T(4,128)S(1)} collective-permute-done((f32[16,4,8]{2,1,0:T(4,128)S(1)}, f32[16,4,8]{2,1,0:T(4,128)S(1)}, u32[]{:S(2)}, u32[]{:S(2)}) %collective-permute-start.1) | collective-permute-done | bytes 2080 | tf_op jit(solution)/shard_map/ppermute | solution.py:39
  109.8 0.1 divide_bitcast_fusion
  109.9 0.7 copy.63
  (13 shorter events, 0.1 us)
Async XLA Ops:
  0.0 2.4 %copy-start = (s32[2048]{0:T(1024)S(1)}, s32[2048]{0:T(1024)}, u32[]{:S(2)}) copy-start(s32[2048]{0:T(1024)} %param.8) | copy-start | bytes 24580
  0.0 2.6 %copy-start.1 = (f32[8]{0:T(128)S(1)}, f32[8]{0:T(128)}, u32[]{:S(2)}) copy-start(f32[8]{0:T(128)} %param.7) | copy-start | bytes 100
  4.0 34.1 %all-to-all-start.1 = ((f32[128,1,8]{2,1,0:T(1,128)}), f32[128,1,8]{2,1,0:T(1,128)S(1)}, u32[]{:S(2)}, u32[]{:S(2)}) async-start(f32[128,1,8]{2,1,0:T(1,128)} %copy.58), calls=%async_computation.1 | async-start | bytes 131072 | tf_op jit(solution)/shard_map/all_to_all | solution.py:71
  38.0 28.5 %all-to-all-start = ((bf16[128,8,128]{2,1,0:T(8,128)(2,1)}), bf16[128,8,128]{2,1,0:T(8,128)(2,1)S(1)}, u32[]{:S(2)}, u32[]{:S(2)}) async-start(bf16[128,8,128]{2,1,0:T(8,128)(2,1)} %copy.54), calls=%async_computation | async-start | bytes 524288 | tf_op jit(solution)/shard_map/all_to_all | solution.py:59
  96.7 5.8 %collective-permute-start = (f32[16,4,8]{2,1,0:T(4,128)S(1)}, f32[16,4,8]{2,1,0:T(4,128)S(1)}, u32[]{:S(2)}, u32[]{:S(2)}) collective-permute-start(f32[16,4,8]{2,1,0:T(4,128)S(1)} %bitcast_subtract_fusion), channel_id=1, source_target_pairs={{0,1},{1,0},{2,3},{3,2},{4,5},{5,4},{6,7},{7,6},{8,9},{9,8},{10,11... | collective-permute-start | bytes 6152 | tf_op jit(solution)/shard_map/ppermute | solution.py:39
  102.5 7.3 %collective-permute-start.1 = (f32[16,4,8]{2,1,0:T(4,128)S(1)}, f32[16,4,8]{2,1,0:T(4,128)S(1)}, u32[]{:S(2)}, u32[]{:S(2)}) collective-permute-start(f32[16,4,8]{2,1,0:T(4,128)S(1)} %add.97), channel_id=1, source_target_pairs={{0,2},{1,3},{2,0},{3,1},{4,6},{5,7},{6,4},{7,5},{8,10},{9,11},{10,... | collective-permute-start | bytes 6152 | tf_op jit(solution)/shard_map/ppermute | solution.py:39

commit v4 on v3

--- a/solution.py
+++ b/solution.py
@@ -56,22 +56,30 @@
     keep_cols = jnp.einsum("cjb,bl->jcl", keep, spread, preferred_element_type=jnp.float32)
     shaped = visibilities[0].reshape(local_chans, n_chan, shard_cols).transpose(1, 0, 2)
     tapered = (shaped.astype(jnp.float32) * (keep_cols * taper[None, :, None])).astype(jnp.bfloat16)
-    turned = lax.all_to_all(tapered, "chan", 0, 0, tiled=True)
-    turned = turned.reshape(channels, shard_cols)
-
-    cos_tab, sin_tab = tables(channels, 128)
-    cos_part = jnp.dot(cos_tab, turned, preferred_element_type=jnp.float32)
-    sin_part = jnp.dot(sin_tab, turned, preferred_element_type=jnp.float32)
 
     member_full = (group_ids[:, None] == jnp.arange(G, dtype=jnp.int32)[None, :]).astype(jnp.bfloat16)
     member_full = member_full.reshape(n_chan, shard_bl, G)
     sums = jnp.einsum("jcbk,jbg->cgk", tapered.reshape(n_chan, local_chans, shard_bl, 8), member_full,
                       preferred_element_type=jnp.float32)
     sums = sums.reshape(local_chans, G * 8).T
-    column = lax.all_to_all(sums, "chan", 0, 0, tiled=True).reshape(channels)
-    col_hi = column.astype(jnp.bfloat16)
-    col_lo = (column - col_hi.astype(jnp.float32)).astype(jnp.bfloat16)
-    col_parts = jnp.stack([col_hi, col_lo], axis=1)
+    sums_hi = lax.reduce_precision(sums, exponent_bits=8, mantissa_bits=7)
+    sums_lo = sums - sums_hi
+    block = local_chans * shard_cols
+    pad = -(block + 2 * local_chans) % 128
+    payload = jnp.concatenate([
+        tapered.reshape(n_chan, block),
+        sums_hi.astype(jnp.bfloat16),
+        sums_lo.astype(jnp.bfloat16),
+        jnp.zeros((n_chan, pad), jnp.bfloat16),
+    ], axis=1)
+    got = lax.all_to_all(payload.reshape(n_chan, 1, -1), "chan", 0, 0, tiled=True).reshape(n_chan, -1)
+    turned = got[:, :block].reshape(channels, shard_cols)
+    col_parts = got[:, block:block + 2 * local_chans].reshape(n_chan, 2, local_chans)
+    col_parts = col_parts.transpose(0, 2, 1).reshape(channels, 2)
+
+    cos_tab, sin_tab = tables(channels, 128)
+    cos_part = jnp.dot(cos_tab, turned, preferred_element_type=jnp.float32)
+    sin_part = jnp.dot(sin_tab, turned, preferred_element_type=jnp.float32)
     col_cos = jnp.sum(jnp.dot(cos_tab, col_parts, preferred_element_type=jnp.float32), axis=1)
     col_sin = jnp.sum(jnp.dot(sin_tab, col_parts, preferred_element_type=jnp.float32), axis=1)
 

time: 111 us -> 93.9 us (0.85)
  starting transfers between devices: 37.8 us -> 24 us
  waiting for transfers between devices: 16.9 us -> 9.85 us
  blocking collectives: 21.5 us -> 26.4 us
  matrix products: 10.5 us -> 8.88 us
    all_to_all x2 -> x1, starting transfers between devices: 31.7 us -> 18 us  [body(): lax.all_to_all(payload.reshape(n_chan, 1, -1), 'chan', 0, 0, tiled=True)]
    all_to_all x2 -> x1, waiting for transfers between devices: 9.99 us -> 2.94 us  [body(): lax.all_to_all(payload.reshape(n_chan, 1, -1), 'chan', 0, 0, tiled=True)]
    all_to_all x1, blocking collectives: 21.5 us -> 26.4 us  [body(): got = lax.all_to_all(payload, 'chan', 0, 0, tiled=True)]
    unnamed x5 -> x11, local copies, waits for them, and re-layouts: 0.11 us -> 2.58 us
    dot_general x1, matrix products: 2.25 us -> 0.66 us  [body(): jnp.dot(cos_tab, col_parts, preferred_element_type=jnp.float32)]
  transfers between devices with their start and end apart: 4 -> 3, of which waited for: 3 -> 3; matrix products, arithmetic and copies ran while one was open for 19% -> 14% of each run, Pallas kernels for 0% -> 0%
where the time goes in v4:
time: 93.9 us; the launch traced here: 93.2 us
  blocking collectives  26.4 us (28%)
  starting transfers between devices  24 us (26%)
  other arithmetic  12.2 us (13%)
  local copies, waits for them, and re-layouts  11.3 us (12%)
  waiting for transfers between devices  9.85 us (10%)
  matrix products  8.88 us (9%)
    all_to_all x1, blocking collectives, body(): got = lax.all_to_all(payload, 'chan', 0, 0, tiled=True)  26.4 us
    all_to_all x1, starting transfers between devices, body(): lax.all_to_all(payload.reshape(n_chan, 1, -1), 'chan', 0, 0, tiled=True)  18 us
    ppermute x2, waiting for transfers between devices, tm_sum(): x = x + lax.ppermute(x, 'tm', pairs)  6.91 us
    convert_element_type x1, other arithmetic, tables(): ((ca * cb - sa * sb) * scale).astype(jnp.bfloat16).reshape(length, length)  6.51 us
    ppermute x2, starting transfers between devices, tm_sum(): x = x + lax.ppermute(x, 'tm', pairs)  6.05 us
    dot_general x5, matrix products, hi_dot(): jnp.dot(a, b, precision=lax.Precision.HIGHEST, preferred_element_type=jnp...  4.05 us
    all_to_all x1, waiting for transfers between devices, body(): lax.all_to_all(payload.reshape(n_chan, 1, -1), 'chan', 0, 0, tiled=True)  2.94 us
    unnamed x11, local copies, waits for them, and re-layouts  2.58 us
  transfers between devices with their start and end apart: 3, of which 3 were waited for; matrix products, arithmetic and copies ran while one was open for 14% of the time, Pallas kernels for 0%

profile of v4, /device:TPU:6, one launch (start us, length us, event | category | flops | bytes accessed | tf_op | source)
XLA Modules:
  0.0 93.2 jit_solution(3188474855497312605)
XLA Ops:
  0.0 0.9 subtract_convert_fusion
  0.9 0.2 convert_element_type.143
  1.1 1.0 %convert_bitcast_fusion = f32[1,8,128,128]{3,1,2,0:T(8,128)S(1)} fusion(bf16[1,8,16384]{2,1,0:T(8,128)(2,1)} %param.5), kind=kLoop, calls=%fused_computation.33 | loop fusion | flops 131072 | bytes 786432
  2.1 0.1 copy.120
  2.2 0.2 copy.76
  2.4 0.3 fusion.14
  2.7 0.1 copy.80
  3.0 0.2 convolution_bitcast_fusion
  3.3 0.1 reshape.313
  3.4 0.1 copy.81
  3.5 0.1 copy.82
  3.7 0.1 concatenate.6
  3.8 0.5 broadcast.321
  4.3 0.8 reduce
  5.1 1.1 %reshape.328 = bf16[128,2,576]{2,1,0:T(2,128)(2,1)} reshape(bf16[128,1152]{1,0:T(8,128)(2,1)S(1)} %reduce) | data formatting | bytes 589824
  6.1 18.0 %all-to-all-start = ((bf16[128,2,576]{2,1,0:T(2,128)(2,1)}), bf16[128,2,576]{2,1,0:T(2,128)(2,1)S(1)}, u32[]{:S(2)}, u32[]{:S(2)}) async-start(bf16[128,2,576]{2,1,0:T(2,128)(2,1)} %reshape.328), calls=%async_computation | async-start | bytes 655360 | tf_op jit(solution)/shard_map/all_to_all | solution.py:75
  24.1 2.1 %fusion.31 = (f32[1024,128]{1,0:T(8,128)S(1)}, f32[1024,128]{1,0:T(8,128)S(1)}) fusion(), kind=kLoop, calls=%fused_computation.42 | loop fusion | flops 1835008 | bytes 1048576 | tf_op jit(solution)/shard_map/sin | solution.py:22
  26.2 0.2 fusion.56
  26.6 0.1 broadcast_multiply_fusion
  26.8 1.0 %copy.75 = f32[1024,8]{1,0:T(8,128)} copy(f32[1024,8]{0,1:T(8,128)S(1)} %get-tuple-element.12) | data formatting | bytes 65536 | tf_op jit(solution)/shard_map/sin | solution.py:21
  27.8 1.0 %copy.74 = f32[1024,8]{1,0:T(8,128)} copy(f32[1024,8]{0,1:T(8,128)S(1)} %get-tuple-element.11) | data formatting | bytes 65536 | tf_op jit(solution)/shard_map/cos | solution.py:21
  28.8 0.1 mul.436
  28.9 0.5 mul.437
  29.4 0.1 mul.439
  29.5 0.1 mul.446
  29.7 0.8 mul.454
  30.5 6.5 %multiply_convert_fusion.1 = (bf16[1024,8,128]{2,1,0:T(8,128)(2,1)}, bf16[1024,8,128]{2,1,0:T(8,128)(2,1)S(1)}) fusion(f32[1024,128]{1,0:T(8,128)S(1)} %get-tuple-element.13, f32[1024,8]{1,0:T(8,128)} %copy.75, f32[1024,128]{1,0:T(8,128)S(1)} %get-tuple-element.14, f32[1024,8]{1,0:T(8,128)} %copy.74), kind=kLoop, calls=%fused_computation.1 | loop fusion | flops 10485760 | bytes 5308416 | tf_op jit(solution)/shard_map/convert_element_type | solution.py:24
  37.0 2.9 %all-to-all-done = bf16[128,2,576]{2,1,0:T(2,128)(2,1)S(1)} async-done(((bf16[128,2,576]{2,1,0:T(2,128)(2,1)}), bf16[128,2,576]{2,1,0:T(2,128)(2,1)S(1)}, u32[]{:S(2)}, u32[]{:S(2)}) %all-to-all-start) | async-done | bytes 294944 | tf_op jit(solution)/shard_map/all_to_all | solution.py:75
  40.0 0.5 reshape.329
  40.5 0.7 copy.84
  41.2 0.1 copy.87
  41.3 0.1 reshape.319
  41.5 0.7 fusion.21
  42.1 0.9 copy-done
  43.1 0.7 fusion.18
  43.7 0.1 copy.85
  43.9 0.1 reshape.316
  44.0 2.3 %fusion.6 = f32[1024,128]{1,0:T(8,128)S(1)} fusion(bf16[1024,128]{1,0:T(8,128)(2,1)S(1)} %reshape.316, bf16[128,8,8,128]{3,2,1,0:T(8,128)(2,1)} %bitcast.84), kind=kOutput, calls=%fused_computation.8 | convolution fusion | flops 268435456 | bytes 2883584 | tf_op jit(solution)/shard_map/dot_general | solution.py:81
  46.3 0.7 fusion.2
  47.0 0.1 reshape.321
  47.1 0.1 reshape.320
  47.2 0.8 fusion.40
  48.0 0.8 fusion.36
  48.7 0.8 fusion.17
  49.5 0.8 fusion.16
  50.3 1.0 %fusion.68 = f32[1024,64]{1,0:T(8,128)S(1)} fusion(f32[1024,64]{0,1:T(8,128)S(1)} %fusion.16, f32[64,64]{1,0:T(8,128)S(1)} %copy-done.1), kind=kOutput, calls=%fused_computation.102 | convolution fusion | flops 50331648 | bytes 540672 | tf_op jit(solution)/shard_map/dot_general | solution.py:30
  51.3 0.1 reshape.317
  51.4 0.1 maximum_bitcast_fusion
  51.5 0.3 copy.88
  51.9 26.4 %all_to_all.17 = f32[128,1,528]{2,1,0:T(1,128)S(1)} all-to-all(f32[128,1,528]{2,1,0:T(1,128)S(1)} %copy.88), channel_id=1, replica_groups=mesh['chan'=128,'tm'=4] {'chan'}, dimensions={0} | all-to-all | bytes 540672 | tf_op jit(solution)/shard_map/all_to_all | solution.py:107
  78.3 0.2 copy.89
  78.5 0.1 slice_reduce_fusion
  78.6 0.1 copy.90
  78.7 0.1 reshape.322
  78.9 0.1 fusion.46
  79.0 0.1 reshape.323
  79.1 0.2 copy.91
  79.3 2.7 %collective-permute-start = (f32[16,4,8]{2,1,0:T(4,128)S(1)}, f32[16,4,8]{2,1,0:T(4,128)S(1)}, u32[]{:S(2)}, u32[]{:S(2)}) collective-permute-start(f32[16,4,8]{2,1,0:T(4,128)S(1)} %bitcast_subtract_fusion), channel_id=1, source_target_pairs={{0,1},{1,0},{2,3},{3,2},{4,5},{5,4},{6,7},{7,6},{8,9},{9,8},{10,11... | collective-permute-start | bytes 6152 | tf_op jit(solution)/shard_map/ppermute | solution.py:39
  82.0 0.1 convert_reduce_fusion
  82.1 2.9 %collective-permute-done = f32[16,4,8]{2,1,0:T(4,128)S(1)} collective-permute-done((f32[16,4,8]{2,1,0:T(4,128)S(1)}, f32[16,4,8]{2,1,0:T(4,128)S(1)}, u32[]{:S(2)}, u32[]{:S(2)}) %collective-permute-start) | collective-permute-done | bytes 2080 | tf_op jit(solution)/shard_map/ppermute | solution.py:39
  85.1 3.3 %collective-permute-start.1 = (f32[16,4,8]{2,1,0:T(4,128)S(1)}, f32[16,4,8]{2,1,0:T(4,128)S(1)}, u32[]{:S(2)}, u32[]{:S(2)}) collective-permute-start(f32[16,4,8]{2,1,0:T(4,128)S(1)} %add.100), channel_id=1, source_target_pairs={{0,2},{1,3},{2,0},{3,1},{4,6},{5,7},{6,4},{7,5},{8,10},{9,11},{10,... | collective-permute-start | bytes 6152 | tf_op jit(solution)/shard_map/ppermute | solution.py:39
  88.4 4.0 %collective-permute-done.1 = f32[16,4,8]{2,1,0:T(4,128)S(1)} collective-permute-done((f32[16,4,8]{2,1,0:T(4,128)S(1)}, f32[16,4,8]{2,1,0:T(4,128)S(1)}, u32[]{:S(2)}, u32[]{:S(2)}) %collective-permute-start.1) | collective-permute-done | bytes 2080 | tf_op jit(solution)/shard_map/ppermute | solution.py:39
  92.4 0.1 divide_bitcast_fusion
  92.5 0.7 copy.92
  (26 shorter events, 0.5 us)
Async XLA Ops:
  0.0 2.4 %copy-start.3 = (f32[8]{0:T(128)S(1)}, f32[8]{0:T(128)}, u32[]{:S(2)}) copy-start(f32[8]{0:T(128)} %param.7) | copy-start | bytes 100
  1.1 1.8 %copy-start.2 = (s32[2048]{0:T(1024)S(1)}, s32[2048]{0:T(1024)}, u32[]{:S(2)}) copy-start(s32[2048]{0:T(1024)} %param.8) | copy-start | bytes 24580
  6.1 33.8 %all-to-all-start = ((bf16[128,2,576]{2,1,0:T(2,128)(2,1)}), bf16[128,2,576]{2,1,0:T(2,128)(2,1)S(1)}, u32[]{:S(2)}, u32[]{:S(2)}) async-start(bf16[128,2,576]{2,1,0:T(2,128)(2,1)} %reshape.328), calls=%async_computation | async-start | bytes 655360 | tf_op jit(solution)/shard_map/all_to_all | solution.py:75
  41.5 1.6 %copy-start = (bf16[1024,8,128]{2,1,0:T(8,128)(2,1)S(1)}, bf16[1024,8,128]{2,1,0:T(8,128)(2,1)}, u32[]{:S(2)}) copy-start(bf16[1024,8,128]{2,1,0:T(8,128)(2,1)} %get-tuple-element.5) | copy-start | bytes 6291460
  47.2 3.1 %copy-start.1 = (f32[64,64]{1,0:T(8,128)S(1)}, f32[64,64]{1,0:T(8,128)}, u32[]{:S(2)}) copy-start(f32[64,64]{1,0:T(8,128)} %mul.454) | copy-start | bytes 49156
  79.3 5.8 %collective-permute-start = (f32[16,4,8]{2,1,0:T(4,128)S(1)}, f32[16,4,8]{2,1,0:T(4,128)S(1)}, u32[]{:S(2)}, u32[]{:S(2)}) collective-permute-start(f32[16,4,8]{2,1,0:T(4,128)S(1)} %bitcast_subtract_fusion), channel_id=1, source_target_pairs={{0,1},{1,0},{2,3},{3,2},{4,5},{5,4},{6,7},{7,6},{8,9},{9,8},{10,11... | collective-permute-start | bytes 6152 | tf_op jit(solution)/shard_map/ppermute | solution.py:39
  85.1 7.3 %collective-permute-start.1 = (f32[16,4,8]{2,1,0:T(4,128)S(1)}, f32[16,4,8]{2,1,0:T(4,128)S(1)}, u32[]{:S(2)}, u32[]{:S(2)}) collective-permute-start(f32[16,4,8]{2,1,0:T(4,128)S(1)} %add.100), channel_id=1, source_target_pairs={{0,2},{1,3},{2,0},{3,1},{4,6},{5,7},{6,4},{7,5},{8,10},{9,11},{10,... | collective-permute-start | bytes 6152 | tf_op jit(solution)/shard_map/ppermute | solution.py:39

commit v5 on v4

--- a/solution.py
+++ b/solution.py
@@ -77,6 +77,10 @@
     col_parts = got[:, block:block + 2 * local_chans].reshape(n_chan, 2, local_chans)
     col_parts = col_parts.transpose(0, 2, 1).reshape(channels, 2)
 
+    cols = jnp.arange(shard_cols, dtype=jnp.int32)
+    target = (cols % 2) * (shard_cols // 2) + cols // 2
+    permute = (target[:, None] == cols[None, :]).astype(jnp.bfloat16)
+    turned = jnp.dot(turned, permute, preferred_element_type=jnp.float32).astype(jnp.bfloat16)
     cos_tab, sin_tab = tables(channels, 128)
     cos_part = jnp.dot(cos_tab, turned, preferred_element_type=jnp.float32)
     sin_part = jnp.dot(sin_tab, turned, preferred_element_type=jnp.float32)
@@ -87,15 +91,10 @@
     shard_groups = lax.dynamic_slice_in_dim(group_ids, me * shard_bl, shard_bl)
     member = (shard_groups[:, None] == jnp.arange(G, dtype=jnp.int32)[None, :]).astype(jnp.float32)
     eye_s = jnp.eye(4, dtype=jnp.float32)
-    eye_b = jnp.eye(shard_bl, dtype=jnp.float32)
-    r_one = jnp.array([0.0, 1.0], jnp.float32)
-    r_zero = 1.0 - r_one
-    p_bs = eye_b[:, None, None, :, None] * eye_s[None, :, None, None, :]
-    p0 = (p_bs * r_zero[None, None, :, None, None]).reshape(shard_cols, shard_bl * 4)
-    p1 = (p_bs * r_one[None, None, :, None, None]).reshape(shard_cols, shard_bl * 4)
     m_pow = (member[:, None, :, None] * eye_s[None, :, None, :]).reshape(shard_bl * 4, G * 4)
-    real_part = hi_dot(cos_part, p0) + hi_dot(sin_part, p1)
-    imag_part = hi_dot(cos_part, p1) - hi_dot(sin_part, p0)
+    half = shard_cols // 2
+    real_part = cos_part[:, :half] + sin_part[:, half:]
+    imag_part = cos_part[:, half:] - sin_part[:, :half]
     auto = hi_dot(real_part * real_part + imag_part * imag_part, m_pow)
 
     own_d = channels // n_chan

time: 93.9 us -> 92.5 us (0.985)
  local copies, waits for them, and re-layouts: 11.3 us -> 8.96 us
  waiting for transfers between devices: 9.85 us -> 11.5 us
  blocking collectives: 26.4 us -> 25.1 us
    dot_general x5 -> x1, matrix products: 4.05 us -> 2.03 us  [hi_dot(): jnp.dot(a, b, precision=lax.Precision.HIGHEST, preferred_element_type=jnp...]
    dot_general x1, matrix products: 0.71 us -> 2.42 us  [body(): sin_part = jnp.dot(sin_tab, turned, preferred_element_type=jnp.float32)]
    all_to_all x1, waiting for transfers between devices: 2.94 us -> 4.64 us  [body(): lax.all_to_all(payload.reshape(n_chan, 1, -1), 'chan', 0, 0, tiled=True)]
    dot_general x1, matrix products: 0.66 us -> 2.25 us  [body(): jnp.dot(sin_tab, col_parts, preferred_element_type=jnp.float32)]
    all_to_all x1, blocking collectives: 26.4 us -> 25.1 us  [body(): got = lax.all_to_all(payload, 'chan', 0, 0, tiled=True)]
    unnamed x11 -> x7, local copies, waits for them, and re-layouts: 2.58 us -> 1.66 us
  transfers between devices with their start and end apart: 3 -> 3, of which waited for: 3 -> 3; matrix products, arithmetic and copies ran while one was open for 14% -> 12% of each run, Pallas kernels for 0% -> 0%
where the time goes in v5:
time: 92.5 us; the launch traced here: 91.8 us
  blocking collectives  25.1 us (27%)
  starting transfers between devices  23.9 us (26%)
  other arithmetic  12.2 us (13%)
  waiting for transfers between devices  11.5 us (12%)
  matrix products  9.77 us (11%)
  local copies, waits for them, and re-layouts  8.96 us (10%)
    all_to_all x1, blocking collectives, body(): got = lax.all_to_all(payload, 'chan', 0, 0, tiled=True)  25.1 us
    all_to_all x1, starting transfers between devices, body(): lax.all_to_all(payload.reshape(n_chan, 1, -1), 'chan', 0, 0, tiled=True)  17.8 us
    ppermute x2, waiting for transfers between devices, tm_sum(): x = x + lax.ppermute(x, 'tm', pairs)  6.91 us
    convert_element_type x1, other arithmetic, tables(): ((ca * cb - sa * sb) * scale).astype(jnp.bfloat16).reshape(length, length)  6.51 us
    ppermute x2, starting transfers between devices, tm_sum(): x = x + lax.ppermute(x, 'tm', pairs)  6.05 us
    all_to_all x1, waiting for transfers between devices, body(): lax.all_to_all(payload.reshape(n_chan, 1, -1), 'chan', 0, 0, tiled=True)  4.64 us
    dot_general x1, matrix products, body(): sin_part = jnp.dot(sin_tab, turned, preferred_element_type=jnp.float32)  2.42 us
    dot_general x1, matrix products, body(): jnp.dot(sin_tab, col_parts, preferred_element_type=jnp.float32)  2.25 us
  transfers between devices with their start and end apart: 3, of which 3 were waited for; matrix products, arithmetic and copies ran while one was open for 12% of the time, Pallas kernels for 0%

profile of v5, /device:TPU:6, one launch (start us, length us, event | category | flops | bytes accessed | tf_op | source)
XLA Modules:
  0.0 91.8 jit_solution(9380671548536846317)
XLA Ops:
  0.0 0.9 subtract_convert_fusion
  0.9 0.2 convert_element_type.124
  1.1 0.0 copy-start
  1.1 1.0 %convert_bitcast_fusion = f32[1,8,128,128]{3,1,2,0:T(8,128)S(1)} fusion(bf16[1,8,16384]{2,1,0:T(8,128)(2,1)} %param.4), kind=kLoop, calls=%fused_computation.29 | loop fusion | flops 131072 | bytes 786432
  2.1 0.1 copy.119
  2.2 0.2 copy.75
  2.4 0.0 copy-done.1
  2.4 0.3 fusion.14
  2.7 0.1 copy.79
  2.8 0.0 copy-done
  2.9 0.1 eq.88
  2.9 0.1 copy.77
  3.0 0.2 convolution_bitcast_fusion
  3.2 0.1 copy.78
  3.3 0.1 reshape.309
  3.4 0.1 copy.80
  3.5 0.1 copy.81
  3.7 0.1 concatenate.6
  3.8 0.5 broadcast.346
  4.3 0.8 reduce
  5.1 1.1 %reshape.324 = bf16[128,2,576]{2,1,0:T(2,128)(2,1)} reshape(bf16[128,1152]{1,0:T(8,128)(2,1)S(1)} %reduce) | data formatting | bytes 589824
  6.1 17.8 %all-to-all-start = ((bf16[128,2,576]{2,1,0:T(2,128)(2,1)}), bf16[128,2,576]{2,1,0:T(2,128)(2,1)S(1)}, u32[]{:S(2)}, u32[]{:S(2)}) async-start(bf16[128,2,576]{2,1,0:T(2,128)(2,1)} %reshape.324), calls=%async_computation | async-start | bytes 655360 | tf_op jit(solution)/shard_map/all_to_all | solution.py:75
  24.0 2.1 %fusion.36 = (f32[1024,128]{1,0:T(8,128)S(1)}, f32[1024,128]{1,0:T(8,128)S(1)}) fusion(), kind=kLoop, calls=%fused_computation.45 | loop fusion | flops 1835008 | bytes 1048576 | tf_op jit(solution)/shard_map/sin | solution.py:22
  26.1 0.2 fusion.52
  26.3 0.1 dynamic_slice.3
  26.4 0.1 fusion.55
  26.4 0.1 broadcast_multiply_fusion
  26.5 1.0 %copy.74 = f32[1024,8]{1,0:T(8,128)} copy(f32[1024,8]{0,1:T(8,128)S(1)} %get-tuple-element.10) | data formatting | bytes 65536 | tf_op jit(solution)/shard_map/sin | solution.py:21
  27.6 1.0 %copy.73 = f32[1024,8]{1,0:T(8,128)} copy(f32[1024,8]{0,1:T(8,128)S(1)} %get-tuple-element.9) | data formatting | bytes 65536 | tf_op jit(solution)/shard_map/cos | solution.py:21
  28.6 0.2 mul.372
  28.8 6.5 %multiply_convert_fusion.1 = (bf16[1024,8,128]{2,1,0:T(8,128)(2,1)S(1)}, bf16[1024,8,128]{2,1,0:T(8,128)(2,1)}) fusion(f32[1024,128]{1,0:T(8,128)S(1)} %get-tuple-element.11, f32[1024,8]{1,0:T(8,128)} %copy.74, f32[1024,128]{1,0:T(8,128)S(1)} %get-tuple-element.12, f32[1024,8]{1,0:T(8,128)} %copy.73), kind=kLoop, calls=%fused_computation.1 | loop fusion | flops 10485760 | bytes 5308416 | tf_op jit(solution)/shard_map/convert_element_type | solution.py:24
  35.3 4.6 %all-to-all-done = bf16[128,2,576]{2,1,0:T(2,128)(2,1)S(1)} async-done(((bf16[128,2,576]{2,1,0:T(2,128)(2,1)}), bf16[128,2,576]{2,1,0:T(2,128)(2,1)S(1)}, u32[]{:S(2)}, u32[]{:S(2)}) %all-to-all-start) | async-done | bytes 294944 | tf_op jit(solution)/shard_map/all_to_all | solution.py:75
  40.0 0.5 reshape.325
  40.5 0.7 copy.83
  41.2 0.1 copy.86
  41.3 0.1 reshape.315
  41.5 2.3 %fusion.18 = f32[1024]{0:T(1024)S(1)} fusion(bf16[1024,2]{0,1:T(2,128)(2,1)S(1)} %reshape.315, bf16[128,8,8,128]{3,2,1,0:T(8,128)(2,1)} %bitcast.78), kind=kOutput, calls=%fused_computation.21 | convolution fusion | flops 4195328 | bytes 2105344 | tf_op jit(solution)/shard_map/dot_general | solution.py:88
  43.7 0.7 fusion.15
  44.4 0.1 copy.84
  44.5 0.1 reshape.312
  44.7 0.3 convolution_convert_fusion
  45.0 2.4 %fusion.2 = f32[1024,128]{0,1:T(8,128)S(1)} fusion(bf16[1024,128]{1,0:T(8,128)(2,1)S(1)} %convolution_convert_fusion, bf16[128,8,8,128]{3,2,1,0:T(8,128)(2,1)} %bitcast.79), kind=kOutput, calls=%fused_computation.4 | convolution fusion | flops 268435456 | bytes 2883584 | tf_op jit(solution)/shard_map/dot_general | solution.py:86
  47.4 1.6 %fusion.6 = f32[1024,128]{0,1:T(8,128)} fusion(bf16[1024,128]{1,0:T(8,128)(2,1)S(1)} %convolution_convert_fusion, bf16[128,8,8,128]{3,2,1,0:T(8,128)(2,1)S(1)} %bitcast.77), kind=kOutput, calls=%fused_computation.8 | convolution fusion | flops 268435456 | bytes 2883584 | tf_op jit(solution)/shard_map/dot_general | solution.py:85
  49.0 0.1 reshape.317
  49.1 0.1 reshape.316
  49.2 2.0 %fusion.29 = f32[1024,64]{1,0:T(8,128)S(1)} fusion(f32[64,64]{1,0:T(8,128)S(1)} %mul.372, f32[1024,128]{0,1:T(8,128)S(1)} %fusion.2, f32[1024,128]{0,1:T(8,128)} %fusion.6), kind=kOutput, calls=%fused_computation.38 | convolution fusion | flops 50659328 | bytes 1327104 | tf_op jit(solution)/shard_map/dot_general | solution.py:30
  51.2 0.1 reshape.313
  51.4 0.1 maximum_bitcast_fusion
  51.5 0.3 copy.87
  51.8 25.1 %all_to_all.17 = f32[128,1,528]{2,1,0:T(1,128)S(1)} all-to-all(f32[128,1,528]{2,1,0:T(1,128)S(1)} %copy.87), channel_id=1, replica_groups=mesh['chan'=128,'tm'=4] {'chan'}, dimensions={0} | all-to-all | bytes 540672 | tf_op jit(solution)/shard_map/all_to_all | solution.py:106
  76.9 0.2 copy.88
  77.1 0.1 slice_reduce_fusion
  77.2 0.1 copy.89
  77.3 0.1 reshape.318
  77.4 0.1 fusion.45
  77.5 0.1 reshape.319
  77.6 0.2 copy.90
  77.8 2.7 %collective-permute-start = (f32[16,4,8]{2,1,0:T(4,128)S(1)}, f32[16,4,8]{2,1,0:T(4,128)S(1)}, u32[]{:S(2)}, u32[]{:S(2)}) collective-permute-start(f32[16,4,8]{2,1,0:T(4,128)S(1)} %bitcast_subtract_fusion), channel_id=1, source_target_pairs={{0,1},{1,0},{2,3},{3,2},{4,5},{5,4},{6,7},{7,6},{8,9},{9,8},{10,11... | collective-permute-start | bytes 6152 | tf_op jit(solution)/shard_map/ppermute | solution.py:39
  80.6 0.1 convert_reduce_fusion
  80.7 2.9 %collective-permute-done = f32[16,4,8]{2,1,0:T(4,128)S(1)} collective-permute-done((f32[16,4,8]{2,1,0:T(4,128)S(1)}, f32[16,4,8]{2,1,0:T(4,128)S(1)}, u32[]{:S(2)}, u32[]{:S(2)}) %collective-permute-start) | collective-permute-done | bytes 2080 | tf_op jit(solution)/shard_map/ppermute | solution.py:39
  83.7 3.3 %collective-permute-start.1 = (f32[16,4,8]{2,1,0:T(4,128)S(1)}, f32[16,4,8]{2,1,0:T(4,128)S(1)}, u32[]{:S(2)}, u32[]{:S(2)}) collective-permute-start(f32[16,4,8]{2,1,0:T(4,128)S(1)} %add.121), channel_id=1, source_target_pairs={{0,2},{1,3},{2,0},{3,1},{4,6},{5,7},{6,4},{7,5},{8,10},{9,11},{10,... | collective-permute-start | bytes 6152 | tf_op jit(solution)/shard_map/ppermute | solution.py:39
  87.0 4.0 %collective-permute-done.1 = f32[16,4,8]{2,1,0:T(4,128)S(1)} collective-permute-done((f32[16,4,8]{2,1,0:T(4,128)S(1)}, f32[16,4,8]{2,1,0:T(4,128)S(1)}, u32[]{:S(2)}, u32[]{:S(2)}) %collective-permute-start.1) | collective-permute-done | bytes 2080 | tf_op jit(solution)/shard_map/ppermute | solution.py:39
  91.0 0.1 divide_bitcast_fusion
  91.1 0.7 copy.91
  (13 shorter events, 0.1 us)
Async XLA Ops:
  0.0 2.4 %copy-start.1 = (f32[8]{0:T(128)S(1)}, f32[8]{0:T(128)}, u32[]{:S(2)}) copy-start(f32[8]{0:T(128)} %param.6) | copy-start | bytes 100
  1.1 1.8 %copy-start = (s32[2048]{0:T(1024)S(1)}, s32[2048]{0:T(1024)}, u32[]{:S(2)}) copy-start(s32[2048]{0:T(1024)} %param.7) | copy-start | bytes 24580
  6.1 33.8 %all-to-all-start = ((bf16[128,2,576]{2,1,0:T(2,128)(2,1)}), bf16[128,2,576]{2,1,0:T(2,128)(2,1)S(1)}, u32[]{:S(2)}, u32[]{:S(2)}) async-start(bf16[128,2,576]{2,1,0:T(2,128)(2,1)} %reshape.324), calls=%async_computation | async-start | bytes 655360 | tf_op jit(solution)/shard_map/all_to_all | solution.py:75
  77.8 5.8 %collective-permute-start = (f32[16,4,8]{2,1,0:T(4,128)S(1)}, f32[16,4,8]{2,1,0:T(4,128)S(1)}, u32[]{:S(2)}, u32[]{:S(2)}) collective-permute-start(f32[16,4,8]{2,1,0:T(4,128)S(1)} %bitcast_subtract_fusion), channel_id=1, source_target_pairs={{0,1},{1,0},{2,3},{3,2},{4,5},{5,4},{6,7},{7,6},{8,9},{9,8},{10,11... | collective-permute-start | bytes 6152 | tf_op jit(solution)/shard_map/ppermute | solution.py:39
  83.7 7.3 %collective-permute-start.1 = (f32[16,4,8]{2,1,0:T(4,128)S(1)}, f32[16,4,8]{2,1,0:T(4,128)S(1)}, u32[]{:S(2)}, u32[]{:S(2)}) collective-permute-start(f32[16,4,8]{2,1,0:T(4,128)S(1)} %add.121), channel_id=1, source_target_pairs={{0,2},{1,3},{2,0},{3,1},{4,6},{5,7},{6,4},{7,5},{8,10},{9,11},{10,... | collective-permute-start | bytes 6152 | tf_op jit(solution)/shard_map/ppermute | solution.py:39

commit v6 on v5

--- a/solution.py
+++ b/solution.py
@@ -26,19 +26,25 @@
     return cos_tab, sin_tab
 
 
-def hi_dot(a, b):
-    return jnp.dot(a, b, precision=lax.Precision.HIGHEST, preferred_element_type=jnp.float32)
+def tm_sum(x, n):
+    me = lax.axis_index("tm")
+    got = [x] + [lax.ppermute(x, "tm", [(i, (i + k) % n) for i in range(n)]) for k in range(1, n)]
+    got = jnp.stack(got)
+    ordered = jnp.take(got, (me - jnp.arange(n)) % n, axis=0)
+    while ordered.shape[0] > 1:
+        if ordered.shape[0] % 2:
+            ordered = jnp.concatenate([ordered[:1] + ordered[1:2], ordered[2:]])
+        else:
+            ordered = ordered[0::2] + ordered[1::2]
+    return ordered[0]
 
 
-def tm_sum(x, n):
-    if n & (n - 1):
-        return lax.psum(x, "tm")
-    step = 1
-    while step < n:
-        pairs = [(i, i ^ step) for i in range(n)]
-        x = x + lax.ppermute(x, "tm", pairs)
-        step *= 2
-    return x
+def split_dot(a, b):
+    hi = lax.reduce_precision(a, exponent_bits=8, mantissa_bits=7)
+    lo = a - hi
+    b16 = b.astype(jnp.bfloat16)
+    return (jnp.dot(hi.astype(jnp.bfloat16), b16, preferred_element_type=jnp.float32)
+            + jnp.dot(lo.astype(jnp.bfloat16), b16, preferred_element_type=jnp.float32))
 
 
 def body(visibilities, flags, taper, group_ids):
@@ -95,7 +101,7 @@
     half = shard_cols // 2
     real_part = cos_part[:, :half] + sin_part[:, half:]
     imag_part = cos_part[:, half:] - sin_part[:, :half]
-    auto = hi_dot(real_part * real_part + imag_part * imag_part, m_pow)
+    auto = split_dot(real_part * real_part + imag_part * imag_part, m_pow)
 
     own_d = channels // n_chan
     payload = jnp.concatenate([

time: 92.5 us -> 91.9 us (level)
  the two profiles are of different devices: /device:TPU:6 before, /device:TPU:8 now
where the time goes in v6:
time: 91.9 us; the launch traced here: 91.1 us
  starting transfers between devices  36.6 us (40%)
  waiting for transfers between devices  24.5 us (27%)
  other arithmetic  12.8 us (14%)
  local copies, waits for them, and re-layouts  10.8 us (12%)
  matrix products  5.92 us (6%)
    all_to_all x1, starting transfers between devices, body(): lax.all_to_all(payload.reshape(n_chan, 1, -1), 'chan', 0, 0, tiled=True)  17.4 us
    all_to_all x1, waiting for transfers between devices, body(): got = lax.all_to_all(payload, 'chan', 0, 0, tiled=True)  15.8 us
    ppermute x3, starting transfers between devices, tm_sum(): lax.ppermute(x, 'tm', [(i, (i + k) % n) for i in range(n)])  10.2 us
    all_to_all x1, starting transfers between devices, body(): got = lax.all_to_all(payload, 'chan', 0, 0, tiled=True)  9.1 us
    convert_element_type x1, other arithmetic, tables(): ((ca * cb - sa * sb) * scale).astype(jnp.bfloat16).reshape(length, length)  6.51 us
    all_to_all x1, waiting for transfers between devices, body(): lax.all_to_all(payload.reshape(n_chan, 1, -1), 'chan', 0, 0, tiled=True)  4.64 us
    ppermute x3, waiting for transfers between devices, tm_sum(): lax.ppermute(x, 'tm', [(i, (i + k) % n) for i in range(n)])  4.01 us
    dot_general x1, matrix products, body(): jnp.dot(sin_tab, col_parts, preferred_element_type=jnp.float32)  2.4 us
  transfers between devices with their start and end apart: 5, of which 4 were waited for; matrix products, arithmetic and copies ran while one was open for 13% of the time, Pallas kernels for 0%

profile of v6, /device:TPU:8, one launch (start us, length us, event | category | flops | bytes accessed | tf_op | source)
XLA Modules:
  0.0 91.1 jit_solution(7522671026263779598)
XLA Ops:
  0.0 0.9 subtract_convert_fusion
  0.9 0.8 eq.90
  1.7 0.2 convert_element_type.136
  1.9 1.0 %convert_bitcast_fusion = f32[1,8,128,128]{3,1,2,0:T(8,128)S(1)} fusion(bf16[1,8,16384]{2,1,0:T(8,128)(2,1)} %param.4), kind=kLoop, calls=%fused_computation.31 | loop fusion | flops 131072 | bytes 786432
  2.9 0.1 copy.140
  3.0 0.2 copy.90
  3.3 0.3 fusion.14
  3.5 0.2 convolution_bitcast_fusion
  3.8 0.1 reshape.364
  3.9 0.1 copy.96
  4.1 0.1 copy.95
  4.2 0.1 copy.94
  4.4 0.1 concatenate.6
  4.5 0.5 broadcast.447
  5.0 0.8 reduce
  5.8 1.0 %reshape.387 = bf16[128,2,576]{2,1,0:T(2,128)(2,1)} reshape(bf16[128,1152]{1,0:T(8,128)(2,1)S(1)} %reduce) | data formatting | bytes 589824
  6.8 17.4 %all-to-all-start = ((bf16[128,2,576]{2,1,0:T(2,128)(2,1)}), bf16[128,2,576]{2,1,0:T(2,128)(2,1)S(1)}, u32[]{:S(2)}, u32[]{:S(2)}) async-start(bf16[128,2,576]{2,1,0:T(2,128)(2,1)} %reshape.387), calls=%async_computation | async-start | bytes 655360 | tf_op jit(solution)/shard_map/all_to_all | solution.py:81
  24.2 2.1 %fusion.32 = (f32[1024,128]{1,0:T(8,128)S(1)}, f32[1024,128]{1,0:T(8,128)S(1)}) fusion(), kind=kLoop, calls=%fused_computation.47 | loop fusion | flops 1835008 | bytes 1048576 | tf_op jit(solution)/shard_map/sin | solution.py:22
  26.3 0.1 dynamic_slice.3
  26.4 0.2 fusion.50
  26.7 0.1 multiply_convert_fusion.2
  26.8 0.2 convert_element_type.147
  27.0 1.0 %copy.88 = f32[1024,8]{1,0:T(8,128)} copy(f32[1024,8]{0,1:T(8,128)S(1)} %get-tuple-element.13) | data formatting | bytes 65536 | tf_op jit(solution)/shard_map/cos | solution.py:21
  28.1 1.0 %copy.89 = f32[1024,8]{1,0:T(8,128)} copy(f32[1024,8]{0,1:T(8,128)S(1)} %get-tuple-element.14) | data formatting | bytes 65536 | tf_op jit(solution)/shard_map/sin | solution.py:21
  29.1 6.5 %multiply_convert_fusion.1 = (bf16[1024,8,128]{2,1,0:T(8,128)(2,1)S(1)}, bf16[1024,8,128]{2,1,0:T(8,128)(2,1)}) fusion(f32[1024,128]{1,0:T(8,128)S(1)} %get-tuple-element.15, f32[1024,8]{1,0:T(8,128)} %copy.89, f32[1024,128]{1,0:T(8,128)S(1)} %get-tuple-element.16, f32[1024,8]{1,0:T(8,128)} %copy.88), kind=kLoop, calls=%fused_computation.2 | loop fusion | flops 10485760 | bytes 5308416 | tf_op jit(solution)/shard_map/convert_element_type | solution.py:24
  35.6 4.6 %all-to-all-done = bf16[128,2,576]{2,1,0:T(2,128)(2,1)S(1)} async-done(((bf16[128,2,576]{2,1,0:T(2,128)(2,1)}), bf16[128,2,576]{2,1,0:T(2,128)(2,1)S(1)}, u32[]{:S(2)}, u32[]{:S(2)}) %all-to-all-start) | async-done | bytes 294944 | tf_op jit(solution)/shard_map/all_to_all | solution.py:81
  40.2 0.5 reshape.388
  40.7 0.7 copy.98
  41.5 0.1 copy.99
  41.6 0.1 reshape.367
  41.7 0.1 copy.101
  41.9 0.1 reshape.370
  42.0 0.3 convolution_convert_fusion
  42.3 2.4 %fusion.18 = f32[1024]{0:T(1024)S(1)} fusion(bf16[1024,2]{0,1:T(2,128)(2,1)S(1)} %reshape.370, bf16[128,8,8,128]{3,2,1,0:T(8,128)(2,1)} %bitcast.92), kind=kOutput, calls=%fused_computation.23 | convolution fusion | flops 4195328 | bytes 2105344 | tf_op jit(solution)/shard_map/dot_general | solution.py:94
  44.7 0.8 fusion.2
  45.5 0.7 fusion.15
  46.2 0.8 fusion.6
  47.0 0.1 reshape.371
  47.1 0.1 reshape.372
  47.3 0.2 fusion.35
  47.5 0.2 convolution_add_fusion
  47.7 0.2 copy.100
  47.9 0.1 reshape.368
  48.1 0.1 maximum_bitcast_fusion
  48.2 1.0 %copy.102 = f32[128,1,528]{2,1,0:T(1,128)} copy(f32[128,1,528]{2,0,1:T(8,128)S(1)} %maximum_bitcast_fusion) | data formatting | bytes 540672 | tf_op jit(solution)/shard_map/all_to_all | solution.py:112
  49.2 9.1 %all-to-all-start.1 = ((f32[128,1,528]{2,1,0:T(1,128)}), f32[128,1,528]{2,1,0:T(1,128)S(1)}, u32[]{:S(2)}, u32[]{:S(2)}) async-start(f32[128,1,528]{2,1,0:T(1,128)} %copy.102), calls=%async_computation.1 | async-start | bytes 655360 | tf_op jit(solution)/shard_map/all_to_all | solution.py:112
  58.4 0.1 convert_reduce_fusion
  58.5 15.8 %all-to-all-done.1 = f32[128,1,528]{2,1,0:T(1,128)S(1)} async-done(((f32[128,1,528]{2,1,0:T(1,128)}), f32[128,1,528]{2,1,0:T(1,128)S(1)}, u32[]{:S(2)}, u32[]{:S(2)}) %all-to-all-start.1) | async-done | bytes 270368 | tf_op jit(solution)/shard_map/all_to_all | solution.py:112
  74.4 0.2 copy.103
  74.5 0.2 slice_reduce_fusion
  74.7 0.1 copy.104
  74.8 0.1 reshape.374
  74.9 0.1 copy.109
  75.0 0.1 reshape.373
  75.2 0.1 fusion.66
  75.3 0.1 copy.113
  75.5 0.1 copy.115
  75.6 4.7 %collective-permute-start.2 = (f32[16,4,8]{0,2,1:T(8,128)S(1)}, f32[16,4,8]{0,2,1:T(8,128)S(1)}, u32[]{:S(2)}, u32[]{:S(2)}) collective-permute-start(f32[16,4,8]{0,2,1:T(8,128)S(1)} %bitcast_subtract_fusion), channel_id=1, source_target_pairs={{0,3},{1,0},{2,1},{3,2},{4,7},{5,4},{6,5},{7,6},{8,11},{9,8},{10,9... | collective-permute-start | bytes 6152 | tf_op jit(solution)/shard_map/ppermute | solution.py:31
  80.3 2.7 %collective-permute-start.1 = (f32[16,4,8]{0,2,1:T(8,128)S(1)}, f32[16,4,8]{0,2,1:T(8,128)S(1)}, u32[]{:S(2)}, u32[]{:S(2)}) collective-permute-start(f32[16,4,8]{0,2,1:T(8,128)S(1)} %bitcast_subtract_fusion), channel_id=1, source_target_pairs={{0,2},{1,3},{2,0},{3,1},{4,6},{5,7},{6,4},{7,5},{8,10},{9,11},{10,... | collective-permute-start | bytes 6152 | tf_op jit(solution)/shard_map/ppermute | solution.py:31
  83.0 2.8 %collective-permute-start = (f32[16,4,8]{0,2,1:T(8,128)S(1)}, f32[16,4,8]{0,2,1:T(8,128)S(1)}, u32[]{:S(2)}, u32[]{:S(2)}) collective-permute-start(f32[16,4,8]{0,2,1:T(8,128)S(1)} %bitcast_subtract_fusion), channel_id=1, source_target_pairs={{0,1},{1,2},{2,3},{3,0},{4,5},{5,6},{6,7},{7,4},{8,9},{9,10},{10,1... | collective-permute-start | bytes 6152 | tf_op jit(solution)/shard_map/ppermute | solution.py:31
  85.8 1.6 %collective-permute-done.1 = f32[16,4,8]{0,2,1:T(8,128)S(1)} collective-permute-done((f32[16,4,8]{0,2,1:T(8,128)S(1)}, f32[16,4,8]{0,2,1:T(8,128)S(1)}, u32[]{:S(2)}, u32[]{:S(2)}) %collective-permute-start.1) | collective-permute-done | bytes 2080 | tf_op jit(solution)/shard_map/ppermute | solution.py:31
  87.4 2.4 %collective-permute-done = f32[16,4,8]{0,2,1:T(8,128)S(1)} collective-permute-done((f32[16,4,8]{0,2,1:T(8,128)S(1)}, f32[16,4,8]{0,2,1:T(8,128)S(1)}, u32[]{:S(2)}, u32[]{:S(2)}) %collective-permute-start) | collective-permute-done | bytes 2080 | tf_op jit(solution)/shard_map/ppermute | solution.py:31
  89.8 0.6 gather_fusion
  90.5 0.6 fusion.48
  (30 shorter events, 0.6 us)
Async XLA Ops:
  0.0 3.2 %copy-start.2 = (f32[8]{0:T(128)S(1)}, f32[8]{0:T(128)}, u32[]{:S(2)}) copy-start(f32[8]{0:T(128)} %param.6) | copy-start | bytes 100
  4.1 22.2 %copy-start.1 = (s32[2048]{0:T(1024)S(1)}, s32[2048]{0:T(1024)}, u32[]{:S(2)}) copy-start(s32[2048]{0:T(1024)} %param.7) | copy-start | bytes 24580
  6.8 33.4 %all-to-all-start = ((bf16[128,2,576]{2,1,0:T(2,128)(2,1)}), bf16[128,2,576]{2,1,0:T(2,128)(2,1)S(1)}, u32[]{:S(2)}, u32[]{:S(2)}) async-start(bf16[128,2,576]{2,1,0:T(2,128)(2,1)} %reshape.387), calls=%async_computation | async-start | bytes 655360 | tf_op jit(solution)/shard_map/all_to_all | solution.py:81
  42.0 2.7 %copy-start = (bf16[1024,8,128]{2,1,0:T(8,128)(2,1)S(1)}, bf16[1024,8,128]{2,1,0:T(8,128)(2,1)}, u32[]{:S(2)}) copy-start(bf16[1024,8,128]{2,1,0:T(8,128)(2,1)} %get-tuple-element.6) | copy-start | bytes 6291460
  49.2 25.1 %all-to-all-start.1 = ((f32[128,1,528]{2,1,0:T(1,128)}), f32[128,1,528]{2,1,0:T(1,128)S(1)}, u32[]{:S(2)}, u32[]{:S(2)}) async-start(f32[128,1,528]{2,1,0:T(1,128)} %copy.102), calls=%async_computation.1 | async-start | bytes 655360 | tf_op jit(solution)/shard_map/all_to_all | solution.py:112
  75.6 10.2 %collective-permute-start.2 = (f32[16,4,8]{0,2,1:T(8,128)S(1)}, f32[16,4,8]{0,2,1:T(8,128)S(1)}, u32[]{:S(2)}, u32[]{:S(2)}) collective-permute-start(f32[16,4,8]{0,2,1:T(8,128)S(1)} %bitcast_subtract_fusion), channel_id=1, source_target_pairs={{0,3},{1,0},{2,1},{3,2},{4,7},{5,4},{6,5},{7,6},{8,11},{9,8},{10,9... | collective-permute-start | bytes 6152 | tf_op jit(solution)/shard_map/ppermute | solution.py:31
  80.3 7.1 %collective-permute-start.1 = (f32[16,4,8]{0,2,1:T(8,128)S(1)}, f32[16,4,8]{0,2,1:T(8,128)S(1)}, u32[]{:S(2)}, u32[]{:S(2)}) collective-permute-start(f32[16,4,8]{0,2,1:T(8,128)S(1)} %bitcast_subtract_fusion), channel_id=1, source_target_pairs={{0,2},{1,3},{2,0},{3,1},{4,6},{5,7},{6,4},{7,5},{8,10},{9,11},{10,... | collective-permute-start | bytes 6152 | tf_op jit(solution)/shard_map/ppermute | solution.py:31
  83.0 6.8 %collective-permute-start = (f32[16,4,8]{0,2,1:T(8,128)S(1)}, f32[16,4,8]{0,2,1:T(8,128)S(1)}, u32[]{:S(2)}, u32[]{:S(2)}) collective-permute-start(f32[16,4,8]{0,2,1:T(8,128)S(1)} %bitcast_subtract_fusion), channel_id=1, source_target_pairs={{0,1},{1,2},{2,3},{3,0},{4,5},{5,6},{6,7},{7,4},{8,9},{9,10},{10,1... | collective-permute-start | bytes 6152 | tf_op jit(solution)/shard_map/ppermute | solution.py:31

commit v7 on v5

--- a/solution.py
+++ b/solution.py
@@ -26,10 +26,6 @@
     return cos_tab, sin_tab
 
 
-def hi_dot(a, b):
-    return jnp.dot(a, b, precision=lax.Precision.HIGHEST, preferred_element_type=jnp.float32)
-
-
 def tm_sum(x, n):
     if n & (n - 1):
         return lax.psum(x, "tm")
@@ -39,6 +35,14 @@
         x = x + lax.ppermute(x, "tm", pairs)
         step *= 2
     return x
+
+
+def split_dot(a, b):
+    hi = lax.reduce_precision(a, exponent_bits=8, mantissa_bits=7)
+    lo = a - hi
+    b16 = b.astype(jnp.bfloat16)
+    return (jnp.dot(hi.astype(jnp.bfloat16), b16, preferred_element_type=jnp.float32)
+            + jnp.dot(lo.astype(jnp.bfloat16), b16, preferred_element_type=jnp.float32))
 
 
 def body(visibilities, flags, taper, group_ids):
@@ -81,11 +85,14 @@
     target = (cols % 2) * (shard_cols // 2) + cols // 2
     permute = (target[:, None] == cols[None, :]).astype(jnp.bfloat16)
     turned = jnp.dot(turned, permute, preferred_element_type=jnp.float32).astype(jnp.bfloat16)
+    extra = 128 - col_parts.shape[1]
+    rhs = jnp.concatenate([turned, col_parts, jnp.zeros((channels, extra), jnp.bfloat16)], axis=1)
     cos_tab, sin_tab = tables(channels, 128)
-    cos_part = jnp.dot(cos_tab, turned, preferred_element_type=jnp.float32)
-    sin_part = jnp.dot(sin_tab, turned, preferred_element_type=jnp.float32)
-    col_cos = jnp.sum(jnp.dot(cos_tab, col_parts, preferred_element_type=jnp.float32), axis=1)
-    col_sin = jnp.sum(jnp.dot(sin_tab, col_parts, preferred_element_type=jnp.float32), axis=1)
+    cos_all = jnp.dot(cos_tab, rhs, preferred_element_type=jnp.float32)
+    sin_all = jnp.dot(sin_tab, rhs, preferred_element_type=jnp.float32)
+    cos_part, sin_part = cos_all[:, :shard_cols], sin_all[:, :shard_cols]
+    col_cos = cos_all[:, shard_cols] + cos_all[:, shard_cols + 1]
+    col_sin = sin_all[:, shard_cols] + sin_all[:, shard_cols + 1]
 
     me = lax.axis_index("chan")
     shard_groups = lax.dynamic_slice_in_dim(group_ids, me * shard_bl, shard_bl)
@@ -95,7 +102,7 @@
     half = shard_cols // 2
     real_part = cos_part[:, :half] + sin_part[:, half:]
     imag_part = cos_part[:, half:] - sin_part[:, :half]
-    auto = hi_dot(real_part * real_part + imag_part * imag_part, m_pow)
+    auto = split_dot(real_part * real_part + imag_part * imag_part, m_pow)
 
     own_d = channels // n_chan
     payload = jnp.concatenate([

time: 92.5 us -> 89.1 us (0.963)
  matrix products: 9.77 us -> 4.37 us
  waiting for transfers between devices: 11.5 us -> 9.52 us
  other arithmetic: 12.2 us -> 14.1 us
  blocking collectives: 25.1 us -> 26.8 us
    dot_general x5 -> x4, matrix products: 8.99 us -> 3.54 us  [the longest x1 2.34 us: body(): sin_all = jnp.dot(sin_tab, rhs, preferred_element_type=jnp.float32)]
    all_to_all x1, waiting for transfers between devices: 4.64 us -> 2.6 us  [body(): lax.all_to_all(payload.reshape(n_chan, 1, -1), 'chan', 0, 0, tiled=True)]
    cos x0 -> x1, other arithmetic: none -> 1.91 us  [tables(): cb, sb = (jnp.cos(pb)[:, None, :], jnp.sin(pb)[:, None, :])]
    all_to_all x1, blocking collectives: 25.1 us -> 26.8 us  [body(): got = lax.all_to_all(payload, 'chan', 0, 0, tiled=True)]
  transfers between devices with their start and end apart: 3 -> 3, of which waited for: 3 -> 3; matrix products, arithmetic and copies ran while one was open for 12% -> 15% of each run, Pallas kernels for 0% -> 0%
where the time goes in v7:
time: 89.1 us; the launch traced here: 88.4 us
  blocking collectives  26.8 us (30%)
  starting transfers between devices  24 us (27%)
  other arithmetic  14.1 us (16%)
  waiting for transfers between devices  9.52 us (11%)
  local copies, waits for them, and re-layouts  9.23 us (10%)
  matrix products  4.37 us (5%)
    all_to_all x1, blocking collectives, body(): got = lax.all_to_all(payload, 'chan', 0, 0, tiled=True)  26.8 us
    all_to_all x1, starting transfers between devices, body(): lax.all_to_all(payload.reshape(n_chan, 1, -1), 'chan', 0, 0, tiled=True)  18 us
    ppermute x2, waiting for transfers between devices, tm_sum(): x = x + lax.ppermute(x, 'tm', pairs)  6.92 us
    convert_element_type x1, other arithmetic, tables(): ((ca * cb - sa * sb) * scale).astype(jnp.bfloat16).reshape(length, length)  6.51 us
    ppermute x2, starting transfers between devices, tm_sum(): x = x + lax.ppermute(x, 'tm', pairs)  6.04 us
    all_to_all x1, waiting for transfers between devices, body(): lax.all_to_all(payload.reshape(n_chan, 1, -1), 'chan', 0, 0, tiled=True)  2.6 us
    dot_general x1, matrix products, body(): sin_all = jnp.dot(sin_tab, rhs, preferred_element_type=jnp.float32)  2.34 us
    sin x1, other arithmetic, tables(): cb, sb = (jnp.cos(pb)[:, None, :], jnp.sin(pb)[:, None, :])  1.93 us
  transfers between devices with their start and end apart: 3, of which 3 were waited for; matrix products, arithmetic and copies ran while one was open for 15% of the time, Pallas kernels for 0%

profile of v7, /device:TPU:6, one launch (start us, length us, event | category | flops | bytes accessed | tf_op | source)
XLA Modules:
  0.0 88.4 jit_solution(6190432030994468858)
XLA Ops:
  0.0 0.9 subtract_convert_fusion
  0.9 0.2 convert_element_type.106
  1.1 1.0 %convert_bitcast_fusion = f32[1,8,128,128]{3,1,2,0:T(8,128)S(1)} fusion(bf16[1,8,16384]{2,1,0:T(8,128)(2,1)} %param.4), kind=kLoop, calls=%fused_computation.23 | loop fusion | flops 131072 | bytes 786432
  2.1 0.1 copy.107
  2.2 0.2 copy.76
  2.4 0.3 fusion.8
  2.7 0.1 copy.80
  2.9 0.1 eq.88
  2.9 0.1 copy.78
  3.0 0.2 convolution_bitcast_fusion
  3.2 0.1 copy.79
  3.3 0.1 reshape.280
  3.4 0.1 copy.81
  3.5 0.1 copy.82
  3.7 0.1 concatenate.9
  3.8 0.5 broadcast.323
  4.3 0.8 reduce.8
  5.1 1.1 %reshape.305 = bf16[128,2,576]{2,1,0:T(2,128)(2,1)} reshape(bf16[128,1152]{1,0:T(8,128)(2,1)S(1)} %reduce.8) | data formatting | bytes 589824
  6.1 18.0 %all-to-all-start = ((bf16[128,2,576]{2,1,0:T(2,128)(2,1)}), bf16[128,2,576]{2,1,0:T(2,128)(2,1)S(1)}, u32[]{:S(2)}, u32[]{:S(2)}) async-start(bf16[128,2,576]{2,1,0:T(2,128)(2,1)} %reshape.305), calls=%async_computation | async-start | bytes 655360 | tf_op jit(solution)/shard_map/all_to_all | solution.py:79
  24.1 1.9 %fusion.22 = f32[1024,128]{1,0:T(8,128)S(1)} fusion(), kind=kLoop, calls=%fused_computation.41 | loop fusion | flops 1835008 | bytes 524288 | tf_op jit(solution)/shard_map/sin | solution.py:22
  26.1 1.9 %fusion.23 = f32[1024,128]{1,0:T(8,128)S(1)} fusion(), kind=kLoop, calls=%fused_computation.42 | loop fusion | flops 1835008 | bytes 524288 | tf_op jit(solution)/shard_map/cos | solution.py:22
  28.0 0.2 fusion.40
  28.2 0.1 dynamic_slice.3
  28.3 0.1 fusion.43
  28.4 0.1 multiply_convert_fusion.2
  28.5 1.0 %copy.75 = f32[1024,8]{1,0:T(8,128)} copy(f32[1024,8]{0,1:T(8,128)S(1)} %get-tuple-element.10) | data formatting | bytes 65536 | tf_op jit(solution)/shard_map/sin | solution.py:21
  29.5 1.0 %copy.74 = f32[1024,8]{1,0:T(8,128)} copy(f32[1024,8]{0,1:T(8,128)S(1)} %get-tuple-element.9) | data formatting | bytes 65536 | tf_op jit(solution)/shard_map/cos | solution.py:21
  30.5 0.2 convert_element_type.117
  30.8 0.1 pad.5.clone
  30.9 6.5 %multiply_convert_fusion.1 = (bf16[1024,8,128]{2,1,0:T(8,128)(2,1)S(1)}, bf16[1024,8,128]{2,1,0:T(8,128)(2,1)}) fusion(f32[1024,128]{1,0:T(8,128)S(1)} %fusion.22, f32[1024,8]{1,0:T(8,128)} %copy.75, f32[1024,128]{1,0:T(8,128)S(1)} %fusion.23, f32[1024,8]{1,0:T(8,128)} %copy.74), kind=kLoop, calls=%fused_computation.1 | loop fusion | flops 10485760 | bytes 5308416 | tf_op jit(solution)/shard_map/convert_element_type | solution.py:24
  37.4 2.6 %all-to-all-done = bf16[128,2,576]{2,1,0:T(2,128)(2,1)S(1)} async-done(((bf16[128,2,576]{2,1,0:T(2,128)(2,1)}), bf16[128,2,576]{2,1,0:T(2,128)(2,1)S(1)}, u32[]{:S(2)}, u32[]{:S(2)}) %all-to-all-start) | async-done | bytes 294944 | tf_op jit(solution)/shard_map/all_to_all | solution.py:79
  40.0 0.5 reshape.306
  40.5 0.7 copy.84
  41.2 0.1 copy.86
  41.3 0.1 reshape.285
  41.5 0.1 copy.85
  41.6 0.1 reshape.283
  41.7 0.3 convolution_convert_fusion
  42.1 2.3 %fusion = f32[1024,256]{0,1:T(8,128)S(1)} fusion(bf16[128,8,8,128]{3,2,1,0:T(8,128)(2,1)} %bitcast.66, bf16[1024,2]{0,1:T(2,128)(2,1)S(1)} %reshape.285, bf16[1024,128]{0,1:T(8,128)(2,1)S(1)} %convolution_convert_fusion, bf16[256]{0:T(256)(128)(2,1)S(1)} %pad.5.clone), kind=kOutput, calls=%fused_computation.2 | convolution fusion | flops 538443776 | bytes 3412480 | tf_op jit(solution)/shard_map/dot_general | solution.py:92
  44.4 0.7 fusion.3
  45.2 0.1 fusion.17
  45.3 0.1 add.122
  45.4 0.1 add.120
  45.5 0.2 fusion.25
  45.7 0.2 convolution_add_fusion
  45.9 0.2 copy.87
  46.1 0.1 reshape.286
  46.3 0.1 maximum_bitcast_fusion
  46.4 0.3 copy.88
  46.7 26.8 %all_to_all.17 = f32[128,1,528]{2,1,0:T(1,128)S(1)} all-to-all(f32[128,1,528]{2,1,0:T(1,128)S(1)} %copy.88), channel_id=1, replica_groups=mesh['chan'=128,'tm'=4] {'chan'}, dimensions={0} | all-to-all | bytes 540672 | tf_op jit(solution)/shard_map/all_to_all | solution.py:113
  73.5 0.2 copy.89
  73.7 0.1 slice_reduce_fusion
  73.8 0.1 copy.90
  73.9 0.1 reshape.287
  74.1 0.1 fusion.33
  74.1 0.1 reshape.288
  74.3 0.2 copy.91
  74.4 2.7 %collective-permute-start = (f32[16,4,8]{2,1,0:T(4,128)S(1)}, f32[16,4,8]{2,1,0:T(4,128)S(1)}, u32[]{:S(2)}, u32[]{:S(2)}) collective-permute-start(f32[16,4,8]{2,1,0:T(4,128)S(1)} %bitcast_subtract_fusion), channel_id=1, source_target_pairs={{0,1},{1,0},{2,3},{3,2},{4,5},{5,4},{6,7},{7,6},{8,9},{9,8},{10,11... | collective-permute-start | bytes 6152 | tf_op jit(solution)/shard_map/ppermute | solution.py:35
  77.2 0.1 convert_reduce_fusion
  77.3 2.9 %collective-permute-done = f32[16,4,8]{2,1,0:T(4,128)S(1)} collective-permute-done((f32[16,4,8]{2,1,0:T(4,128)S(1)}, f32[16,4,8]{2,1,0:T(4,128)S(1)}, u32[]{:S(2)}, u32[]{:S(2)}) %collective-permute-start) | collective-permute-done | bytes 2080 | tf_op jit(solution)/shard_map/ppermute | solution.py:35
  80.3 3.3 %collective-permute-start.1 = (f32[16,4,8]{2,1,0:T(4,128)S(1)}, f32[16,4,8]{2,1,0:T(4,128)S(1)}, u32[]{:S(2)}, u32[]{:S(2)}) collective-permute-start(f32[16,4,8]{2,1,0:T(4,128)S(1)} %add.126), channel_id=1, source_target_pairs={{0,2},{1,3},{2,0},{3,1},{4,6},{5,7},{6,4},{7,5},{8,10},{9,11},{10,... | collective-permute-start | bytes 6152 | tf_op jit(solution)/shard_map/ppermute | solution.py:35
  83.6 4.0 %collective-permute-done.1 = f32[16,4,8]{2,1,0:T(4,128)S(1)} collective-permute-done((f32[16,4,8]{2,1,0:T(4,128)S(1)}, f32[16,4,8]{2,1,0:T(4,128)S(1)}, u32[]{:S(2)}, u32[]{:S(2)}) %collective-permute-start.1) | collective-permute-done | bytes 2080 | tf_op jit(solution)/shard_map/ppermute | solution.py:35
  87.6 0.1 divide_bitcast_fusion
  87.7 0.7 copy.92
  (18 shorter events, 0.1 us)
Async XLA Ops:
  0.0 2.4 %copy-start.1 = (f32[8]{0:T(128)S(1)}, f32[8]{0:T(128)}, u32[]{:S(2)}) copy-start(f32[8]{0:T(128)} %param.6) | copy-start | bytes 100
  1.1 1.8 %copy-start = (s32[2048]{0:T(1024)S(1)}, s32[2048]{0:T(1024)}, u32[]{:S(2)}) copy-start(s32[2048]{0:T(1024)} %param.7) | copy-start | bytes 24580
  6.1 33.8 %all-to-all-start = ((bf16[128,2,576]{2,1,0:T(2,128)(2,1)}), bf16[128,2,576]{2,1,0:T(2,128)(2,1)S(1)}, u32[]{:S(2)}, u32[]{:S(2)}) async-start(bf16[128,2,576]{2,1,0:T(2,128)(2,1)} %reshape.305), calls=%async_computation | async-start | bytes 655360 | tf_op jit(solution)/shard_map/all_to_all | solution.py:79
  74.4 5.8 %collective-permute-start = (f32[16,4,8]{2,1,0:T(4,128)S(1)}, f32[16,4,8]{2,1,0:T(4,128)S(1)}, u32[]{:S(2)}, u32[]{:S(2)}) collective-permute-start(f32[16,4,8]{2,1,0:T(4,128)S(1)} %bitcast_subtract_fusion), channel_id=1, source_target_pairs={{0,1},{1,0},{2,3},{3,2},{4,5},{5,4},{6,7},{7,6},{8,9},{9,8},{10,11... | collective-permute-start | bytes 6152 | tf_op jit(solution)/shard_map/ppermute | solution.py:35
  80.3 7.3 %collective-permute-start.1 = (f32[16,4,8]{2,1,0:T(4,128)S(1)}, f32[16,4,8]{2,1,0:T(4,128)S(1)}, u32[]{:S(2)}, u32[]{:S(2)}) collective-permute-start(f32[16,4,8]{2,1,0:T(4,128)S(1)} %add.126), channel_id=1, source_target_pairs={{0,2},{1,3},{2,0},{3,1},{4,6},{5,7},{6,4},{7,5},{8,10},{9,11},{10,... | collective-permute-start | bytes 6152 | tf_op jit(solution)/shard_map/ppermute | solution.py:35

commit v8 on v7

--- a/solution.py
+++ b/solution.py
@@ -6,6 +6,7 @@
 from jax.sharding import PartitionSpec as P
 
 G = 16
+CHAN_PARTS = (("cz", 8), ("cy", 8), ("cc", 2))
 
 
 def tables(length, minor):
@@ -37,6 +38,22 @@
     return x
 
 
+def chan_all_to_all(x, parts):
+    sizes = [n for _, n in parts]
+    rest = x.shape[1:]
+    x = x.reshape(*sizes, *rest)
+    for k in reversed(range(len(parts))):
+        x = lax.all_to_all(x, parts[k][0], k, k, tiled=True)
+    return x.reshape(-1, *rest)
+
+
+def chan_index(parts):
+    me = 0
+    for name, n in parts:
+        me = me * n + lax.axis_index(name)
+    return me
+
+
 def split_dot(a, b):
     hi = lax.reduce_precision(a, exponent_bits=8, mantissa_bits=7)
     lo = a - hi
@@ -45,10 +62,10 @@
             + jnp.dot(lo.astype(jnp.bfloat16), b16, preferred_element_type=jnp.float32))
 
 
-def body(visibilities, flags, taper, group_ids):
+def body(visibilities, flags, taper, group_ids, parts=CHAN_PARTS):
     _, local_chans, column_entries = visibilities.shape
     baselines = column_entries // 8
-    n_chan = lax.axis_size("chan")
+    n_chan = math.prod(n for _, n in parts)
     channels = local_chans * n_chan
     shard_bl = baselines // n_chan
     shard_cols = shard_bl * 8
@@ -76,7 +93,7 @@
         sums_lo.astype(jnp.bfloat16),
         jnp.zeros((n_chan, pad), jnp.bfloat16),
     ], axis=1)
-    got = lax.all_to_all(payload.reshape(n_chan, 1, -1), "chan", 0, 0, tiled=True).reshape(n_chan, -1)
+    got = chan_all_to_all(payload.reshape(n_chan, 1, -1), parts).reshape(n_chan, -1)
     turned = got[:, :block].reshape(channels, shard_cols)
     col_parts = got[:, block:block + 2 * local_chans].reshape(n_chan, 2, local_chans)
     col_parts = col_parts.transpose(0, 2, 1).reshape(channels, 2)
@@ -94,7 +111,7 @@
     col_cos = cos_all[:, shard_cols] + cos_all[:, shard_cols + 1]
     col_sin = sin_all[:, shard_cols] + sin_all[:, shard_cols + 1]
 
-    me = lax.axis_index("chan")
+    me = chan_index(parts)
     shard_groups = lax.dynamic_slice_in_dim(group_ids, me * shard_bl, shard_bl)
     member = (shard_groups[:, None] == jnp.arange(G, dtype=jnp.int32)[None, :]).astype(jnp.float32)
     eye_s = jnp.eye(4, dtype=jnp.float32)
@@ -110,7 +127,7 @@
         col_cos.reshape(n_chan, own_d),
         col_sin.reshape(n_chan, own_d),
     ], axis=1)
-    got = lax.all_to_all(payload, "chan", 0, 0, tiled=True)
+    got = chan_all_to_all(payload, parts)
     auto_own = jnp.sum(got[:, :own_d * G * 4], axis=0).reshape(own_d, G, 4)
     cs = got[:, own_d * G * 4:].reshape(G, 4, 2, 2, own_d)
     group_real = cs[:, :, 0, 0] + cs[:, :, 1, 1]
@@ -127,10 +144,13 @@
 
 
 def solution(mesh):
+    names = tuple(name for name, _ in CHAN_PARTS)
+    split = jax.sharding.Mesh(
+        mesh.devices.reshape(*(n for _, n in CHAN_PARTS), mesh.shape["tm"]), names + ("tm",))
     return jax.shard_map(
         body,
-        mesh=mesh,
-        in_specs=(P("tm", "chan", None), P("tm", "chan", None), P("chan"), P()),
-        out_specs=P(None, None, "chan"),
+        mesh=split,
+        in_specs=(P("tm", names, None), P("tm", names, None), P(names), P()),
+        out_specs=P(None, None, names),
         check_vma=False,
     )

time: 89.1 us -> 111 us (1.25)
  blocking collectives: 26.8 us -> 39.7 us
  waiting for transfers between devices: 9.52 us -> 18.8 us
    all_to_all x1 -> x4, blocking collectives: 26.8 us -> 39.7 us  [chan_all_to_all(): x = lax.all_to_all(x, parts[k][0], k, k, tiled=True)]
    all_to_all x1 -> x2, waiting for transfers between devices: 2.6 us -> 11.9 us  [chan_all_to_all(): x = lax.all_to_all(x, parts[k][0], k, k, tiled=True)]
    unnamed x7 -> x5, local copies, waits for them, and re-layouts: 1.66 us -> 0.11 us
    concatenate x1 -> x3, local copies, waits for them, and re-layouts: 0.12 us -> 1.66 us  [body(): jnp.concatenate([tapered.reshape(n_chan, block), sums_hi.astype(jnp.bfloa...]
    all_to_all x3 -> x4, local copies, waits for them, and re-layouts: 1.17 us -> 2.23 us  [chan_all_to_all(): x = lax.all_to_all(x, parts[k][0], k, k, tiled=True)]
    all_to_all x1 -> x2, starting transfers between devices: 18 us -> 17.4 us  [chan_all_to_all(): x = lax.all_to_all(x, parts[k][0], k, k, tiled=True)]
  transfers between devices with their start and end apart: 3 -> 4, of which waited for: 3 -> 4; matrix products, arithmetic and copies ran while one was open for 15% -> 12% of each run, Pallas kernels for 0% -> 0%
where the time goes in v8:
time: 111 us; the launch traced here: 110 us
  blocking collectives  39.7 us (36%)
  starting transfers between devices  23.5 us (21%)
  waiting for transfers between devices  18.8 us (17%)
  other arithmetic  14.8 us (13%)
  local copies, waits for them, and re-layouts  8.6 us (8%)
  matrix products  4.37 us (4%)
    all_to_all x4, blocking collectives, chan_all_to_all(): x = lax.all_to_all(x, parts[k][0], k, k, tiled=True)  39.7 us
    all_to_all x2, starting transfers between devices, chan_all_to_all(): x = lax.all_to_all(x, parts[k][0], k, k, tiled=True)  17.4 us
    all_to_all x2, waiting for transfers between devices, chan_all_to_all(): x = lax.all_to_all(x, parts[k][0], k, k, tiled=True)  11.9 us
    ppermute x2, waiting for transfers between devices, tm_sum(): x = x + lax.ppermute(x, 'tm', pairs)  6.91 us
    convert_element_type x1, other arithmetic, tables(): ((ca * cb - sa * sb) * scale).astype(jnp.bfloat16).reshape(length, length)  6.52 us
    ppermute x2, starting transfers between devices, tm_sum(): x = x + lax.ppermute(x, 'tm', pairs)  6.05 us
    sin x1, other arithmetic, tables(): cb, sb = (jnp.cos(pb)[:, None, :], jnp.sin(pb)[:, None, :])  2.67 us
    cos x1, other arithmetic, tables(): cb, sb = (jnp.cos(pb)[:, None, :], jnp.sin(pb)[:, None, :])  2.67 us
  transfers between devices with their start and end apart: 4, of which 4 were waited for; matrix products, arithmetic and copies ran while one was open for 12% of the time, Pallas kernels for 0%

profile of v8, /device:TPU:6, one launch (start us, length us, event | category | flops | bytes accessed | tf_op | source)
XLA Modules:
  0.0 110.1 jit_solution(8498425763711543345)
XLA Ops:
  0.0 0.9 subtract_convert_fusion
  0.9 0.2 convert_element_type.106
  1.1 1.0 convert_bitcast_fusion
  2.1 0.1 copy.106
  2.2 0.2 copy.74
  2.4 0.3 fusion.8
  2.7 0.2 copy.76
  2.9 0.1 concatenate.19
  3.0 0.1 eq.88
  3.1 0.2 convolution_bitcast_fusion
  3.3 0.1 copy.78
  3.4 0.1 reshape.284
  3.5 0.1 copy.79
  3.7 0.1 copy.80
  3.8 1.6 %concatenate.22 = bf16[8,8,2,1,1152]{4,2,1,0,3:T(2,128)(2,1)S(1)} concatenate(bf16[8,8,2,1,1024]{4,2,1,0,3:T(2,128)(2,1)S(1)} %concatenate.19, bf16[8,8,2,1,8]{4,2,1,0,3:T(2,128)(2,1)S(1)} %bitcast.65, bf16[8,8,2,1,8]{4,2,1,0,3:T(2,128)(2,1)S(1)} %bitcast.66, bf16[8,8,2,1,112]{4,2,1,0,3:T(2,128)(2,1)S(1)} %broadcast_in_dim.4), dimensions={4} | concatenate | bytes 589824 | tf_op jit(solution)/shard_map/concatenate | solution.py:90
  5.4 4.0 %all_to_all.30 = bf16[8,8,2,1,1152]{4,1,0,3,2:T(8,128)(2,1)S(1)} all-to-all(bf16[8,8,2,1,1152]{4,1,0,3,2:T(8,128)(2,1)S(1)} %copy.81), channel_id=1, replica_groups=mesh['cz'=8,'cy'=8,'cc'=2,'tm'=4] {'cc'}, dimensions={2} | all-to-all | bytes 589824 | tf_op jit(solution)/shard_map/all_to_all | solution.py:46
  9.4 1.0 copy.82
  10.4 7.1 %all-to-all-start.1 = ((bf16[8,8,2,1,1152]{4,2,0,3,1:T(2,128)(2,1)}), bf16[8,8,2,1,1152]{4,2,0,3,1:T(2,128)(2,1)S(1)}, u32[]{:S(2)}, u32[]{:S(2)}) async-start(bf16[8,8,2,1,1152]{4,2,0,3,1:T(2,128)(2,1)} %copy.82), calls=%async_computation.1 | async-start | bytes 589824 | tf_op jit(solution)/shard_map/all_to_all | solution.py:46
  17.5 0.2 fusion.40
  17.7 0.2 copy.73
  17.9 0.2 copy.72
  18.2 0.1 dynamic_slice.3
  18.2 0.1 fusion.43
  18.3 0.1 multiply_convert_fusion.2
  18.4 0.2 convert_element_type.117
  18.7 0.1 pad.5.clone
  18.8 2.7 %fusion.22 = f32[1024,128]{1,0:T(8,128)} fusion(), kind=kLoop, calls=%fused_computation.41 | loop fusion | flops 1835008 | bytes 524288 | tf_op jit(solution)/shard_map/sin | solution.py:23
  21.4 2.7 %fusion.23 = f32[1024,128]{1,0:T(8,128)} fusion(), kind=kLoop, calls=%fused_computation.42 | loop fusion | flops 1835008 | bytes 524288 | tf_op jit(solution)/shard_map/cos | solution.py:23
  24.1 6.3 %all-to-all-done.1 = bf16[8,8,2,1,1152]{4,2,0,3,1:T(2,128)(2,1)S(1)} async-done(((bf16[8,8,2,1,1152]{4,2,0,3,1:T(2,128)(2,1)}), bf16[8,8,2,1,1152]{4,2,0,3,1:T(2,128)(2,1)S(1)}, u32[]{:S(2)}, u32[]{:S(2)}) %all-to-all-start.1) | async-done | bytes 294944 | tf_op jit(solution)/shard_map/all_to_all | solution.py:46
  30.4 0.9 copy.83
  31.3 10.3 %all-to-all-start.2 = ((bf16[8,8,2,1,1152]{4,2,1,3,0:T(2,128)(2,1)}), bf16[8,8,2,1,1152]{4,2,1,3,0:T(2,128)(2,1)S(1)}, u32[]{:S(2)}, u32[]{:S(2)}) async-start(bf16[8,8,2,1,1152]{4,2,1,3,0:T(2,128)(2,1)} %copy.83), calls=%async_computation.2 | async-start | bytes 589824 | tf_op jit(solution)/shard_map/all_to_all | solution.py:46
  41.6 6.5 %multiply_convert_fusion.1 = (bf16[1024,8,128]{2,1,0:T(8,128)(2,1)S(1)}, bf16[1024,8,128]{2,1,0:T(8,128)(2,1)}) fusion(f32[1024,128]{1,0:T(8,128)} %fusion.22, f32[1024,8]{1,0:T(8,128)S(1)} %copy.73, f32[1024,128]{1,0:T(8,128)} %fusion.23, f32[1024,8]{1,0:T(8,128)S(1)} %copy.72), kind=kLoop, calls=%fused_computation.1 | loop fusion | flops 10485760 | bytes 5308416 | tf_op jit(solution)/shard_map/convert_element_type | solution.py:25
  48.1 5.6 %all-to-all-done.2 = bf16[8,8,2,1,1152]{4,2,1,3,0:T(2,128)(2,1)S(1)} async-done(((bf16[8,8,2,1,1152]{4,2,1,3,0:T(2,128)(2,1)}), bf16[8,8,2,1,1152]{4,2,1,3,0:T(2,128)(2,1)S(1)}, u32[]{:S(2)}, u32[]{:S(2)}) %all-to-all-start.2) | async-done | bytes 294944 | tf_op jit(solution)/shard_map/all_to_all | solution.py:46
  53.7 0.1 reshape_reshape.4
  53.9 0.1 copy.85
  54.1 0.1 reshape.287
  54.2 0.1 reshape.285
  54.3 0.3 convolution_convert_fusion
  54.7 2.3 %fusion = f32[1024,256]{0,1:T(8,128)S(1)} fusion(bf16[128,8,8,128]{3,2,1,0:T(8,128)(2,1)} %bitcast.62, bf16[1024,2]{0,1:T(2,128)(2,1)S(1)} %reshape.287, bf16[1024,128]{0,1:T(8,128)(2,1)S(1)} %convolution_convert_fusion, bf16[256]{0:T(256)(128)(2,1)S(1)} %pad.5.clone), kind=kOutput, calls=%fused_computation.2 | convolution fusion | flops 538443776 | bytes 3412480 | tf_op jit(solution)/shard_map/dot_general | solution.py:109
  57.0 0.8 fusion.3
  57.8 0.1 fusion.17
  57.9 0.1 add.132
  58.0 0.1 add.130
  58.2 0.2 fusion.25
  58.4 0.2 convolution_add_fusion
  58.7 0.2 copy.86
  58.9 0.2 concatenate.24
  59.1 0.2 pad_maximum_fusion
  59.3 4.0 %all_to_all.31 = f32[8,8,2,528]{3,1,0,2:T(8,128)S(1)} all-to-all(f32[8,8,2,528]{3,1,0,2:T(8,128)S(1)} %copy.87), channel_id=1, replica_groups=mesh['cz'=8,'cy'=8,'cc'=2,'tm'=4] {'cc'}, dimensions={2} | all-to-all | bytes 540672 | tf_op jit(solution)/shard_map/all_to_all | solution.py:46
  63.3 0.3 copy.88
  63.6 16.2 %all_to_all.32 = f32[8,8,2,528]{3,2,0,1:T(2,128)S(1)} all-to-all(f32[8,8,2,528]{3,2,0,1:T(2,128)S(1)} %copy.88), channel_id=1, replica_groups=mesh['cz'=8,'cy'=8,'cc'=2,'tm'=4] {'cy'}, dimensions={1} | all-to-all | bytes 540672 | tf_op jit(solution)/shard_map/all_to_all | solution.py:46
  79.9 15.5 %all_to_all.33 = f32[8,8,2,528]{3,2,1,0:T(2,128)S(1)} all-to-all(f32[8,8,2,528]{3,2,1,0:T(2,128)S(1)} %copy.89), channel_id=1, replica_groups=mesh['cz'=8,'cy'=8,'cc'=2,'tm'=4] {'cz'}, dimensions={0} | all-to-all | bytes 540672 | tf_op jit(solution)/shard_map/all_to_all | solution.py:46
  95.4 0.2 reshape.288
  95.7 0.1 reshape.289
  95.8 0.1 fusion.33
  95.9 0.1 reshape.290
  96.0 0.2 copy.90
  96.2 2.7 %collective-permute-start = (f32[16,4,8]{2,1,0:T(4,128)S(1)}, f32[16,4,8]{2,1,0:T(4,128)S(1)}, u32[]{:S(2)}, u32[]{:S(2)}) collective-permute-start(f32[16,4,8]{2,1,0:T(4,128)S(1)} %bitcast_subtract_fusion), channel_id=1, source_target_pairs={{0,1},{1,0},{2,3},{3,2},{4,5},{5,4},{6,7},{7,6},{8,9},{9,8},{10,11... | collective-permute-start | bytes 6152 | tf_op jit(solution)/shard_map/ppermute | solution.py:36
  99.0 0.1 convert_reduce_fusion
  99.1 2.9 %collective-permute-done = f32[16,4,8]{2,1,0:T(4,128)S(1)} collective-permute-done((f32[16,4,8]{2,1,0:T(4,128)S(1)}, f32[16,4,8]{2,1,0:T(4,128)S(1)}, u32[]{:S(2)}, u32[]{:S(2)}) %collective-permute-start) | collective-permute-done | bytes 2080 | tf_op jit(solution)/shard_map/ppermute | solution.py:36
  102.0 3.3 %collective-permute-start.1 = (f32[16,4,8]{2,1,0:T(4,128)S(1)}, f32[16,4,8]{2,1,0:T(4,128)S(1)}, u32[]{:S(2)}, u32[]{:S(2)}) collective-permute-start(f32[16,4,8]{2,1,0:T(4,128)S(1)} %add.136), channel_id=1, source_target_pairs={{0,2},{1,3},{2,0},{3,1},{4,6},{5,7},{6,4},{7,5},{8,10},{9,11},{10,... | collective-permute-start | bytes 6152 | tf_op jit(solution)/shard_map/ppermute | solution.py:36
  105.4 4.0 %collective-permute-done.1 = f32[16,4,8]{2,1,0:T(4,128)S(1)} collective-permute-done((f32[16,4,8]{2,1,0:T(4,128)S(1)}, f32[16,4,8]{2,1,0:T(4,128)S(1)}, u32[]{:S(2)}, u32[]{:S(2)}) %collective-permute-start.1) | collective-permute-done | bytes 2080 | tf_op jit(solution)/shard_map/ppermute | solution.py:36
  109.4 0.1 divide_bitcast_fusion
  109.5 0.7 copy.91
  (24 shorter events, 0.4 us)
Async XLA Ops:
  0.0 2.4 %copy-start.1 = (f32[8]{0:T(128)S(1)}, f32[8]{0:T(128)}, u32[]{:S(2)}) copy-start(f32[8]{0:T(128)} %param.6) | copy-start | bytes 100
  2.1 0.9 copy-start
  10.4 20.0 %all-to-all-start.1 = ((bf16[8,8,2,1,1152]{4,2,0,3,1:T(2,128)(2,1)}), bf16[8,8,2,1,1152]{4,2,0,3,1:T(2,128)(2,1)S(1)}, u32[]{:S(2)}, u32[]{:S(2)}) async-start(bf16[8,8,2,1,1152]{4,2,0,3,1:T(2,128)(2,1)} %copy.82), calls=%async_computation.1 | async-start | bytes 589824 | tf_op jit(solution)/shard_map/all_to_all | solution.py:46
  31.3 22.4 %all-to-all-start.2 = ((bf16[8,8,2,1,1152]{4,2,1,3,0:T(2,128)(2,1)}), bf16[8,8,2,1,1152]{4,2,1,3,0:T(2,128)(2,1)S(1)}, u32[]{:S(2)}, u32[]{:S(2)}) async-start(bf16[8,8,2,1,1152]{4,2,1,3,0:T(2,128)(2,1)} %copy.83), calls=%async_computation.2 | async-start | bytes 589824 | tf_op jit(solution)/shard_map/all_to_all | solution.py:46
  96.2 5.8 %collective-permute-start = (f32[16,4,8]{2,1,0:T(4,128)S(1)}, f32[16,4,8]{2,1,0:T(4,128)S(1)}, u32[]{:S(2)}, u32[]{:S(2)}) collective-permute-start(f32[16,4,8]{2,1,0:T(4,128)S(1)} %bitcast_subtract_fusion), channel_id=1, source_target_pairs={{0,1},{1,0},{2,3},{3,2},{4,5},{5,4},{6,7},{7,6},{8,9},{9,8},{10,11... | collective-permute-start | bytes 6152 | tf_op jit(solution)/shard_map/ppermute | solution.py:36
  102.0 7.3 %collective-permute-start.1 = (f32[16,4,8]{2,1,0:T(4,128)S(1)}, f32[16,4,8]{2,1,0:T(4,128)S(1)}, u32[]{:S(2)}, u32[]{:S(2)}) collective-permute-start(f32[16,4,8]{2,1,0:T(4,128)S(1)} %add.136), channel_id=1, source_target_pairs={{0,2},{1,3},{2,0},{3,1},{4,6},{5,7},{6,4},{7,5},{8,10},{9,11},{10,... | collective-permute-start | bytes 6152 | tf_op jit(solution)/shard_map/ppermute | solution.py:36

commit v9 on v7

--- a/solution.py
+++ b/solution.py
@@ -31,7 +31,8 @@
         return lax.psum(x, "tm")
     step = 1
     while step < n:
-        pairs = [(i, i ^ step) for i in range(n)]
+        width = 2 * step
+        pairs = [(i, (i // width) * width + width - 1 - i % width) for i in range(n)]
         x = x + lax.ppermute(x, "tm", pairs)
         step *= 2
     return x

time: 89.1 us -> 88.8 us (level)
  starting transfers between devices: 24 us -> 23.1 us
    ppermute x2, starting transfers between devices: 6.04 us -> 5.12 us  [tm_sum(): x = x + lax.ppermute(x, 'tm', pairs)]
where the time goes in v9:
time: 88.8 us; the launch traced here: 88.1 us
  blocking collectives  26.8 us (30%)
  starting transfers between devices  23.1 us (26%)
  other arithmetic  14.1 us (16%)
  waiting for transfers between devices  10.1 us (11%)
  local copies, waits for them, and re-layouts  9.23 us (10%)
  matrix products  4.37 us (5%)
    all_to_all x1, blocking collectives, body(): got = lax.all_to_all(payload, 'chan', 0, 0, tiled=True)  26.8 us
    all_to_all x1, starting transfers between devices, body(): lax.all_to_all(payload.reshape(n_chan, 1, -1), 'chan', 0, 0, tiled=True)  18 us
    ppermute x2, waiting for transfers between devices, tm_sum(): x = x + lax.ppermute(x, 'tm', pairs)  7.54 us
    convert_element_type x1, other arithmetic, tables(): ((ca * cb - sa * sb) * scale).astype(jnp.bfloat16).reshape(length, length)  6.51 us
    ppermute x2, starting transfers between devices, tm_sum(): x = x + lax.ppermute(x, 'tm', pairs)  5.12 us
    all_to_all x1, waiting for transfers between devices, body(): lax.all_to_all(payload.reshape(n_chan, 1, -1), 'chan', 0, 0, tiled=True)  2.6 us
    dot_general x1, matrix products, body(): sin_all = jnp.dot(sin_tab, rhs, preferred_element_type=jnp.float32)  2.34 us
    sin x1, other arithmetic, tables(): cb, sb = (jnp.cos(pb)[:, None, :], jnp.sin(pb)[:, None, :])  1.93 us
  transfers between devices with their start and end apart: 3, of which 3 were waited for; matrix products, arithmetic and copies ran while one was open for 15% of the time, Pallas kernels for 0%

profile of v9, /device:TPU:6, one launch (start us, length us, event | category | flops | bytes accessed | tf_op | source)
XLA Modules:
  0.0 88.1 jit_solution(3503307003301855999)
XLA Ops:
  0.0 0.9 subtract_convert_fusion
  0.9 0.2 convert_element_type.106
  1.1 1.0 %convert_bitcast_fusion = f32[1,8,128,128]{3,1,2,0:T(8,128)S(1)} fusion(bf16[1,8,16384]{2,1,0:T(8,128)(2,1)} %param.4), kind=kLoop, calls=%fused_computation.23 | loop fusion | flops 131072 | bytes 786432
  2.1 0.1 copy.107
  2.2 0.2 copy.76
  2.4 0.3 fusion.8
  2.7 0.1 copy.80
  2.9 0.1 eq.88
  2.9 0.1 copy.78
  3.0 0.2 convolution_bitcast_fusion
  3.2 0.1 copy.79
  3.3 0.1 reshape.280
  3.4 0.1 copy.81
  3.5 0.1 copy.82
  3.7 0.1 concatenate.9
  3.8 0.5 broadcast.323
  4.3 0.8 reduce.8
  5.1 1.1 %reshape.305 = bf16[128,2,576]{2,1,0:T(2,128)(2,1)} reshape(bf16[128,1152]{1,0:T(8,128)(2,1)S(1)} %reduce.8) | data formatting | bytes 589824
  6.1 18.0 %all-to-all-start = ((bf16[128,2,576]{2,1,0:T(2,128)(2,1)}), bf16[128,2,576]{2,1,0:T(2,128)(2,1)S(1)}, u32[]{:S(2)}, u32[]{:S(2)}) async-start(bf16[128,2,576]{2,1,0:T(2,128)(2,1)} %reshape.305), calls=%async_computation | async-start | bytes 655360 | tf_op jit(solution)/shard_map/all_to_all | solution.py:80
  24.1 1.9 %fusion.22 = f32[1024,128]{1,0:T(8,128)S(1)} fusion(), kind=kLoop, calls=%fused_computation.41 | loop fusion | flops 1835008 | bytes 524288 | tf_op jit(solution)/shard_map/sin | solution.py:22
  26.1 1.9 %fusion.23 = f32[1024,128]{1,0:T(8,128)S(1)} fusion(), kind=kLoop, calls=%fused_computation.42 | loop fusion | flops 1835008 | bytes 524288 | tf_op jit(solution)/shard_map/cos | solution.py:22
  28.0 0.2 fusion.40
  28.2 0.1 dynamic_slice.3
  28.3 0.1 fusion.43
  28.4 0.1 multiply_convert_fusion.2
  28.5 1.0 %copy.75 = f32[1024,8]{1,0:T(8,128)} copy(f32[1024,8]{0,1:T(8,128)S(1)} %get-tuple-element.10) | data formatting | bytes 65536 | tf_op jit(solution)/shard_map/sin | solution.py:21
  29.5 1.0 %copy.74 = f32[1024,8]{1,0:T(8,128)} copy(f32[1024,8]{0,1:T(8,128)S(1)} %get-tuple-element.9) | data formatting | bytes 65536 | tf_op jit(solution)/shard_map/cos | solution.py:21
  30.5 0.2 convert_element_type.117
  30.8 0.1 pad.5.clone
  30.9 6.5 %multiply_convert_fusion.1 = (bf16[1024,8,128]{2,1,0:T(8,128)(2,1)S(1)}, bf16[1024,8,128]{2,1,0:T(8,128)(2,1)}) fusion(f32[1024,128]{1,0:T(8,128)S(1)} %fusion.22, f32[1024,8]{1,0:T(8,128)} %copy.75, f32[1024,128]{1,0:T(8,128)S(1)} %fusion.23, f32[1024,8]{1,0:T(8,128)} %copy.74), kind=kLoop, calls=%fused_computation.1 | loop fusion | flops 10485760 | bytes 5308416 | tf_op jit(solution)/shard_map/convert_element_type | solution.py:24
  37.4 2.6 %all-to-all-done = bf16[128,2,576]{2,1,0:T(2,128)(2,1)S(1)} async-done(((bf16[128,2,576]{2,1,0:T(2,128)(2,1)}), bf16[128,2,576]{2,1,0:T(2,128)(2,1)S(1)}, u32[]{:S(2)}, u32[]{:S(2)}) %all-to-all-start) | async-done | bytes 294944 | tf_op jit(solution)/shard_map/all_to_all | solution.py:80
  40.0 0.5 reshape.306
  40.5 0.7 copy.84
  41.2 0.1 copy.86
  41.3 0.1 reshape.285
  41.5 0.1 copy.85
  41.6 0.1 reshape.283
  41.7 0.3 convolution_convert_fusion
  42.1 2.3 %fusion = f32[1024,256]{0,1:T(8,128)S(1)} fusion(bf16[128,8,8,128]{3,2,1,0:T(8,128)(2,1)} %bitcast.66, bf16[1024,2]{0,1:T(2,128)(2,1)S(1)} %reshape.285, bf16[1024,128]{0,1:T(8,128)(2,1)S(1)} %convolution_convert_fusion, bf16[256]{0:T(256)(128)(2,1)S(1)} %pad.5.clone), kind=kOutput, calls=%fused_computation.2 | convolution fusion | flops 538443776 | bytes 3412480 | tf_op jit(solution)/shard_map/dot_general | solution.py:93
  44.4 0.7 fusion.3
  45.2 0.1 fusion.17
  45.3 0.1 add.122
  45.4 0.1 add.120
  45.5 0.2 fusion.25
  45.7 0.2 convolution_add_fusion
  45.9 0.2 copy.87
  46.1 0.1 reshape.286
  46.3 0.1 maximum_bitcast_fusion
  46.4 0.3 copy.88
  46.7 26.8 %all_to_all.17 = f32[128,1,528]{2,1,0:T(1,128)S(1)} all-to-all(f32[128,1,528]{2,1,0:T(1,128)S(1)} %copy.88), channel_id=1, replica_groups=mesh['chan'=128,'tm'=4] {'chan'}, dimensions={0} | all-to-all | bytes 540672 | tf_op jit(solution)/shard_map/all_to_all | solution.py:114
  73.5 0.2 copy.89
  73.7 0.1 slice_reduce_fusion
  73.8 0.1 copy.90
  73.9 0.1 reshape.287
  74.1 0.1 fusion.33
  74.1 0.1 reshape.288
  74.3 0.2 copy.91
  74.4 2.7 %collective-permute-start = (f32[16,4,8]{2,1,0:T(4,128)S(1)}, f32[16,4,8]{2,1,0:T(4,128)S(1)}, u32[]{:S(2)}, u32[]{:S(2)}) collective-permute-start(f32[16,4,8]{2,1,0:T(4,128)S(1)} %bitcast_subtract_fusion), channel_id=1, source_target_pairs={{0,1},{1,0},{2,3},{3,2},{4,5},{5,4},{6,7},{7,6},{8,9},{9,8},{10,11... | collective-permute-start | bytes 6152 | tf_op jit(solution)/shard_map/ppermute | solution.py:36
  77.2 0.1 convert_reduce_fusion
  77.3 2.9 %collective-permute-done = f32[16,4,8]{2,1,0:T(4,128)S(1)} collective-permute-done((f32[16,4,8]{2,1,0:T(4,128)S(1)}, f32[16,4,8]{2,1,0:T(4,128)S(1)}, u32[]{:S(2)}, u32[]{:S(2)}) %collective-permute-start) | collective-permute-done | bytes 2080 | tf_op jit(solution)/shard_map/ppermute | solution.py:36
  80.3 2.4 %collective-permute-start.1 = (f32[16,4,8]{2,1,0:T(4,128)S(1)}, f32[16,4,8]{2,1,0:T(4,128)S(1)}, u32[]{:S(2)}, u32[]{:S(2)}) collective-permute-start(f32[16,4,8]{2,1,0:T(4,128)S(1)} %add.126), channel_id=1, source_target_pairs={{0,3},{1,2},{2,1},{3,0},{4,7},{5,6},{6,5},{7,4},{8,11},{9,10},{10,... | collective-permute-start | bytes 6152 | tf_op jit(solution)/shard_map/ppermute | solution.py:36
  82.7 4.6 %collective-permute-done.1 = f32[16,4,8]{2,1,0:T(4,128)S(1)} collective-permute-done((f32[16,4,8]{2,1,0:T(4,128)S(1)}, f32[16,4,8]{2,1,0:T(4,128)S(1)}, u32[]{:S(2)}, u32[]{:S(2)}) %collective-permute-start.1) | collective-permute-done | bytes 2080 | tf_op jit(solution)/shard_map/ppermute | solution.py:36
  87.3 0.1 divide_bitcast_fusion
  87.4 0.7 copy.92
  (18 shorter events, 0.1 us)
Async XLA Ops:
  0.0 2.4 %copy-start.1 = (f32[8]{0:T(128)S(1)}, f32[8]{0:T(128)}, u32[]{:S(2)}) copy-start(f32[8]{0:T(128)} %param.6) | copy-start | bytes 100
  1.1 1.8 %copy-start = (s32[2048]{0:T(1024)S(1)}, s32[2048]{0:T(1024)}, u32[]{:S(2)}) copy-start(s32[2048]{0:T(1024)} %param.7) | copy-start | bytes 24580
  6.1 33.8 %all-to-all-start = ((bf16[128,2,576]{2,1,0:T(2,128)(2,1)}), bf16[128,2,576]{2,1,0:T(2,128)(2,1)S(1)}, u32[]{:S(2)}, u32[]{:S(2)}) async-start(bf16[128,2,576]{2,1,0:T(2,128)(2,1)} %reshape.305), calls=%async_computation | async-start | bytes 655360 | tf_op jit(solution)/shard_map/all_to_all | solution.py:80
  74.4 5.8 %collective-permute-start = (f32[16,4,8]{2,1,0:T(4,128)S(1)}, f32[16,4,8]{2,1,0:T(4,128)S(1)}, u32[]{:S(2)}, u32[]{:S(2)}) collective-permute-start(f32[16,4,8]{2,1,0:T(4,128)S(1)} %bitcast_subtract_fusion), channel_id=1, source_target_pairs={{0,1},{1,0},{2,3},{3,2},{4,5},{5,4},{6,7},{7,6},{8,9},{9,8},{10,11... | collective-permute-start | bytes 6152 | tf_op jit(solution)/shard_map/ppermute | solution.py:36
  80.3 7.0 %collective-permute-start.1 = (f32[16,4,8]{2,1,0:T(4,128)S(1)}, f32[16,4,8]{2,1,0:T(4,128)S(1)}, u32[]{:S(2)}, u32[]{:S(2)}) collective-permute-start(f32[16,4,8]{2,1,0:T(4,128)S(1)} %add.126), channel_id=1, source_target_pairs={{0,3},{1,2},{2,1},{3,0},{4,7},{5,6},{6,5},{7,4},{8,11},{9,10},{10,... | collective-permute-start | bytes 6152 | tf_op jit(solution)/shard_map/ppermute | solution.py:36

commit v10 on v9

--- a/solution.py
+++ b/solution.py
@@ -69,17 +69,16 @@
     sums = sums.reshape(local_chans, G * 8).T
     sums_hi = lax.reduce_precision(sums, exponent_bits=8, mantissa_bits=7)
     sums_lo = sums - sums_hi
-    block = local_chans * shard_cols
-    pad = -(block + 2 * local_chans) % 128
-    payload = jnp.concatenate([
-        tapered.reshape(n_chan, block),
+    pad = shard_cols - 2 * local_chans
+    extra_row = jnp.concatenate([
         sums_hi.astype(jnp.bfloat16),
         sums_lo.astype(jnp.bfloat16),
         jnp.zeros((n_chan, pad), jnp.bfloat16),
     ], axis=1)
-    got = lax.all_to_all(payload.reshape(n_chan, 1, -1), "chan", 0, 0, tiled=True).reshape(n_chan, -1)
-    turned = got[:, :block].reshape(channels, shard_cols)
-    col_parts = got[:, block:block + 2 * local_chans].reshape(n_chan, 2, local_chans)
+    payload = jnp.concatenate([tapered, extra_row[:, None, :]], axis=1)
+    got = lax.all_to_all(payload, "chan", 0, 0, tiled=True)
+    turned = got[:, :local_chans, :].reshape(channels, shard_cols)
+    col_parts = got[:, local_chans, :2 * local_chans].reshape(n_chan, 2, local_chans)
     col_parts = col_parts.transpose(0, 2, 1).reshape(channels, 2)
 
     cols = jnp.arange(shard_cols, dtype=jnp.int32)

time: 88.8 us -> 88.3 us (level)
  waiting for transfers between devices: 10.1 us -> 13.3 us
  blocking collectives: 26.8 us -> 23.7 us
  local copies, waits for them, and re-layouts: 9.23 us -> 8.04 us
  matrix products: 4.37 us -> 5.33 us
    all_to_all x1, waiting for transfers between devices: 2.6 us -> 5.76 us  [body(): got = lax.all_to_all(payload, 'chan', 0, 0, tiled=True)]
    all_to_all x1, blocking collectives: 26.8 us -> 23.7 us  [body(): got = lax.all_to_all(payload, 'chan', 0, 0, tiled=True)]
    unnamed x7 -> x6, local copies, waits for them, and re-layouts: 1.66 us -> 0.18 us
    concatenate x1 -> x2, local copies, waits for them, and re-layouts: 0.12 us -> 1.28 us  [the longest x1 1.21 us: body(): payload = jnp.concatenate([tapered, extra_row[:, None, :]], axis=1)]
    dot_general x1, matrix products: 0.34 us -> 1.28 us  [body(): jnp.dot(turned, permute, preferred_element_type=jnp.float32)]
where the time goes in v10:
time: 88.3 us; the launch traced here: 87.6 us
  blocking collectives  23.7 us (27%)
  starting transfers between devices  23.5 us (27%)
  other arithmetic  13.4 us (15%)
  waiting for transfers between devices  13.3 us (15%)
  local copies, waits for them, and re-layouts  8.04 us (9%)
  matrix products  5.33 us (6%)
    all_to_all x1, blocking collectives, body(): got = lax.all_to_all(payload, 'chan', 0, 0, tiled=True)  23.7 us
    all_to_all x1, starting transfers between devices, body(): got = lax.all_to_all(payload, 'chan', 0, 0, tiled=True)  18.3 us
    ppermute x2, waiting for transfers between devices, tm_sum(): x = x + lax.ppermute(x, 'tm', pairs)  7.53 us
    convert_element_type x1, other arithmetic, tables(): ((ca * cb - sa * sb) * scale).astype(jnp.bfloat16).reshape(length, length)  6.51 us
    all_to_all x1, waiting for transfers between devices, body(): got = lax.all_to_all(payload, 'chan', 0, 0, tiled=True)  5.76 us
    ppermute x2, starting transfers between devices, tm_sum(): x = x + lax.ppermute(x, 'tm', pairs)  5.14 us
    dot_general x1, matrix products, body(): sin_all = jnp.dot(sin_tab, rhs, preferred_element_type=jnp.float32)  2.35 us
    sin x1, other arithmetic, tables(): cb, sb = (jnp.cos(pb)[:, None, :], jnp.sin(pb)[:, None, :])  1.93 us
  transfers between devices with their start and end apart: 3, of which 3 were waited for; matrix products, arithmetic and copies ran while one was open for 15% of the time, Pallas kernels for 0%

profile of v10, /device:TPU:6, one launch (start us, length us, event | category | flops | bytes accessed | tf_op | source)
XLA Modules:
  0.0 87.6 jit_solution(14633301391873099863)
XLA Ops:
  0.0 0.0 copy-start
  0.0 0.0 copy-start.1
  0.0 0.9 subtract_convert_fusion
  0.9 0.2 convert_element_type.106
  1.1 1.0 %convert_bitcast_fusion = f32[1,8,128,128]{3,1,2,0:T(8,128)S(1)} fusion(bf16[1,8,16384]{2,1,0:T(8,128)(2,1)} %param.4), kind=kLoop, calls=%fused_computation.23 | loop fusion | flops 131072 | bytes 786432
  2.1 0.1 copy.83
  2.2 0.2 copy.55
  2.4 0.0 copy-done
  2.4 0.1 eq.88
  2.5 0.1 copy.57
  2.6 0.0 copy-done.1
  2.6 0.3 fusion.8
  2.9 0.2 convolution_bitcast_fusion
  3.1 0.1 copy.58
  3.1 0.1 reshape.267
  3.3 0.1 pad.10.clone
  3.4 0.1 maximum_bitcast_fusion.1
  3.5 1.2 %copy.59 = bf16[128,9,128]{2,1,0:T(8,128)(2,1)} copy(bf16[128,9,128]{0,2,1:T(8,128)(2,1)S(1)} %pad_maximum_fusion) | data formatting | bytes 589824 | tf_op jit(solution)/shard_map/concatenate | solution.py:78
  4.7 18.3 %all-to-all-start = ((bf16[128,9,128]{2,1,0:T(8,128)(2,1)}), bf16[128,9,128]{2,1,0:T(8,128)(2,1)}, u32[]{:S(2)}, u32[]{:S(2)}) async-start(bf16[128,9,128]{2,1,0:T(8,128)(2,1)} %copy.59), calls=%async_computation | async-start | bytes 1048576 | tf_op jit(solution)/shard_map/all_to_all | solution.py:79
  23.0 1.9 %fusion.22 = f32[1024,128]{1,0:T(8,128)S(1)} fusion(), kind=kLoop, calls=%fused_computation.43 | loop fusion | flops 1835008 | bytes 524288 | tf_op jit(solution)/shard_map/sin | solution.py:22
  25.0 1.9 %fusion.23 = f32[1024,128]{1,0:T(8,128)S(1)} fusion(), kind=kLoop, calls=%fused_computation.44 | loop fusion | flops 1835008 | bytes 524288 | tf_op jit(solution)/shard_map/cos | solution.py:22
  26.9 0.2 fusion.40
  27.1 0.1 dynamic_slice.3
  27.2 0.1 fusion.43
  27.3 0.1 multiply_convert_fusion.2
  27.4 1.0 %copy.54 = f32[1024,8]{1,0:T(8,128)} copy(f32[1024,8]{0,1:T(8,128)S(1)} %get-tuple-element.10) | data formatting | bytes 65536 | tf_op jit(solution)/shard_map/sin | solution.py:21
  28.4 1.0 %copy.53 = f32[1024,8]{1,0:T(8,128)} copy(f32[1024,8]{0,1:T(8,128)S(1)} %get-tuple-element.9) | data formatting | bytes 65536 | tf_op jit(solution)/shard_map/cos | solution.py:21
  29.4 0.1 pad.5.clone
  29.5 0.2 convert_element_type.117
  29.7 6.5 %multiply_convert_fusion.1 = (bf16[1024,8,128]{2,1,0:T(8,128)(2,1)S(1)}, bf16[1024,8,128]{2,1,0:T(8,128)(2,1)}) fusion(f32[1024,128]{1,0:T(8,128)S(1)} %fusion.22, f32[1024,8]{1,0:T(8,128)} %copy.54, f32[1024,128]{1,0:T(8,128)S(1)} %fusion.23, f32[1024,8]{1,0:T(8,128)} %copy.53), kind=kLoop, calls=%fused_computation.1 | loop fusion | flops 10485760 | bytes 5308416 | tf_op jit(solution)/shard_map/convert_element_type | solution.py:24
  36.3 5.8 %all-to-all-done = bf16[128,9,128]{2,1,0:T(8,128)(2,1)} async-done(((bf16[128,9,128]{2,1,0:T(8,128)(2,1)}), bf16[128,9,128]{2,1,0:T(8,128)(2,1)}, u32[]{:S(2)}, u32[]{:S(2)}) %all-to-all-start) | async-done | bytes 294944 | tf_op jit(solution)/shard_map/all_to_all | solution.py:79
  42.0 1.0 %slice.71 = bf16[128,1,16]{2,1,0:T(2,128)(2,1)S(1)} slice(bf16[128,9,128]{2,1,0:T(8,128)(2,1)} %all-to-all-done), slice={[0:128], [8:9], [0:16]} | slice | bytes 8192 | tf_op jit(solution)/shard_map/slice | solution.py:81
  43.0 0.1 copy.70
  43.1 0.1 copy.61
  43.2 0.1 reshape.269
  43.4 1.3 %convolution_convert_fusion = bf16[1024,128]{0,1:T(8,128)(2,1)S(1)} fusion(bf16[128,9,128]{2,1,0:T(8,128)(2,1)} %all-to-all-done, s32[128]{0:T(128)S(1)} %fusion.51), kind=kOutput, calls=%fused_computation.12 | convolution fusion | flops 33701888 | bytes 524800 | tf_op jit(solution)/shard_map/dot_general | solution.py:87
  44.6 2.4 %fusion = f32[1024,256]{0,1:T(8,128)S(1)} fusion(bf16[128,8,8,128]{3,2,1,0:T(8,128)(2,1)} %bitcast.65, bf16[1024,2]{0,1:T(2,128)(2,1)S(1)} %reshape.269, bf16[1024,128]{0,1:T(8,128)(2,1)S(1)} %convolution_convert_fusion, bf16[256]{0:T(256)(128)(2,1)S(1)} %pad.5.clone), kind=kOutput, calls=%fused_computation.2 | convolution fusion | flops 538443776 | bytes 3412480 | tf_op jit(solution)/shard_map/dot_general | solution.py:92
  47.0 0.8 fusion.3
  47.8 0.1 fusion.17
  47.9 0.1 add.122
  48.0 0.1 add.120
  48.0 0.2 fusion.25
  48.3 0.2 convolution_add_fusion
  48.5 0.2 copy.62
  48.7 0.1 reshape.270
  48.9 0.1 maximum_bitcast_fusion
  48.9 0.3 copy.63
  49.3 23.7 %all_to_all.17 = f32[128,1,528]{2,1,0:T(1,128)S(1)} all-to-all(f32[128,1,528]{2,1,0:T(1,128)S(1)} %copy.63), channel_id=1, replica_groups=mesh['chan'=128,'tm'=4] {'chan'}, dimensions={0} | all-to-all | bytes 540672 | tf_op jit(solution)/shard_map/all_to_all | solution.py:113
  73.0 0.2 copy.64
  73.2 0.1 slice_reduce_fusion
  73.3 0.1 copy.65
  73.4 0.1 reshape.271
  73.6 0.1 fusion.33
  73.6 0.1 reshape.272
  73.8 0.2 copy.66
  74.0 2.7 %collective-permute-start = (f32[16,4,8]{2,1,0:T(4,128)S(1)}, f32[16,4,8]{2,1,0:T(4,128)S(1)}, u32[]{:S(2)}, u32[]{:S(2)}) collective-permute-start(f32[16,4,8]{2,1,0:T(4,128)S(1)} %bitcast_subtract_fusion), channel_id=1, source_target_pairs={{0,1},{1,0},{2,3},{3,2},{4,5},{5,4},{6,7},{7,6},{8,9},{9,8},{10,11... | collective-permute-start | bytes 6152 | tf_op jit(solution)/shard_map/ppermute | solution.py:36
  76.7 0.1 convert_reduce_fusion
  76.8 2.9 %collective-permute-done = f32[16,4,8]{2,1,0:T(4,128)S(1)} collective-permute-done((f32[16,4,8]{2,1,0:T(4,128)S(1)}, f32[16,4,8]{2,1,0:T(4,128)S(1)}, u32[]{:S(2)}, u32[]{:S(2)}) %collective-permute-start) | collective-permute-done | bytes 2080 | tf_op jit(solution)/shard_map/ppermute | solution.py:36
  79.8 2.4 %collective-permute-start.1 = (f32[16,4,8]{2,1,0:T(4,128)S(1)}, f32[16,4,8]{2,1,0:T(4,128)S(1)}, u32[]{:S(2)}, u32[]{:S(2)}) collective-permute-start(f32[16,4,8]{2,1,0:T(4,128)S(1)} %add.126), channel_id=1, source_target_pairs={{0,3},{1,2},{2,1},{3,0},{4,7},{5,6},{6,5},{7,4},{8,11},{9,10},{10,... | collective-permute-start | bytes 6152 | tf_op jit(solution)/shard_map/ppermute | solution.py:36
  82.2 4.6 %collective-permute-done.1 = f32[16,4,8]{2,1,0:T(4,128)S(1)} collective-permute-done((f32[16,4,8]{2,1,0:T(4,128)S(1)}, f32[16,4,8]{2,1,0:T(4,128)S(1)}, u32[]{:S(2)}, u32[]{:S(2)}) %collective-permute-start.1) | collective-permute-done | bytes 2080 | tf_op jit(solution)/shard_map/ppermute | solution.py:36
  86.8 0.1 divide_bitcast_fusion
  86.9 0.7 copy.67
  (13 shorter events, 0.1 us)
Async XLA Ops:
  0.0 2.4 %copy-start = (s32[2048]{0:T(1024)S(1)}, s32[2048]{0:T(1024)}, u32[]{:S(2)}) copy-start(s32[2048]{0:T(1024)} %param.7) | copy-start | bytes 24580
  0.0 2.6 %copy-start.1 = (f32[8]{0:T(128)S(1)}, f32[8]{0:T(128)}, u32[]{:S(2)}) copy-start(f32[8]{0:T(128)} %param.6) | copy-start | bytes 100
  4.7 37.3 %all-to-all-start = ((bf16[128,9,128]{2,1,0:T(8,128)(2,1)}), bf16[128,9,128]{2,1,0:T(8,128)(2,1)}, u32[]{:S(2)}, u32[]{:S(2)}) async-start(bf16[128,9,128]{2,1,0:T(8,128)(2,1)} %copy.59), calls=%async_computation | async-start | bytes 1048576 | tf_op jit(solution)/shard_map/all_to_all | solution.py:79
  74.0 5.8 %collective-permute-start = (f32[16,4,8]{2,1,0:T(4,128)S(1)}, f32[16,4,8]{2,1,0:T(4,128)S(1)}, u32[]{:S(2)}, u32[]{:S(2)}) collective-permute-start(f32[16,4,8]{2,1,0:T(4,128)S(1)} %bitcast_subtract_fusion), channel_id=1, source_target_pairs={{0,1},{1,0},{2,3},{3,2},{4,5},{5,4},{6,7},{7,6},{8,9},{9,8},{10,11... | collective-permute-start | bytes 6152 | tf_op jit(solution)/shard_map/ppermute | solution.py:36
  79.8 7.0 %collective-permute-start.1 = (f32[16,4,8]{2,1,0:T(4,128)S(1)}, f32[16,4,8]{2,1,0:T(4,128)S(1)}, u32[]{:S(2)}, u32[]{:S(2)}) collective-permute-start(f32[16,4,8]{2,1,0:T(4,128)S(1)} %add.126), channel_id=1, source_target_pairs={{0,3},{1,2},{2,1},{3,0},{4,7},{5,6},{6,5},{7,4},{8,11},{9,10},{10,... | collective-permute-start | bytes 6152 | tf_op jit(solution)/shard_map/ppermute | solution.py:36

commit v11 on v10

--- a/solution.py
+++ b/solution.py
@@ -27,15 +27,13 @@
 
 
 def tm_sum(x, n):
-    if n & (n - 1):
-        return lax.psum(x, "tm")
-    step = 1
-    while step < n:
-        width = 2 * step
-        pairs = [(i, (i // width) * width + width - 1 - i % width) for i in range(n)]
-        x = x + lax.ppermute(x, "tm", pairs)
-        step *= 2
-    return x
+    got = lax.all_to_all(jnp.broadcast_to(x[None], (n, *x.shape)), "tm", 0, 0, tiled=True)
+    while got.shape[0] > 1:
+        if got.shape[0] % 2:
+            got = jnp.concatenate([got[:1] + got[1:2], got[2:]])
+        else:
+            got = got[0::2] + got[1::2]
+    return got[0]
 
 
 def split_dot(a, b):

time: 88.3 us -> 87.7 us (level)
  the two profiles are of different devices: /device:TPU:6 before, /device:TPU:1 now
where the time goes in v11:
time: 87.7 us; the launch traced here: 86.9 us
  starting transfers between devices  29.6 us (34%)
  waiting for transfers between devices  27.6 us (31%)
  other arithmetic  14.6 us (17%)
  local copies, waits for them, and re-layouts  9.44 us (11%)
  matrix products  5.33 us (6%)
    all_to_all x2, starting transfers between devices, body(): got = lax.all_to_all(payload, 'chan', 0, 0, tiled=True)  25.6 us
    all_to_all x2, waiting for transfers between devices, body(): got = lax.all_to_all(payload, 'chan', 0, 0, tiled=True)  23.4 us
    convert_element_type x1, other arithmetic, tables(): ((ca * cb - sa * sb) * scale).astype(jnp.bfloat16).reshape(length, length)  6.51 us
    all_to_all x1, waiting for transfers between devices, tm_sum(): lax.all_to_all(jnp.broadcast_to(x[None], (n, *x.shape)), 'tm', 0, 0, tile...  4.16 us
    all_to_all x1, starting transfers between devices, tm_sum(): lax.all_to_all(jnp.broadcast_to(x[None], (n, *x.shape)), 'tm', 0, 0, tile...  4 us
    dot_general x1, matrix products, body(): sin_all = jnp.dot(sin_tab, rhs, preferred_element_type=jnp.float32)  2.36 us
    sin x1, other arithmetic, tables(): cb, sb = (jnp.cos(pb)[:, None, :], jnp.sin(pb)[:, None, :])  1.93 us
    cos x1, other arithmetic, tables(): cb, sb = (jnp.cos(pb)[:, None, :], jnp.sin(pb)[:, None, :])  1.91 us
  transfers between devices with their start and end apart: 3, of which 3 were waited for; matrix products, arithmetic and copies ran while one was open for 15% of the time, Pallas kernels for 0%

profile of v11, /device:TPU:1, one launch (start us, length us, event | category | flops | bytes accessed | tf_op | source)
XLA Modules:
  0.0 86.9 jit_solution(16251504763003977161)
XLA Ops:
  0.0 0.0 copy-start.1
  0.0 0.9 %subtract_convert_fusion = bf16[1,8,2048]{2,1,0:T(8,128)(2,1)S(1)} fusion(s32[1,8,2048]{2,1,0:T(8,128)} %param.5), kind=kLoop, calls=%fused_computation.52 | loop fusion | flops 32768 | bytes 98304 | tf_op jit(solution)/shard_map/convert_element_type | solution.py:56
  0.9 0.2 convert_element_type.106
  1.1 1.0 %convert_bitcast_fusion = f32[1,8,128,128]{3,1,2,0:T(8,128)S(1)} fusion(bf16[1,8,16384]{2,1,0:T(8,128)(2,1)} %param.4), kind=kLoop, calls=%fused_computation.23 | loop fusion | flops 131072 | bytes 786432
  2.1 0.1 copy.83
  2.2 0.2 copy.55
  2.4 0.0 copy-done
  2.4 0.1 eq.88
  2.5 0.1 copy.57
  2.6 0.0 copy-done.1
  2.6 0.3 fusion.8
  2.9 0.2 convolution_bitcast_fusion
  3.1 0.1 copy.58
  3.1 0.1 reshape.268
  3.3 0.1 pad.10.clone
  3.3 0.1 maximum_bitcast_fusion.1
  3.5 1.2 %copy.59 = bf16[128,9,128]{2,1,0:T(8,128)(2,1)} copy(bf16[128,9,128]{0,2,1:T(8,128)(2,1)S(1)} %pad_maximum_fusion) | data formatting | bytes 589824 | tf_op jit(solution)/shard_map/concatenate | solution.py:76
  4.7 18.9 %all-to-all-start = ((bf16[128,9,128]{2,1,0:T(8,128)(2,1)}), bf16[128,9,128]{2,1,0:T(8,128)(2,1)}, u32[]{:S(2)}, u32[]{:S(2)}) async-start(bf16[128,9,128]{2,1,0:T(8,128)(2,1)} %copy.59), calls=%async_computation | async-start | bytes 1048576 | tf_op jit(solution)/shard_map/all_to_all | solution.py:77
  23.6 1.9 %fusion.22 = f32[1024,128]{1,0:T(8,128)S(1)} fusion(), kind=kLoop, calls=%fused_computation.43 | loop fusion | flops 1835008 | bytes 524288 | tf_op jit(solution)/shard_map/sin | solution.py:22
  25.5 1.9 %fusion.23 = f32[1024,128]{1,0:T(8,128)S(1)} fusion(), kind=kLoop, calls=%fused_computation.44 | loop fusion | flops 1835008 | bytes 524288 | tf_op jit(solution)/shard_map/cos | solution.py:22
  27.4 0.2 fusion.43
  27.6 0.1 dynamic_slice.3
  27.7 0.1 fusion.46
  27.8 0.1 multiply_convert_fusion.2
  27.9 1.0 %copy.54 = f32[1024,8]{1,0:T(8,128)} copy(f32[1024,8]{0,1:T(8,128)S(1)} %get-tuple-element.10) | data formatting | bytes 65536 | tf_op jit(solution)/shard_map/sin | solution.py:21
  28.9 1.0 %copy.53 = f32[1024,8]{1,0:T(8,128)} copy(f32[1024,8]{0,1:T(8,128)S(1)} %get-tuple-element.9) | data formatting | bytes 65536 | tf_op jit(solution)/shard_map/cos | solution.py:21
  29.9 0.1 pad.5.clone
  30.0 0.2 convert_element_type.117
  30.3 6.5 %multiply_convert_fusion.1 = (bf16[1024,8,128]{2,1,0:T(8,128)(2,1)S(1)}, bf16[1024,8,128]{2,1,0:T(8,128)(2,1)}) fusion(f32[1024,128]{1,0:T(8,128)S(1)} %fusion.22, f32[1024,8]{1,0:T(8,128)} %copy.54, f32[1024,128]{1,0:T(8,128)S(1)} %fusion.23, f32[1024,8]{1,0:T(8,128)} %copy.53), kind=kLoop, calls=%fused_computation.1 | loop fusion | flops 10485760 | bytes 5308416 | tf_op jit(solution)/shard_map/convert_element_type | solution.py:24
  36.8 7.0 %all-to-all-done = bf16[128,9,128]{2,1,0:T(8,128)(2,1)} async-done(((bf16[128,9,128]{2,1,0:T(8,128)(2,1)}), bf16[128,9,128]{2,1,0:T(8,128)(2,1)}, u32[]{:S(2)}, u32[]{:S(2)}) %all-to-all-start) | async-done | bytes 294944 | tf_op jit(solution)/shard_map/all_to_all | solution.py:77
  43.8 1.0 %slice.89 = bf16[128,1,16]{2,1,0:T(2,128)(2,1)S(1)} slice(bf16[128,9,128]{2,1,0:T(8,128)(2,1)} %all-to-all-done), slice={[0:128], [8:9], [0:16]} | slice | bytes 8192 | tf_op jit(solution)/shard_map/slice | solution.py:79
  44.8 0.1 copy.70
  44.8 0.1 copy.61
  45.0 0.1 reshape.270
  45.1 1.3 %convolution_convert_fusion = bf16[1024,128]{0,1:T(8,128)(2,1)S(1)} fusion(bf16[128,9,128]{2,1,0:T(8,128)(2,1)} %all-to-all-done, s32[128]{0:T(128)S(1)} %fusion.54), kind=kOutput, calls=%fused_computation.12 | convolution fusion | flops 33701888 | bytes 524800 | tf_op jit(solution)/shard_map/dot_general | solution.py:85
  46.4 2.4 %fusion = f32[1024,256]{0,1:T(8,128)S(1)} fusion(bf16[128,8,8,128]{3,2,1,0:T(8,128)(2,1)} %bitcast.74, bf16[1024,2]{0,1:T(2,128)(2,1)S(1)} %reshape.270, bf16[1024,128]{0,1:T(8,128)(2,1)S(1)} %convolution_convert_fusion, bf16[256]{0:T(256)(128)(2,1)S(1)} %pad.5.clone), kind=kOutput, calls=%fused_computation.2 | convolution fusion | flops 538443776 | bytes 3412480 | tf_op jit(solution)/shard_map/dot_general | solution.py:90
  48.8 0.8 fusion.3
  49.5 0.1 fusion.17
  49.6 0.1 add.122
  49.7 0.1 add.120
  49.8 0.2 fusion.25
  50.0 0.2 convolution_add_fusion
  50.3 0.2 copy.62
  50.5 0.1 reshape.271
  50.6 0.1 maximum_bitcast_fusion
  50.7 1.0 %copy.63 = f32[128,1,528]{2,1,0:T(1,128)} copy(f32[128,1,528]{2,0,1:T(8,128)S(1)} %maximum_bitcast_fusion) | data formatting | bytes 540672 | tf_op jit(solution)/shard_map/all_to_all | solution.py:111
  51.7 6.8 %all-to-all-start.1 = ((f32[128,1,528]{2,1,0:T(1,128)}), f32[128,1,528]{2,1,0:T(1,128)S(1)}, u32[]{:S(2)}, u32[]{:S(2)}) async-start(f32[128,1,528]{2,1,0:T(1,128)} %copy.63), calls=%async_computation.1 | async-start | bytes 655360 | tf_op jit(solution)/shard_map/all_to_all | solution.py:111
  58.5 0.1 convert_reduce_fusion
  58.6 16.4 %all-to-all-done.1 = f32[128,1,528]{2,1,0:T(1,128)S(1)} async-done(((f32[128,1,528]{2,1,0:T(1,128)}), f32[128,1,528]{2,1,0:T(1,128)S(1)}, u32[]{:S(2)}, u32[]{:S(2)}) %all-to-all-start.1) | async-done | bytes 270368 | tf_op jit(solution)/shard_map/all_to_all | solution.py:111
  75.1 0.2 copy.64
  75.2 0.1 slice_reduce_fusion
  75.4 0.1 copy.65
  75.5 0.1 reshape.272
  75.6 0.1 fusion.33
  75.7 0.1 reshape.273
  75.8 0.2 copy.66
  76.0 0.1 copy.67
  76.1 0.7 reshape.290
  76.8 4.0 %all-to-all-start.2 = ((f32[4,1,512]{2,1,0:T(1,128)}), f32[4,1,512]{2,1,0:T(1,128)S(1)}, u32[]{:S(2)}, u32[]{:S(2)}) async-start(f32[4,1,512]{2,1,0:T(1,128)} %reshape.290), calls=%async_computation.2 | async-start | bytes 16384 | tf_op jit(solution)/shard_map/all_to_all | solution.py:30
  80.8 4.2 %all-to-all-done.2 = f32[4,1,512]{2,1,0:T(1,128)S(1)} async-done(((f32[4,1,512]{2,1,0:T(1,128)}), f32[4,1,512]{2,1,0:T(1,128)S(1)}, u32[]{:S(2)}, u32[]{:S(2)}) %all-to-all-start.2) | async-done | bytes 8224 | tf_op jit(solution)/shard_map/all_to_all | solution.py:30
  85.0 0.5 broadcast.326
  85.5 0.7 reduce.8
  86.2 0.1 reshape.291
  86.3 0.6 fusion.41
  (15 shorter events, 0.1 us)
Async XLA Ops:
  0.0 2.4 %copy-start = (s32[2048]{0:T(1024)S(1)}, s32[2048]{0:T(1024)}, u32[]{:S(2)}) copy-start(s32[2048]{0:T(1024)} %param.7) | copy-start | bytes 24580
  0.0 2.6 %copy-start.1 = (f32[8]{0:T(128)S(1)}, f32[8]{0:T(128)}, u32[]{:S(2)}) copy-start(f32[8]{0:T(128)} %param.6) | copy-start | bytes 100
  4.7 39.1 %all-to-all-start = ((bf16[128,9,128]{2,1,0:T(8,128)(2,1)}), bf16[128,9,128]{2,1,0:T(8,128)(2,1)}, u32[]{:S(2)}, u32[]{:S(2)}) async-start(bf16[128,9,128]{2,1,0:T(8,128)(2,1)} %copy.59), calls=%async_computation | async-start | bytes 1048576 | tf_op jit(solution)/shard_map/all_to_all | solution.py:77
  51.7 23.3 %all-to-all-start.1 = ((f32[128,1,528]{2,1,0:T(1,128)}), f32[128,1,528]{2,1,0:T(1,128)S(1)}, u32[]{:S(2)}, u32[]{:S(2)}) async-start(f32[128,1,528]{2,1,0:T(1,128)} %copy.63), calls=%async_computation.1 | async-start | bytes 655360 | tf_op jit(solution)/shard_map/all_to_all | solution.py:111
  76.8 8.2 %all-to-all-start.2 = ((f32[4,1,512]{2,1,0:T(1,128)}), f32[4,1,512]{2,1,0:T(1,128)S(1)}, u32[]{:S(2)}, u32[]{:S(2)}) async-start(f32[4,1,512]{2,1,0:T(1,128)} %reshape.290), calls=%async_computation.2 | async-start | bytes 16384 | tf_op jit(solution)/shard_map/all_to_all | solution.py:30

commit v12 on v11

--- a/solution.py
+++ b/solution.py
@@ -27,13 +27,14 @@
 
 
 def tm_sum(x, n):
-    got = lax.all_to_all(jnp.broadcast_to(x[None], (n, *x.shape)), "tm", 0, 0, tiled=True)
+    flat = jnp.broadcast_to(x.reshape(1, 1, -1), (n, 1, x.size))
+    got = lax.all_to_all(flat, "tm", 0, 0, tiled=True)[:, 0]
     while got.shape[0] > 1:
         if got.shape[0] % 2:
             got = jnp.concatenate([got[:1] + got[1:2], got[2:]])
         else:
             got = got[0::2] + got[1::2]
-    return got[0]
+    return got[0].reshape(x.shape)
 
 
 def split_dot(a, b):
@@ -111,17 +112,17 @@
     got = lax.all_to_all(payload, "chan", 0, 0, tiled=True)
     auto_own = jnp.sum(got[:, :own_d * G * 4], axis=0).reshape(own_d, G, 4)
     cs = got[:, own_d * G * 4:].reshape(G, 4, 2, 2, own_d)
+    cs = cs.transpose(1, 0, 2, 3, 4)
     group_real = cs[:, :, 0, 0] + cs[:, :, 1, 1]
     group_imag = cs[:, :, 1, 0] - cs[:, :, 0, 1]
-    cross = group_real * group_real + group_imag * group_imag - auto_own.transpose(1, 2, 0)
+    cross = group_real * group_real + group_imag * group_imag - auto_own.transpose(2, 1, 0)
     cross = tm_sum(cross, times_all)
 
     member_all = (group_ids[None, :] == jnp.arange(G, dtype=jnp.int32)[:, None]).astype(jnp.float32)
     counts = jnp.sum(member_all, axis=1)
     pair_count = jnp.maximum(counts * (counts - 1.0), 1.0)
     norm = jnp.sqrt(pair_count * times_all)
-    spectrum = cross.transpose(1, 0, 2)
-    return spectrum / norm[None, :, None]
+    return cross / norm[None, :, None]
 
 
 def solution(mesh):

time: 87.7 us -> 86.6 us (0.987)
  other arithmetic: 14.6 us -> 13.4 us
  transfers between devices with their start and end apart: 3 -> 3, of which waited for: 3 -> 3; matrix products, arithmetic and copies ran while one was open for 15% -> 16% of each run, Pallas kernels for 0% -> 0%
where the time goes in v12:
time: 86.6 us; the launch traced here: 85.8 us
  starting transfers between devices  29.6 us (34%)
  waiting for transfers between devices  27.6 us (32%)
  other arithmetic  13.4 us (15%)
  local copies, waits for them, and re-layouts  9.59 us (11%)
  matrix products  5.33 us (6%)
    all_to_all x2, starting transfers between devices, body(): got = lax.all_to_all(payload, 'chan', 0, 0, tiled=True)  25.6 us
    all_to_all x2, waiting for transfers between devices, body(): got = lax.all_to_all(payload, 'chan', 0, 0, tiled=True)  23.4 us
    convert_element_type x1, other arithmetic, tables(): ((ca * cb - sa * sb) * scale).astype(jnp.bfloat16).reshape(length, length)  6.51 us
    all_to_all x1, waiting for transfers between devices, tm_sum(): got = lax.all_to_all(flat, 'tm', 0, 0, tiled=True)[:, 0]  4.16 us
    all_to_all x1, starting transfers between devices, tm_sum(): got = lax.all_to_all(flat, 'tm', 0, 0, tiled=True)[:, 0]  4 us
    dot_general x1, matrix products, body(): sin_all = jnp.dot(sin_tab, rhs, preferred_element_type=jnp.float32)  2.36 us
    sin x1, other arithmetic, tables(): cb, sb = (jnp.cos(pb)[:, None, :], jnp.sin(pb)[:, None, :])  1.93 us
    cos x1, other arithmetic, tables(): cb, sb = (jnp.cos(pb)[:, None, :], jnp.sin(pb)[:, None, :])  1.91 us
  transfers between devices with their start and end apart: 3, of which 3 were waited for; matrix products, arithmetic and copies ran while one was open for 16% of the time, Pallas kernels for 0%

profile of v12, /device:TPU:1, one launch (start us, length us, event | category | flops | bytes accessed | tf_op | source)
XLA Modules:
  0.0 85.8 jit_solution(10924333532999215191)
XLA Ops:
  0.0 0.0 copy-start
  0.0 0.0 copy-start.1
  0.0 0.9 %subtract_convert_fusion = bf16[1,8,2048]{2,1,0:T(8,128)(2,1)S(1)} fusion(s32[1,8,2048]{2,1,0:T(8,128)} %param.5), kind=kLoop, calls=%fused_computation.52 | loop fusion | flops 32768 | bytes 98304 | tf_op jit(solution)/shard_map/convert_element_type | solution.py:57
  0.9 0.2 convert_element_type.106
  1.1 1.0 %convert_bitcast_fusion = f32[1,8,128,128]{3,1,2,0:T(8,128)S(1)} fusion(bf16[1,8,16384]{2,1,0:T(8,128)(2,1)} %param.4), kind=kLoop, calls=%fused_computation.23 | loop fusion | flops 131072 | bytes 786432
  2.1 0.1 copy.90
  2.2 0.2 copy.59
  2.4 0.0 copy-done
  2.4 0.1 eq.88
  2.5 0.1 copy.61
  2.6 0.0 copy-done.1
  2.6 0.3 fusion.8
  2.9 0.2 convolution_bitcast_fusion
  3.1 0.1 copy.62
  3.1 0.1 reshape.271
  3.3 0.1 pad.10.clone
  3.3 0.1 maximum_bitcast_fusion.1
  3.5 1.2 %copy.63 = bf16[128,9,128]{2,1,0:T(8,128)(2,1)} copy(bf16[128,9,128]{0,2,1:T(8,128)(2,1)S(1)} %pad_maximum_fusion) | data formatting | bytes 589824 | tf_op jit(solution)/shard_map/concatenate | solution.py:77
  4.7 18.9 %all-to-all-start = ((bf16[128,9,128]{2,1,0:T(8,128)(2,1)}), bf16[128,9,128]{2,1,0:T(8,128)(2,1)}, u32[]{:S(2)}, u32[]{:S(2)}) async-start(bf16[128,9,128]{2,1,0:T(8,128)(2,1)} %copy.63), calls=%async_computation | async-start | bytes 1048576 | tf_op jit(solution)/shard_map/all_to_all | solution.py:78
  23.6 1.9 %fusion.22 = f32[1024,128]{1,0:T(8,128)S(1)} fusion(), kind=kLoop, calls=%fused_computation.43 | loop fusion | flops 1835008 | bytes 524288 | tf_op jit(solution)/shard_map/sin | solution.py:22
  25.5 1.9 %fusion.23 = f32[1024,128]{1,0:T(8,128)S(1)} fusion(), kind=kLoop, calls=%fused_computation.44 | loop fusion | flops 1835008 | bytes 524288 | tf_op jit(solution)/shard_map/cos | solution.py:22
  27.4 0.2 fusion.40
  27.6 0.1 dynamic_slice.3
  27.7 0.1 fusion.43
  27.8 0.1 multiply_convert_fusion.2
  27.9 1.0 %copy.58 = f32[1024,8]{1,0:T(8,128)} copy(f32[1024,8]{0,1:T(8,128)S(1)} %get-tuple-element.10) | data formatting | bytes 65536 | tf_op jit(solution)/shard_map/sin | solution.py:21
  28.9 1.0 %copy.57 = f32[1024,8]{1,0:T(8,128)} copy(f32[1024,8]{0,1:T(8,128)S(1)} %get-tuple-element.9) | data formatting | bytes 65536 | tf_op jit(solution)/shard_map/cos | solution.py:21
  29.9 0.1 pad.5.clone
  30.0 0.2 convert_element_type.117
  30.3 6.5 %multiply_convert_fusion.1 = (bf16[1024,8,128]{2,1,0:T(8,128)(2,1)S(1)}, bf16[1024,8,128]{2,1,0:T(8,128)(2,1)}) fusion(f32[1024,128]{1,0:T(8,128)S(1)} %fusion.22, f32[1024,8]{1,0:T(8,128)} %copy.58, f32[1024,128]{1,0:T(8,128)S(1)} %fusion.23, f32[1024,8]{1,0:T(8,128)} %copy.57), kind=kLoop, calls=%fused_computation.1 | loop fusion | flops 10485760 | bytes 5308416 | tf_op jit(solution)/shard_map/convert_element_type | solution.py:24
  36.8 7.0 %all-to-all-done = bf16[128,9,128]{2,1,0:T(8,128)(2,1)} async-done(((bf16[128,9,128]{2,1,0:T(8,128)(2,1)}), bf16[128,9,128]{2,1,0:T(8,128)(2,1)}, u32[]{:S(2)}, u32[]{:S(2)}) %all-to-all-start) | async-done | bytes 294944 | tf_op jit(solution)/shard_map/all_to_all | solution.py:78
  43.8 1.0 %slice.89 = bf16[128,1,16]{2,1,0:T(2,128)(2,1)S(1)} slice(bf16[128,9,128]{2,1,0:T(8,128)(2,1)} %all-to-all-done), slice={[0:128], [8:9], [0:16]} | slice | bytes 8192 | tf_op jit(solution)/shard_map/slice | solution.py:80
  44.8 0.1 copy.76
  44.8 0.1 copy.65
  45.0 0.1 reshape.273
  45.1 1.3 %convolution_convert_fusion = bf16[1024,128]{0,1:T(8,128)(2,1)S(1)} fusion(bf16[128,9,128]{2,1,0:T(8,128)(2,1)} %all-to-all-done, s32[128]{0:T(128)S(1)} %fusion.52), kind=kOutput, calls=%fused_computation.12 | convolution fusion | flops 33701888 | bytes 524800 | tf_op jit(solution)/shard_map/dot_general | solution.py:86
  46.4 2.4 %fusion = f32[1024,256]{0,1:T(8,128)S(1)} fusion(bf16[128,8,8,128]{3,2,1,0:T(8,128)(2,1)} %bitcast.67, bf16[1024,2]{0,1:T(2,128)(2,1)S(1)} %reshape.273, bf16[1024,128]{0,1:T(8,128)(2,1)S(1)} %convolution_convert_fusion, bf16[256]{0:T(256)(128)(2,1)S(1)} %pad.5.clone), kind=kOutput, calls=%fused_computation.2 | convolution fusion | flops 538443776 | bytes 3412480 | tf_op jit(solution)/shard_map/dot_general | solution.py:91
  48.8 0.8 fusion.3
  49.5 0.1 fusion.17
  49.6 0.1 add.122
  49.7 0.1 add.120
  49.8 0.2 fusion.25
  50.0 0.2 convolution_add_fusion
  50.3 0.2 copy.66
  50.5 0.1 reshape.274
  50.6 0.1 maximum_bitcast_fusion
  50.7 1.0 %copy.67 = f32[128,1,528]{2,1,0:T(1,128)} copy(f32[128,1,528]{2,0,1:T(8,128)S(1)} %maximum_bitcast_fusion) | data formatting | bytes 540672 | tf_op jit(solution)/shard_map/all_to_all | solution.py:112
  51.7 6.8 %all-to-all-start.1 = ((f32[128,1,528]{2,1,0:T(1,128)}), f32[128,1,528]{2,1,0:T(1,128)S(1)}, u32[]{:S(2)}, u32[]{:S(2)}) async-start(f32[128,1,528]{2,1,0:T(1,128)} %copy.67), calls=%async_computation.1 | async-start | bytes 655360 | tf_op jit(solution)/shard_map/all_to_all | solution.py:112
  58.5 0.1 convert_reduce_fusion
  58.6 16.4 %all-to-all-done.1 = f32[128,1,528]{2,1,0:T(1,128)S(1)} async-done(((f32[128,1,528]{2,1,0:T(1,128)}), f32[128,1,528]{2,1,0:T(1,128)S(1)}, u32[]{:S(2)}, u32[]{:S(2)}) %all-to-all-start.1) | async-done | bytes 270368 | tf_op jit(solution)/shard_map/all_to_all | solution.py:112
  75.1 0.2 copy.68
  75.2 0.1 slice_reduce_fusion
  75.4 0.1 copy.69
  75.5 0.1 reshape.275
  75.6 0.1 fusion.33
  75.7 0.1 reshape.276
  75.8 0.2 copy.70
  76.0 0.1 broadcast_in_dim.13
  76.1 0.6 broadcast_in_dim.14
  76.7 4.0 %all-to-all-start.2 = ((f32[4,1,512]{2,1,0:T(1,128)}), f32[4,1,512]{2,1,0:T(1,128)S(1)}, u32[]{:S(2)}, u32[]{:S(2)}) async-start(f32[4,1,512]{2,1,0:T(1,128)} %broadcast_in_dim.14), calls=%async_computation.2 | async-start | bytes 16384 | tf_op jit(solution)/shard_map/all_to_all | solution.py:31
  80.7 4.2 %all-to-all-done.2 = f32[4,1,512]{2,1,0:T(1,128)S(1)} async-done(((f32[4,1,512]{2,1,0:T(1,128)}), f32[4,1,512]{2,1,0:T(1,128)S(1)}, u32[]{:S(2)}, u32[]{:S(2)}) %all-to-all-start.2) | async-done | bytes 8224 | tf_op jit(solution)/shard_map/all_to_all | solution.py:31
  85.0 0.1 reshape_squeeze.8
  85.1 0.1 broadcast_divide_fusion
  85.2 0.7 copy.72
  (18 shorter events, 0.2 us)
Async XLA Ops:
  0.0 2.4 %copy-start = (s32[2048]{0:T(1024)S(1)}, s32[2048]{0:T(1024)}, u32[]{:S(2)}) copy-start(s32[2048]{0:T(1024)} %param.7) | copy-start | bytes 24580
  0.0 2.6 %copy-start.1 = (f32[8]{0:T(128)S(1)}, f32[8]{0:T(128)}, u32[]{:S(2)}) copy-start(f32[8]{0:T(128)} %param.6) | copy-start | bytes 100
  4.7 39.1 %all-to-all-start = ((bf16[128,9,128]{2,1,0:T(8,128)(2,1)}), bf16[128,9,128]{2,1,0:T(8,128)(2,1)}, u32[]{:S(2)}, u32[]{:S(2)}) async-start(bf16[128,9,128]{2,1,0:T(8,128)(2,1)} %copy.63), calls=%async_computation | async-start | bytes 1048576 | tf_op jit(solution)/shard_map/all_to_all | solution.py:78
  51.7 23.3 %all-to-all-start.1 = ((f32[128,1,528]{2,1,0:T(1,128)}), f32[128,1,528]{2,1,0:T(1,128)S(1)}, u32[]{:S(2)}, u32[]{:S(2)}) async-start(f32[128,1,528]{2,1,0:T(1,128)} %copy.67), calls=%async_computation.1 | async-start | bytes 655360 | tf_op jit(solution)/shard_map/all_to_all | solution.py:112
  76.7 8.2 %all-to-all-start.2 = ((f32[4,1,512]{2,1,0:T(1,128)}), f32[4,1,512]{2,1,0:T(1,128)S(1)}, u32[]{:S(2)}, u32[]{:S(2)}) async-start(f32[4,1,512]{2,1,0:T(1,128)} %broadcast_in_dim.14), calls=%async_computation.2 | async-start | bytes 16384 | tf_op jit(solution)/shard_map/all_to_all | solution.py:31

commit v13 on v12

--- a/solution.py
+++ b/solution.py
@@ -68,16 +68,17 @@
     sums = sums.reshape(local_chans, G * 8).T
     sums_hi = lax.reduce_precision(sums, exponent_bits=8, mantissa_bits=7)
     sums_lo = sums - sums_hi
-    pad = shard_cols - 2 * local_chans
-    extra_row = jnp.concatenate([
+    block = local_chans * shard_cols
+    pad = -(block + 2 * local_chans) % 128
+    payload = jnp.concatenate([
+        tapered.reshape(n_chan, block),
         sums_hi.astype(jnp.bfloat16),
         sums_lo.astype(jnp.bfloat16),
         jnp.zeros((n_chan, pad), jnp.bfloat16),
     ], axis=1)
-    payload = jnp.concatenate([tapered, extra_row[:, None, :]], axis=1)
-    got = lax.all_to_all(payload, "chan", 0, 0, tiled=True)
-    turned = got[:, :local_chans, :].reshape(channels, shard_cols)
-    col_parts = got[:, local_chans, :2 * local_chans].reshape(n_chan, 2, local_chans)
+    got = lax.all_to_all(payload.reshape(n_chan, 1, -1), "chan", 0, 0, tiled=True).reshape(n_chan, -1)
+    turned = got[:, :block].reshape(channels, shard_cols)
+    col_parts = got[:, block:block + 2 * local_chans].reshape(n_chan, 2, local_chans)
     col_parts = col_parts.transpose(0, 2, 1).reshape(channels, 2)
 
     cols = jnp.arange(shard_cols, dtype=jnp.int32)

time: 86.6 us -> 87.1 us (level)
  waiting for transfers between devices: 27.6 us -> 23.9 us
  starting transfers between devices: 29.6 us -> 32.8 us
  local copies, waits for them, and re-layouts: 9.59 us -> 10.8 us
  matrix products: 5.33 us -> 4.38 us
    all_to_all x0 -> x1, starting transfers between devices: none -> 18.4 us  [body(): lax.all_to_all(payload.reshape(n_chan, 1, -1), 'chan', 0, 0, tiled=True)]
    all_to_all x2 -> x1, starting transfers between devices: 25.6 us -> 10.4 us  [body(): got = lax.all_to_all(payload, 'chan', 0, 0, tiled=True)]
    all_to_all x2 -> x1, waiting for transfers between devices: 23.4 us -> 16.4 us  [body(): got = lax.all_to_all(payload, 'chan', 0, 0, tiled=True)]
    all_to_all x0 -> x1, waiting for transfers between devices: none -> 3.31 us  [body(): lax.all_to_all(payload.reshape(n_chan, 1, -1), 'chan', 0, 0, tiled=True)]
    unnamed x7 -> x8, local copies, waits for them, and re-layouts: 0.18 us -> 1.67 us
    concatenate x2 -> x1, local copies, waits for them, and re-layouts: 1.28 us -> 0.12 us  [body(): jnp.concatenate([tapered.reshape(n_chan, block), sums_hi.astype(jnp.bfloa...]
    dot_general x1, matrix products: 1.28 us -> 0.34 us  [body(): jnp.dot(turned, permute, preferred_element_type=jnp.float32)]
  transfers between devices with their start and end apart: 3 -> 3, of which waited for: 3 -> 3; matrix products, arithmetic and copies ran while one was open for 16% -> 15% of each run, Pallas kernels for 0% -> 0%
where the time goes in v13:
time: 87.1 us; the launch traced here: 86.3 us
  starting transfers between devices  32.8 us (38%)
  waiting for transfers between devices  23.9 us (27%)
  other arithmetic  14.1 us (16%)
  local copies, waits for them, and re-layouts  10.8 us (12%)
  matrix products  4.38 us (5%)
    all_to_all x1, starting transfers between devices, body(): lax.all_to_all(payload.reshape(n_chan, 1, -1), 'chan', 0, 0, tiled=True)  18.4 us
    all_to_all x1, waiting for transfers between devices, body(): got = lax.all_to_all(payload, 'chan', 0, 0, tiled=True)  16.4 us
    all_to_all x1, starting transfers between devices, body(): got = lax.all_to_all(payload, 'chan', 0, 0, tiled=True)  10.4 us
    convert_element_type x1, other arithmetic, tables(): ((ca * cb - sa * sb) * scale).astype(jnp.bfloat16).reshape(length, length)  6.51 us
    all_to_all x1, waiting for transfers between devices, tm_sum(): got = lax.all_to_all(flat, 'tm', 0, 0, tiled=True)[:, 0]  4.16 us
    all_to_all x1, starting transfers between devices, tm_sum(): got = lax.all_to_all(flat, 'tm', 0, 0, tiled=True)[:, 0]  4.01 us
    all_to_all x1, waiting for transfers between devices, body(): lax.all_to_all(payload.reshape(n_chan, 1, -1), 'chan', 0, 0, tiled=True)  3.31 us
    dot_general x1, matrix products, body(): sin_all = jnp.dot(sin_tab, rhs, preferred_element_type=jnp.float32)  2.34 us
  transfers between devices with their start and end apart: 3, of which 3 were waited for; matrix products, arithmetic and copies ran while one was open for 15% of the time, Pallas kernels for 0%

profile of v13, /device:TPU:1, one launch (start us, length us, event | category | flops | bytes accessed | tf_op | source)
XLA Modules:
  0.0 86.3 jit_solution(285491006681612100)
XLA Ops:
  0.0 0.9 subtract_convert_fusion
  0.9 0.2 convert_element_type.106
  1.1 1.0 %convert_bitcast_fusion = f32[1,8,128,128]{3,1,2,0:T(8,128)S(1)} fusion(bf16[1,8,16384]{2,1,0:T(8,128)(2,1)} %param.4), kind=kLoop, calls=%fused_computation.23 | loop fusion | flops 131072 | bytes 786432
  2.1 0.1 copy.115
  2.2 0.2 copy.81
  2.4 0.3 fusion.8
  2.7 0.1 copy.85
  2.9 0.1 eq.88
  3.0 0.2 convolution_bitcast_fusion
  3.2 0.1 copy.84
  3.3 0.1 reshape.284
  3.4 0.1 copy.86
  3.5 0.1 copy.87
  3.7 0.1 concatenate.9
  3.8 0.5 broadcast.326
  4.3 0.8 reduce.12
  5.1 1.1 %reshape.314 = bf16[128,2,576]{2,1,0:T(2,128)(2,1)} reshape(bf16[128,1152]{1,0:T(8,128)(2,1)S(1)} %reduce.12) | data formatting | bytes 589824
  6.1 18.4 %all-to-all-start = ((bf16[128,2,576]{2,1,0:T(2,128)(2,1)}), bf16[128,2,576]{2,1,0:T(2,128)(2,1)S(1)}, u32[]{:S(2)}, u32[]{:S(2)}) async-start(bf16[128,2,576]{2,1,0:T(2,128)(2,1)} %reshape.314), calls=%async_computation | async-start | bytes 655360 | tf_op jit(solution)/shard_map/all_to_all | solution.py:79
  24.6 1.9 %fusion.22 = f32[1024,128]{1,0:T(8,128)S(1)} fusion(), kind=kLoop, calls=%fused_computation.41 | loop fusion | flops 1835008 | bytes 524288 | tf_op jit(solution)/shard_map/sin | solution.py:22
  26.5 1.9 %fusion.23 = f32[1024,128]{1,0:T(8,128)S(1)} fusion(), kind=kLoop, calls=%fused_computation.42 | loop fusion | flops 1835008 | bytes 524288 | tf_op jit(solution)/shard_map/cos | solution.py:22
  28.4 0.2 fusion.40
  28.7 0.1 dynamic_slice.3
  28.7 0.1 fusion.43
  28.8 0.1 multiply_convert_fusion.2
  28.9 1.0 %copy.80 = f32[1024,8]{1,0:T(8,128)} copy(f32[1024,8]{0,1:T(8,128)S(1)} %get-tuple-element.10) | data formatting | bytes 65536 | tf_op jit(solution)/shard_map/sin | solution.py:21
  29.9 1.0 %copy.79 = f32[1024,8]{1,0:T(8,128)} copy(f32[1024,8]{0,1:T(8,128)S(1)} %get-tuple-element.9) | data formatting | bytes 65536 | tf_op jit(solution)/shard_map/cos | solution.py:21
  31.0 0.2 convert_element_type.117
  31.2 0.1 pad.5.clone
  31.3 6.5 %multiply_convert_fusion.1 = (bf16[1024,8,128]{2,1,0:T(8,128)(2,1)S(1)}, bf16[1024,8,128]{2,1,0:T(8,128)(2,1)}) fusion(f32[1024,128]{1,0:T(8,128)S(1)} %fusion.22, f32[1024,8]{1,0:T(8,128)} %copy.80, f32[1024,128]{1,0:T(8,128)S(1)} %fusion.23, f32[1024,8]{1,0:T(8,128)} %copy.79), kind=kLoop, calls=%fused_computation.1 | loop fusion | flops 10485760 | bytes 5308416 | tf_op jit(solution)/shard_map/convert_element_type | solution.py:24
  37.8 3.3 %all-to-all-done = bf16[128,2,576]{2,1,0:T(2,128)(2,1)S(1)} async-done(((bf16[128,2,576]{2,1,0:T(2,128)(2,1)}), bf16[128,2,576]{2,1,0:T(2,128)(2,1)S(1)}, u32[]{:S(2)}, u32[]{:S(2)}) %all-to-all-start) | async-done | bytes 294944 | tf_op jit(solution)/shard_map/all_to_all | solution.py:79
  41.1 0.5 reshape.315
  41.6 0.7 copy.89
  42.3 0.1 copy.91
  42.5 0.1 reshape.289
  42.6 0.1 copy.90
  42.8 0.1 reshape.287
  42.9 0.3 convolution_convert_fusion
  43.2 2.3 %fusion = f32[1024,256]{0,1:T(8,128)S(1)} fusion(bf16[128,8,8,128]{3,2,1,0:T(8,128)(2,1)} %bitcast.68, bf16[1024,2]{0,1:T(2,128)(2,1)S(1)} %reshape.289, bf16[1024,128]{0,1:T(8,128)(2,1)S(1)} %convolution_convert_fusion, bf16[256]{0:T(256)(128)(2,1)S(1)} %pad.5.clone), kind=kOutput, calls=%fused_computation.2 | convolution fusion | flops 538443776 | bytes 3412480 | tf_op jit(solution)/shard_map/dot_general | solution.py:92
  45.6 0.7 fusion.3
  46.4 0.1 add.122
  46.5 0.1 add.120
  46.6 0.2 fusion.25
  46.8 0.2 convolution_add_fusion
  47.1 0.2 copy.92
  47.3 0.1 reshape.290
  47.4 0.1 maximum_bitcast_fusion
  47.5 1.0 %copy.93 = f32[128,1,528]{2,1,0:T(1,128)} copy(f32[128,1,528]{2,0,1:T(8,128)S(1)} %maximum_bitcast_fusion) | data formatting | bytes 540672 | tf_op jit(solution)/shard_map/all_to_all | solution.py:113
  48.6 10.4 %all-to-all-start.1 = ((f32[128,1,528]{2,1,0:T(1,128)}), f32[128,1,528]{2,1,0:T(1,128)S(1)}, u32[]{:S(2)}, u32[]{:S(2)}) async-start(f32[128,1,528]{2,1,0:T(1,128)} %copy.93), calls=%async_computation.1 | async-start | bytes 655360 | tf_op jit(solution)/shard_map/all_to_all | solution.py:113
  59.0 0.1 convert_reduce_fusion
  59.1 16.4 %all-to-all-done.1 = f32[128,1,528]{2,1,0:T(1,128)S(1)} async-done(((f32[128,1,528]{2,1,0:T(1,128)}), f32[128,1,528]{2,1,0:T(1,128)S(1)}, u32[]{:S(2)}, u32[]{:S(2)}) %all-to-all-start.1) | async-done | bytes 270368 | tf_op jit(solution)/shard_map/all_to_all | solution.py:113
  75.5 0.2 copy.94
  75.7 0.1 slice_reduce_fusion
  75.9 0.1 copy.95
  76.0 0.1 reshape.291
  76.1 0.1 fusion.33
  76.2 0.1 reshape.292
  76.3 0.2 copy.96
  76.5 0.1 broadcast_in_dim.10
  76.6 0.6 broadcast_in_dim.11
  77.2 4.0 %all-to-all-start.2 = ((f32[4,1,512]{2,1,0:T(1,128)}), f32[4,1,512]{2,1,0:T(1,128)S(1)}, u32[]{:S(2)}, u32[]{:S(2)}) async-start(f32[4,1,512]{2,1,0:T(1,128)} %broadcast_in_dim.11), calls=%async_computation.2 | async-start | bytes 16384 | tf_op jit(solution)/shard_map/all_to_all | solution.py:31
  81.2 4.2 %all-to-all-done.2 = f32[4,1,512]{2,1,0:T(1,128)S(1)} async-done(((f32[4,1,512]{2,1,0:T(1,128)}), f32[4,1,512]{2,1,0:T(1,128)S(1)}, u32[]{:S(2)}, u32[]{:S(2)}) %all-to-all-start.2) | async-done | bytes 8224 | tf_op jit(solution)/shard_map/all_to_all | solution.py:31
  85.5 0.1 reshape_squeeze.4
  85.6 0.1 broadcast_divide_fusion
  85.6 0.7 copy.98
  (25 shorter events, 0.3 us)
Async XLA Ops:
  0.0 2.4 %copy-start.1 = (f32[8]{0:T(128)S(1)}, f32[8]{0:T(128)}, u32[]{:S(2)}) copy-start(f32[8]{0:T(128)} %param.6) | copy-start | bytes 100
  1.1 1.8 %copy-start = (s32[2048]{0:T(1024)S(1)}, s32[2048]{0:T(1024)}, u32[]{:S(2)}) copy-start(s32[2048]{0:T(1024)} %param.7) | copy-start | bytes 24580
  6.1 35.0 %all-to-all-start = ((bf16[128,2,576]{2,1,0:T(2,128)(2,1)}), bf16[128,2,576]{2,1,0:T(2,128)(2,1)S(1)}, u32[]{:S(2)}, u32[]{:S(2)}) async-start(bf16[128,2,576]{2,1,0:T(2,128)(2,1)} %reshape.314), calls=%async_computation | async-start | bytes 655360 | tf_op jit(solution)/shard_map/all_to_all | solution.py:79
  48.6 27.0 %all-to-all-start.1 = ((f32[128,1,528]{2,1,0:T(1,128)}), f32[128,1,528]{2,1,0:T(1,128)S(1)}, u32[]{:S(2)}, u32[]{:S(2)}) async-start(f32[128,1,528]{2,1,0:T(1,128)} %copy.93), calls=%async_computation.1 | async-start | bytes 655360 | tf_op jit(solution)/shard_map/all_to_all | solution.py:113
  77.2 8.2 %all-to-all-start.2 = ((f32[4,1,512]{2,1,0:T(1,128)}), f32[4,1,512]{2,1,0:T(1,128)S(1)}, u32[]{:S(2)}, u32[]{:S(2)}) async-start(f32[4,1,512]{2,1,0:T(1,128)} %broadcast_in_dim.11), calls=%async_computation.2 | async-start | bytes 16384 | tf_op jit(solution)/shard_map/all_to_all | solution.py:31

commit v14 on v12

--- a/solution.py
+++ b/solution.py
@@ -54,16 +54,21 @@
     shard_cols = shard_bl * 8
     times_all = lax.axis_size("tm")
 
+    half = shard_cols // 2
+    cols = jnp.arange(shard_cols, dtype=jnp.int32)
+    target = (cols % 2) * half + cols // 2
+    permute = (target[:, None] == cols[None, :]).astype(jnp.bfloat16)
     keep = (1 - flags[0]).astype(jnp.bfloat16).reshape(local_chans, n_chan, shard_bl)
-    spread = (jnp.arange(shard_cols, dtype=jnp.int32)[None, :] // 8
+    spread = ((cols[None, :] % half) // 4
               == jnp.arange(shard_bl, dtype=jnp.int32)[:, None]).astype(jnp.bfloat16)
     keep_cols = jnp.einsum("cjb,bl->jcl", keep, spread, preferred_element_type=jnp.float32)
     shaped = visibilities[0].reshape(local_chans, n_chan, shard_cols).transpose(1, 0, 2)
-    tapered = (shaped.astype(jnp.float32) * (keep_cols * taper[None, :, None])).astype(jnp.bfloat16)
+    shaped = jnp.dot(shaped, permute, preferred_element_type=jnp.float32)
+    tapered = (shaped * (keep_cols * taper[None, :, None])).astype(jnp.bfloat16)
 
     member_full = (group_ids[:, None] == jnp.arange(G, dtype=jnp.int32)[None, :]).astype(jnp.bfloat16)
     member_full = member_full.reshape(n_chan, shard_bl, G)
-    sums = jnp.einsum("jcbk,jbg->cgk", tapered.reshape(n_chan, local_chans, shard_bl, 8), member_full,
+    sums = jnp.einsum("jcrbs,jbg->cgsr", tapered.reshape(n_chan, local_chans, 2, shard_bl, 4), member_full,
                       preferred_element_type=jnp.float32)
     sums = sums.reshape(local_chans, G * 8).T
     sums_hi = lax.reduce_precision(sums, exponent_bits=8, mantissa_bits=7)
@@ -80,10 +85,6 @@
     col_parts = got[:, local_chans, :2 * local_chans].reshape(n_chan, 2, local_chans)
     col_parts = col_parts.transpose(0, 2, 1).reshape(channels, 2)
 
-    cols = jnp.arange(shard_cols, dtype=jnp.int32)
-    target = (cols % 2) * (shard_cols // 2) + cols // 2
-    permute = (target[:, None] == cols[None, :]).astype(jnp.bfloat16)
-    turned = jnp.dot(turned, permute, preferred_element_type=jnp.float32).astype(jnp.bfloat16)
     extra = 128 - col_parts.shape[1]
     rhs = jnp.concatenate([turned, col_parts, jnp.zeros((channels, extra), jnp.bfloat16)], axis=1)
     cos_tab, sin_tab = tables(channels, 128)
@@ -98,7 +99,6 @@
     member = (shard_groups[:, None] == jnp.arange(G, dtype=jnp.int32)[None, :]).astype(jnp.float32)
     eye_s = jnp.eye(4, dtype=jnp.float32)
     m_pow = (member[:, None, :, None] * eye_s[None, :, None, :]).reshape(shard_bl * 4, G * 4)
-    half = shard_cols // 2
     real_part = cos_part[:, :half] + sin_part[:, half:]
     imag_part = cos_part[:, half:] - sin_part[:, :half]
     auto = split_dot(real_part * real_part + imag_part * imag_part, m_pow)

time: 86.6 us -> 87.6 us (1.012)
  local copies, waits for them, and re-layouts: 9.59 us -> 10.9 us
  other arithmetic: 13.4 us -> 12.4 us
    unnamed x1 -> x0, other arithmetic: 0.99 us -> none
    reshape x0 -> x1, local copies, waits for them, and re-layouts: none -> 0.97 us  [body(): turned = got[:, :local_chans, :].reshape(channels, shard_cols)]
  transfers between devices with their start and end apart: 3 -> 3, of which waited for: 3 -> 3; matrix products, arithmetic and copies ran while one was open for 16% -> 15% of each run, Pallas kernels for 0% -> 0%
where the time goes in v14:
time: 87.6 us; the launch traced here: 86.8 us
  starting transfers between devices  29.6 us (34%)
  waiting for transfers between devices  27.6 us (32%)
  other arithmetic  12.4 us (14%)
  local copies, waits for them, and re-layouts  10.9 us (12%)
  matrix products  5.94 us (7%)
    all_to_all x2, starting transfers between devices, body(): got = lax.all_to_all(payload, 'chan', 0, 0, tiled=True)  25.6 us
    all_to_all x2, waiting for transfers between devices, body(): got = lax.all_to_all(payload, 'chan', 0, 0, tiled=True)  23.4 us
    convert_element_type x1, other arithmetic, tables(): ((ca * cb - sa * sb) * scale).astype(jnp.bfloat16).reshape(length, length)  6.51 us
    all_to_all x1, waiting for transfers between devices, tm_sum(): got = lax.all_to_all(flat, 'tm', 0, 0, tiled=True)[:, 0]  4.16 us
    all_to_all x1, starting transfers between devices, tm_sum(): got = lax.all_to_all(flat, 'tm', 0, 0, tiled=True)[:, 0]  4.01 us
    dot_general x1, matrix products, body(): sin_all = jnp.dot(sin_tab, rhs, preferred_element_type=jnp.float32)  2.35 us
    sin x1, other arithmetic, tables(): cb, sb = (jnp.cos(pb)[:, None, :], jnp.sin(pb)[:, None, :])  1.93 us
    cos x1, other arithmetic, tables(): cb, sb = (jnp.cos(pb)[:, None, :], jnp.sin(pb)[:, None, :])  1.91 us
  transfers between devices with their start and end apart: 3, of which 3 were waited for; matrix products, arithmetic and copies ran while one was open for 15% of the time, Pallas kernels for 0%

profile of v14, /device:TPU:1, one launch (start us, length us, event | category | flops | bytes accessed | tf_op | source)
XLA Modules:
  0.0 86.8 jit_solution(15740814210099788894)
XLA Ops:
  0.0 0.9 subtract_convert_fusion
  0.9 0.2 convert_element_type.91
  1.1 0.8 eq.93
  1.9 0.1 copy.74
  1.9 0.9 %fusion.6 = f32[128,8,128]{0,2,1:T(8,128)S(1)} fusion(bf16[8,128,16]{2,1,0:T(8,128)(2,1)S(1)} %convert_element_type.91, f32[8]{0:T(128)} %param.6, s32[128]{0:T(128)S(1)} %and_select_fusion), kind=kOutput, calls=%fused_computation.9 | convolution fusion | flops 4329472 | bytes 557600 | tf_op jit(solution)/shard_map/cjb,bl->jcl/dot_general | solution.py:64
  2.9 1.2 %fusion.8 = bf16[128,8,128]{0,2,1:T(8,128)(2,1)S(1)} fusion(f32[128,8,128]{0,2,1:T(8,128)S(1)} %fusion.6, bf16[8,128,128]{2,0,1:T(8,128)(2,1)} %bitcast.75, s32[128]{0:T(128)S(1)} %fusion.56), kind=kOutput, calls=%fused_computation.12 | convolution fusion | flops 33832960 | bytes 1049088 | tf_op jit(solution)/shard_map/dot_general | solution.py:66
  4.1 0.0 copy-start
  4.1 0.3 convolution_bitcast_fusion.1
  4.4 0.1 copy.76
  4.5 0.1 pad.10.clone
  4.6 0.1 maximum_bitcast_fusion.1
  4.8 1.2 %copy.78 = bf16[128,9,128]{2,1,0:T(8,128)(2,1)} copy(bf16[128,9,128]{0,2,1:T(8,128)(2,1)S(1)} %pad_maximum_fusion) | data formatting | bytes 589824 | tf_op jit(solution)/shard_map/concatenate | solution.py:82
  6.0 18.9 %all-to-all-start = ((bf16[128,9,128]{2,1,0:T(8,128)(2,1)}), bf16[128,9,128]{2,1,0:T(8,128)(2,1)}, u32[]{:S(2)}, u32[]{:S(2)}) async-start(bf16[128,9,128]{2,1,0:T(8,128)(2,1)} %copy.78), calls=%async_computation | async-start | bytes 1048576 | tf_op jit(solution)/shard_map/all_to_all | solution.py:83
  24.8 1.9 %fusion.24 = f32[1024,128]{1,0:T(8,128)S(1)} fusion(), kind=kLoop, calls=%fused_computation.43 | loop fusion | flops 1835008 | bytes 524288 | tf_op jit(solution)/shard_map/sin | solution.py:22
  26.8 0.2 fusion.44
  27.0 0.0 copy-done
  27.0 0.1 dynamic_slice.3
  27.1 0.1 fusion.47
  27.2 0.1 multiply_convert_fusion.2
  27.3 1.9 %fusion.25 = f32[1024,128]{1,0:T(8,128)S(1)} fusion(), kind=kLoop, calls=%fused_computation.44 | loop fusion | flops 1835008 | bytes 524288 | tf_op jit(solution)/shard_map/cos | solution.py:22
  29.2 1.0 %copy.71 = f32[1024,8]{1,0:T(8,128)} copy(f32[1024,8]{0,1:T(8,128)S(1)} %get-tuple-element.10) | data formatting | bytes 65536 | tf_op jit(solution)/shard_map/sin | solution.py:21
  30.2 1.0 %copy.70 = f32[1024,8]{1,0:T(8,128)} copy(f32[1024,8]{0,1:T(8,128)S(1)} %get-tuple-element.9) | data formatting | bytes 65536 | tf_op jit(solution)/shard_map/cos | solution.py:21
  31.2 0.1 pad.5.clone
  31.3 0.2 convert_element_type.101
  31.6 6.5 %multiply_convert_fusion.1 = (bf16[1024,8,128]{2,1,0:T(8,128)(2,1)S(1)}, bf16[1024,8,128]{2,1,0:T(8,128)(2,1)}) fusion(f32[1024,128]{1,0:T(8,128)S(1)} %fusion.24, f32[1024,8]{1,0:T(8,128)} %copy.71, f32[1024,128]{1,0:T(8,128)S(1)} %fusion.25, f32[1024,8]{1,0:T(8,128)} %copy.70), kind=kLoop, calls=%fused_computation.1 | loop fusion | flops 10485760 | bytes 5308416 | tf_op jit(solution)/shard_map/convert_element_type | solution.py:24
  38.1 7.0 %all-to-all-done = bf16[128,9,128]{2,1,0:T(8,128)(2,1)} async-done(((bf16[128,9,128]{2,1,0:T(8,128)(2,1)}), bf16[128,9,128]{2,1,0:T(8,128)(2,1)}, u32[]{:S(2)}, u32[]{:S(2)}) %all-to-all-start) | async-done | bytes 294944 | tf_op jit(solution)/shard_map/all_to_all | solution.py:83
  45.0 1.0 %slice.89 = bf16[128,1,16]{2,1,0:T(2,128)(2,1)S(1)} slice(bf16[128,9,128]{2,1,0:T(8,128)(2,1)} %all-to-all-done), slice={[0:128], [8:9], [0:16]} | slice | bytes 8192 | tf_op jit(solution)/shard_map/slice | solution.py:85
  46.0 0.1 copy.95
  46.1 0.2 copy.92
  46.4 1.0 %slice_bitcast_fusion = bf16[1024,128]{1,0:T(8,128)(2,1)S(1)} fusion(bf16[128,9,128]{2,1,0:T(8,128)(2,1)} %all-to-all-done), kind=kLoop, calls=%fused_computation.37 | loop fusion | bytes 524288 | tf_op jit(solution)/shard_map/reshape | solution.py:84
  47.3 2.3 %fusion = f32[1024,256]{0,1:T(8,128)S(1)} fusion(bf16[128,8,8,128]{3,2,1,0:T(8,128)(2,1)} %bitcast.67, bf16[1024,2]{1,0:T(8,128)(2,1)S(1)} %bitcast.72, bf16[1024,128]{1,0:T(8,128)(2,1)S(1)} %slice_bitcast_fusion, bf16[256]{0:T(256)(128)(2,1)S(1)} %pad.5.clone), kind=kOutput, calls=%fused_computation.2 | convolution fusion | flops 538443776 | bytes 3412480 | tf_op jit(solution)/shard_map/dot_general | solution.py:92
  49.7 0.8 fusion.3
  50.5 0.1 fusion.17
  50.6 0.1 add.134
  50.6 0.1 add.132
  50.7 0.2 fusion.27
  51.0 0.2 convolution_add_fusion
  51.2 0.2 copy.82
  51.4 0.1 reshape.283
  51.5 0.1 maximum_bitcast_fusion
  51.6 1.0 %copy.83 = f32[128,1,528]{2,1,0:T(1,128)} copy(f32[128,1,528]{2,0,1:T(8,128)S(1)} %maximum_bitcast_fusion) | data formatting | bytes 540672 | tf_op jit(solution)/shard_map/all_to_all | solution.py:112
  52.7 6.8 %all-to-all-start.1 = ((f32[128,1,528]{2,1,0:T(1,128)}), f32[128,1,528]{2,1,0:T(1,128)S(1)}, u32[]{:S(2)}, u32[]{:S(2)}) async-start(f32[128,1,528]{2,1,0:T(1,128)} %copy.83), calls=%async_computation.1 | async-start | bytes 655360 | tf_op jit(solution)/shard_map/all_to_all | solution.py:112
  59.4 0.1 convert_reduce_fusion
  59.6 16.4 %all-to-all-done.1 = f32[128,1,528]{2,1,0:T(1,128)S(1)} async-done(((f32[128,1,528]{2,1,0:T(1,128)}), f32[128,1,528]{2,1,0:T(1,128)S(1)}, u32[]{:S(2)}, u32[]{:S(2)}) %all-to-all-start.1) | async-done | bytes 270368 | tf_op jit(solution)/shard_map/all_to_all | solution.py:112
  76.0 0.2 copy.84
  76.2 0.1 slice_reduce_fusion
  76.3 0.1 copy.85
  76.4 0.1 reshape.284
  76.5 0.1 fusion.37
  76.6 0.1 reshape.285
  76.7 0.2 copy.86
  77.0 0.1 broadcast_in_dim.13
  77.0 0.6 broadcast_in_dim.14
  77.7 4.0 %all-to-all-start.2 = ((f32[4,1,512]{2,1,0:T(1,128)}), f32[4,1,512]{2,1,0:T(1,128)S(1)}, u32[]{:S(2)}, u32[]{:S(2)}) async-start(f32[4,1,512]{2,1,0:T(1,128)} %broadcast_in_dim.14), calls=%async_computation.2 | async-start | bytes 16384 | tf_op jit(solution)/shard_map/all_to_all | solution.py:31
  81.7 4.2 %all-to-all-done.2 = f32[4,1,512]{2,1,0:T(1,128)S(1)} async-done(((f32[4,1,512]{2,1,0:T(1,128)}), f32[4,1,512]{2,1,0:T(1,128)S(1)}, u32[]{:S(2)}, u32[]{:S(2)}) %all-to-all-start.2) | async-done | bytes 8224 | tf_op jit(solution)/shard_map/all_to_all | solution.py:31
  85.9 0.1 reshape_squeeze.11
  86.0 0.1 broadcast_divide_fusion
  86.1 0.7 copy.88
  (19 shorter events, 0.3 us)
Async XLA Ops:
  4.1 22.9 %copy-start = (s32[2048]{0:T(1024)S(1)}, s32[2048]{0:T(1024)}, u32[]{:S(2)}) copy-start(s32[2048]{0:T(1024)} %param.7) | copy-start | bytes 24580
  6.0 39.1 %all-to-all-start = ((bf16[128,9,128]{2,1,0:T(8,128)(2,1)}), bf16[128,9,128]{2,1,0:T(8,128)(2,1)}, u32[]{:S(2)}, u32[]{:S(2)}) async-start(bf16[128,9,128]{2,1,0:T(8,128)(2,1)} %copy.78), calls=%async_computation | async-start | bytes 1048576 | tf_op jit(solution)/shard_map/all_to_all | solution.py:83
  52.7 23.3 %all-to-all-start.1 = ((f32[128,1,528]{2,1,0:T(1,128)}), f32[128,1,528]{2,1,0:T(1,128)S(1)}, u32[]{:S(2)}, u32[]{:S(2)}) async-start(f32[128,1,528]{2,1,0:T(1,128)} %copy.83), calls=%async_computation.1 | async-start | bytes 655360 | tf_op jit(solution)/shard_map/all_to_all | solution.py:112
  77.7 8.2 %all-to-all-start.2 = ((f32[4,1,512]{2,1,0:T(1,128)}), f32[4,1,512]{2,1,0:T(1,128)S(1)}, u32[]{:S(2)}, u32[]{:S(2)}) async-start(f32[4,1,512]{2,1,0:T(1,128)} %broadcast_in_dim.14), calls=%async_computation.2 | async-start | bytes 16384 | tf_op jit(solution)/shard_map/all_to_all | solution.py:31

commit v15 on v12

--- a/solution.py
+++ b/solution.py
@@ -84,8 +84,7 @@
     target = (cols % 2) * (shard_cols // 2) + cols // 2
     permute = (target[:, None] == cols[None, :]).astype(jnp.bfloat16)
     turned = jnp.dot(turned, permute, preferred_element_type=jnp.float32).astype(jnp.bfloat16)
-    extra = 128 - col_parts.shape[1]
-    rhs = jnp.concatenate([turned, col_parts, jnp.zeros((channels, extra), jnp.bfloat16)], axis=1)
+    rhs = jnp.concatenate([turned, col_parts], axis=1)
     cos_tab, sin_tab = tables(channels, 128)
     cos_all = jnp.dot(cos_tab, rhs, preferred_element_type=jnp.float32)
     sin_all = jnp.dot(sin_tab, rhs, preferred_element_type=jnp.float32)

time: 86.6 us -> 86.7 us (level)
  transfers between devices with their start and end apart: 3 -> 3, of which waited for: 3 -> 3; matrix products, arithmetic and copies ran while one was open for 16% -> 15% of each run, Pallas kernels for 0% -> 0%
where the time goes in v15:
time: 86.7 us; the launch traced here: 85.9 us
  starting transfers between devices  29.6 us (34%)
  waiting for transfers between devices  27.6 us (32%)
  other arithmetic  13.4 us (15%)
  local copies, waits for them, and re-layouts  9.51 us (11%)
  matrix products  5.49 us (6%)
    all_to_all x2, starting transfers between devices, body(): got = lax.all_to_all(payload, 'chan', 0, 0, tiled=True)  25.5 us
    all_to_all x2, waiting for transfers between devices, body(): got = lax.all_to_all(payload, 'chan', 0, 0, tiled=True)  23.5 us
    convert_element_type x1, other arithmetic, tables(): ((ca * cb - sa * sb) * scale).astype(jnp.bfloat16).reshape(length, length)  6.51 us
    all_to_all x1, waiting for transfers between devices, tm_sum(): got = lax.all_to_all(flat, 'tm', 0, 0, tiled=True)[:, 0]  4.16 us
    all_to_all x1, starting transfers between devices, tm_sum(): got = lax.all_to_all(flat, 'tm', 0, 0, tiled=True)[:, 0]  4.01 us
    dot_general x1, matrix products, body(): sin_all = jnp.dot(sin_tab, rhs, preferred_element_type=jnp.float32)  2.43 us
    sin x1, other arithmetic, tables(): cb, sb = (jnp.cos(pb)[:, None, :], jnp.sin(pb)[:, None, :])  1.93 us
    cos x1, other arithmetic, tables(): cb, sb = (jnp.cos(pb)[:, None, :], jnp.sin(pb)[:, None, :])  1.91 us
  transfers between devices with their start and end apart: 3, of which 3 were waited for; matrix products, arithmetic and copies ran while one was open for 15% of the time, Pallas kernels for 0%

profile of v15, /device:TPU:1, one launch (start us, length us, event | category | flops | bytes accessed | tf_op | source)
XLA Modules:
  0.0 85.9 jit_solution(14369729622616095449)
XLA Ops:
  0.0 0.0 copy-start
  0.0 0.0 copy-start.1
  0.0 0.9 %subtract_convert_fusion = bf16[1,8,2048]{2,1,0:T(8,128)(2,1)S(1)} fusion(s32[1,8,2048]{2,1,0:T(8,128)} %param.5), kind=kLoop, calls=%fused_computation.50 | loop fusion | flops 32768 | bytes 98304 | tf_op jit(solution)/shard_map/convert_element_type | solution.py:57
  0.9 0.2 convert_element_type.106
  1.1 1.0 %convert_bitcast_fusion = f32[1,8,128,128]{3,1,2,0:T(8,128)S(1)} fusion(bf16[1,8,16384]{2,1,0:T(8,128)(2,1)} %param.4), kind=kLoop, calls=%fused_computation.22 | loop fusion | flops 131072 | bytes 786432
  2.1 0.1 copy.90
  2.2 0.2 copy.59
  2.4 0.0 copy-done
  2.4 0.1 eq.88
  2.5 0.1 copy.61
  2.6 0.0 copy-done.1
  2.6 0.3 fusion.8
  2.9 0.2 convolution_bitcast_fusion
  3.1 0.1 copy.62
  3.1 0.1 reshape.271
  3.3 0.1 pad.9.clone
  3.3 0.1 maximum_bitcast_fusion.1
  3.5 1.2 %copy.63 = bf16[128,9,128]{2,1,0:T(8,128)(2,1)} copy(bf16[128,9,128]{0,2,1:T(8,128)(2,1)S(1)} %pad_maximum_fusion) | data formatting | bytes 589824 | tf_op jit(solution)/shard_map/concatenate | solution.py:77
  4.7 18.9 %all-to-all-start = ((bf16[128,9,128]{2,1,0:T(8,128)(2,1)}), bf16[128,9,128]{2,1,0:T(8,128)(2,1)}, u32[]{:S(2)}, u32[]{:S(2)}) async-start(bf16[128,9,128]{2,1,0:T(8,128)(2,1)} %copy.63), calls=%async_computation | async-start | bytes 1048576 | tf_op jit(solution)/shard_map/all_to_all | solution.py:78
  23.6 1.9 %fusion.20 = f32[1024,128]{1,0:T(8,128)S(1)} fusion(), kind=kLoop, calls=%fused_computation.41 | loop fusion | flops 1835008 | bytes 524288 | tf_op jit(solution)/shard_map/sin | solution.py:22
  25.5 1.9 %fusion.21 = f32[1024,128]{1,0:T(8,128)S(1)} fusion(), kind=kLoop, calls=%fused_computation.42 | loop fusion | flops 1835008 | bytes 524288 | tf_op jit(solution)/shard_map/cos | solution.py:22
  27.4 0.2 fusion.38
  27.6 0.1 dynamic_slice.3
  27.7 0.1 fusion.41
  27.8 0.1 multiply_convert_fusion.2
  27.9 1.0 %copy.58 = f32[1024,8]{1,0:T(8,128)} copy(f32[1024,8]{0,1:T(8,128)S(1)} %get-tuple-element.10) | data formatting | bytes 65536 | tf_op jit(solution)/shard_map/sin | solution.py:21
  28.9 1.0 %copy.57 = f32[1024,8]{1,0:T(8,128)} copy(f32[1024,8]{0,1:T(8,128)S(1)} %get-tuple-element.9) | data formatting | bytes 65536 | tf_op jit(solution)/shard_map/cos | solution.py:21
  29.9 0.2 convert_element_type.117
  30.2 6.5 %multiply_convert_fusion.1 = (bf16[1024,8,128]{2,1,0:T(8,128)(2,1)S(1)}, bf16[1024,8,128]{2,1,0:T(8,128)(2,1)}) fusion(f32[1024,128]{1,0:T(8,128)S(1)} %fusion.20, f32[1024,8]{1,0:T(8,128)} %copy.58, f32[1024,128]{1,0:T(8,128)S(1)} %fusion.21, f32[1024,8]{1,0:T(8,128)} %copy.57), kind=kLoop, calls=%fused_computation.1 | loop fusion | flops 10485760 | bytes 5308416 | tf_op jit(solution)/shard_map/convert_element_type | solution.py:24
  36.7 7.1 %all-to-all-done = bf16[128,9,128]{2,1,0:T(8,128)(2,1)} async-done(((bf16[128,9,128]{2,1,0:T(8,128)(2,1)}), bf16[128,9,128]{2,1,0:T(8,128)(2,1)}, u32[]{:S(2)}, u32[]{:S(2)}) %all-to-all-start) | async-done | bytes 294944 | tf_op jit(solution)/shard_map/all_to_all | solution.py:78
  43.8 1.0 %slice.89 = bf16[128,1,16]{2,1,0:T(2,128)(2,1)S(1)} slice(bf16[128,9,128]{2,1,0:T(8,128)(2,1)} %all-to-all-done), slice={[0:128], [8:9], [0:16]} | slice | bytes 8192 | tf_op jit(solution)/shard_map/slice | solution.py:80
  44.8 0.1 copy.76
  44.8 0.1 copy.65
  45.0 0.1 reshape.273
  45.1 1.3 %convolution_convert_fusion = bf16[1024,128]{0,1:T(8,128)(2,1)S(1)} fusion(bf16[128,9,128]{2,1,0:T(8,128)(2,1)} %all-to-all-done, s32[128]{0:T(128)S(1)} %fusion.50), kind=kOutput, calls=%fused_computation.12 | convolution fusion | flops 33701888 | bytes 524800 | tf_op jit(solution)/shard_map/dot_general | solution.py:86
  46.4 2.4 %fusion = f32[1024,130]{0,1:T(8,128)S(1)} fusion(bf16[128,8,8,128]{3,2,1,0:T(8,128)(2,1)} %bitcast.67, bf16[1024,2]{0,1:T(2,128)(2,1)S(1)} %reshape.273, bf16[1024,128]{0,1:T(8,128)(2,1)S(1)} %convolution_convert_fusion), kind=kOutput, calls=%fused_computation.2 | convolution fusion | flops 273162240 | bytes 2895872 | tf_op jit(solution)/shard_map/dot_general | solution.py:90
  48.8 0.8 fusion.3
  49.7 0.1 fusion.17
  49.8 0.1 add.122
  49.9 0.1 add.120
  49.9 0.2 fusion.23
  50.2 0.2 convolution_add_fusion
  50.4 0.2 copy.66
  50.6 0.1 reshape.274
  50.8 0.1 maximum_bitcast_fusion
  50.8 1.0 %copy.67 = f32[128,1,528]{2,1,0:T(1,128)} copy(f32[128,1,528]{2,0,1:T(8,128)S(1)} %maximum_bitcast_fusion) | data formatting | bytes 540672 | tf_op jit(solution)/shard_map/all_to_all | solution.py:111
  51.9 6.7 %all-to-all-start.1 = ((f32[128,1,528]{2,1,0:T(1,128)}), f32[128,1,528]{2,1,0:T(1,128)S(1)}, u32[]{:S(2)}, u32[]{:S(2)}) async-start(f32[128,1,528]{2,1,0:T(1,128)} %copy.67), calls=%async_computation.1 | async-start | bytes 655360 | tf_op jit(solution)/shard_map/all_to_all | solution.py:111
  58.6 0.1 convert_reduce_fusion
  58.7 16.4 %all-to-all-done.1 = f32[128,1,528]{2,1,0:T(1,128)S(1)} async-done(((f32[128,1,528]{2,1,0:T(1,128)}), f32[128,1,528]{2,1,0:T(1,128)S(1)}, u32[]{:S(2)}, u32[]{:S(2)}) %all-to-all-start.1) | async-done | bytes 270368 | tf_op jit(solution)/shard_map/all_to_all | solution.py:111
  75.1 0.2 copy.68
  75.3 0.1 slice_reduce_fusion
  75.4 0.1 copy.69
  75.5 0.1 reshape.275
  75.7 0.1 fusion.31
  75.8 0.1 reshape.276
  75.9 0.2 copy.70
  76.1 0.1 broadcast_in_dim.10
  76.2 0.6 broadcast_in_dim.11
  76.8 4.0 %all-to-all-start.2 = ((f32[4,1,512]{2,1,0:T(1,128)}), f32[4,1,512]{2,1,0:T(1,128)S(1)}, u32[]{:S(2)}, u32[]{:S(2)}) async-start(f32[4,1,512]{2,1,0:T(1,128)} %broadcast_in_dim.11), calls=%async_computation.2 | async-start | bytes 16384 | tf_op jit(solution)/shard_map/all_to_all | solution.py:31
  80.8 4.2 %all-to-all-done.2 = f32[4,1,512]{2,1,0:T(1,128)S(1)} async-done(((f32[4,1,512]{2,1,0:T(1,128)}), f32[4,1,512]{2,1,0:T(1,128)S(1)}, u32[]{:S(2)}, u32[]{:S(2)}) %all-to-all-start.2) | async-done | bytes 8224 | tf_op jit(solution)/shard_map/all_to_all | solution.py:31
  85.1 0.1 reshape_squeeze.8
  85.2 0.1 broadcast_divide_fusion
  85.2 0.7 copy.72
  (17 shorter events, 0.2 us)
Async XLA Ops:
  0.0 2.4 %copy-start = (s32[2048]{0:T(1024)S(1)}, s32[2048]{0:T(1024)}, u32[]{:S(2)}) copy-start(s32[2048]{0:T(1024)} %param.7) | copy-start | bytes 24580
  0.0 2.6 %copy-start.1 = (f32[8]{0:T(128)S(1)}, f32[8]{0:T(128)}, u32[]{:S(2)}) copy-start(f32[8]{0:T(128)} %param.6) | copy-start | bytes 100
  4.7 39.1 %all-to-all-start = ((bf16[128,9,128]{2,1,0:T(8,128)(2,1)}), bf16[128,9,128]{2,1,0:T(8,128)(2,1)}, u32[]{:S(2)}, u32[]{:S(2)}) async-start(bf16[128,9,128]{2,1,0:T(8,128)(2,1)} %copy.63), calls=%async_computation | async-start | bytes 1048576 | tf_op jit(solution)/shard_map/all_to_all | solution.py:78
  51.9 23.2 %all-to-all-start.1 = ((f32[128,1,528]{2,1,0:T(1,128)}), f32[128,1,528]{2,1,0:T(1,128)S(1)}, u32[]{:S(2)}, u32[]{:S(2)}) async-start(f32[128,1,528]{2,1,0:T(1,128)} %copy.67), calls=%async_computation.1 | async-start | bytes 655360 | tf_op jit(solution)/shard_map/all_to_all | solution.py:111
  76.8 8.2 %all-to-all-start.2 = ((f32[4,1,512]{2,1,0:T(1,128)}), f32[4,1,512]{2,1,0:T(1,128)S(1)}, u32[]{:S(2)}, u32[]{:S(2)}) async-start(f32[4,1,512]{2,1,0:T(1,128)} %broadcast_in_dim.11), calls=%async_computation.2 | async-start | bytes 16384 | tf_op jit(solution)/shard_map/all_to_all | solution.py:31
